TPU v7x, 256 devices: a whole 4x4x8 slice. The times are simulated.
256 devices in a mesh: req: 128 (over x, y, z), tp: 2 (over core).
Axes of the slice: x: 4, y: 4, z: 8, core: 2. Of those that a mesh axis runs over, the one named last changes fastest.
Arguments:
- tokens: bfloat16 [65536, 1024], P('req'), may hold values from -6 to 6
- group_len: int32 [128], P('req'), may hold values from 1 to 512, 49152 in all
- cache_len: int32 [128], replicated, may hold values from 1 to 1024, 65536 in all
- cache_keys: bfloat16 [128, 1024, 1024], P('req', None, 'tp'), may hold values from -192 to 192
- cache_values: bfloat16 [128, 1024, 1024], P('req', None, 'tp'), may hold values from -6 to 6
- w_query: bfloat16 [1024, 1024], P(None, 'tp'), may hold values from -0.1875 to 0.1875
- w_key: bfloat16 [1024, 1024], P(None, 'tp'), may hold values from -0.1875 to 0.1875
- w_value: bfloat16 [1024, 1024], P(None, 'tp'), may hold values from -0.1875 to 0.1875
- w_out: bfloat16 [1024, 1024], P('tp'), may hold values from -0.1875 to 0.1875
- w_up: bfloat16 [1024, 2048], P(None, 'tp'), may hold values from -0.1875 to 0.1875
- w_down: bfloat16 [2048, 1024], P('tp'), may hold values from -0.125 to 0.125
- ln_gains: float32 [2, 1024], replicated, may hold values from 0.5 to 1.5
- ln_biases: float32 [2, 1024], replicated, may hold values from -3 to 3
- embed: bfloat16 [49152, 1024], P(('req', 'tp')), may hold values from -0.5 to 0.5
Outputs:
- layer_out: bfloat16 [65536, 1024], P('req')
- top_logit: float32 [128], P('req')
- shard_top: float32 [128, 256], P(None, ('req', 'tp'))
Inputs may be any that keep to these rules, and one draw needn't show every extreme that they name: `cache_len`: one request has exactly 1024 cached positions. `group_len`: one request has a full block of 512 valid tokens.
All inputs are finite; a program needn't handle non-finite values.
Results may differ from a plain program's by a relative error of at most 0.015.
Values may be sent and summed in bfloat16 or wider, within the bound.
No kernel may reach another device: no remote copies, remote signals or barrier semaphores. Data moves between devices by JAX's collectives and lax.ppermute only.
A program may use at most 128 MiB of HBM per device.

v0:
```python
import jax
import jax.numpy as jnp
from jax import lax
from jax.sharding import PartitionSpec as P

HD = 64
BLK = 256


start_peak = -1e30


def normalize(rows, gain, bias):
    center = rows - jnp.mean(rows, axis=-1, keepdims=True)
    spread = jnp.mean(center * center, axis=-1, keepdims=True)
    return center * lax.rsqrt(spread + 1e-05) * gain + bias


def attend(soft_state, queries, keys_blk, values_blk, allowed):
    row_peak, row_total, accum = soft_state
    scale = 1.0 / jnp.sqrt(jnp.float32(queries.shape[2]))
    scores = (
        jnp.einsum("qhd,khd->qhk", queries, keys_blk, preferred_element_type=jnp.float32) * scale
    )
    scores = jnp.where(allowed[:, None, :], scores, -jnp.inf)
    new_peak = jnp.maximum(row_peak, jnp.max(scores, axis=-1))
    factor = jnp.exp(row_peak - new_peak)
    raised = jnp.exp(scores - new_peak[..., None])
    new_total = row_total * factor + jnp.sum(raised, axis=-1)
    new_accum = accum * factor[..., None] + jnp.einsum(
        "qhk,khd->qhd", raised.astype(jnp.bfloat16), values_blk, preferred_element_type=jnp.float32
    )
    return (new_peak, new_total, new_accum)


def cache_pass(soft_state, queries, keys_all, values_all, offset, blocks, length):

    def one_block(block_idx, carry):
        keys_blk = lax.dynamic_slice_in_dim(keys_all, block_idx * BLK, BLK, 0)
        values_blk = lax.dynamic_slice_in_dim(values_all, block_idx * BLK, BLK, 0)
        places = offset + block_idx * BLK + jnp.arange(BLK, dtype=jnp.int32)
        return attend(carry, queries, keys_blk, values_blk, (places < length)[None, :])

    return lax.fori_loop(jnp.int32(0), blocks, one_block, soft_state)


def shards(
    tokens,
    group_len,
    cache_len,
    cache_keys,
    cache_values,
    w_query,
    w_key,
    w_value,
    w_out,
    w_up,
    w_down,
    ln_gains,
    ln_biases,
    embed,
):
    block_rows = tokens.shape[0]
    local_width = w_query.shape[1]
    heads_local = local_width // HD
    cache_rows = cache_keys.shape[1]
    my_index = lax.axis_index("req")
    my_cache = lax.dynamic_index_in_dim(cache_len, my_index, 0, keepdims=False)
    my_valid = group_len[0]
    queries = jnp.dot(tokens, w_query, preferred_element_type=jnp.float32).astype(jnp.bfloat16)
    keys_new = jnp.dot(tokens, w_key, preferred_element_type=jnp.float32).astype(jnp.bfloat16)
    values_new = jnp.dot(tokens, w_value, preferred_element_type=jnp.float32).astype(jnp.bfloat16)
    head_queries = queries.reshape(block_rows, heads_local, HD)
    empty_state = (
        jnp.full((block_rows, heads_local), start_peak, jnp.float32),
        jnp.zeros((block_rows, heads_local), jnp.float32),
        jnp.zeros((block_rows, heads_local, HD), jnp.float32),
    )
    row_ids = jnp.arange(block_rows, dtype=jnp.int32)
    block_allowed = (row_ids[None, :] <= row_ids[:, None]) & (row_ids < my_valid)[None, :]
    soft_state = attend(
        empty_state,
        head_queries,
        keys_new.reshape(block_rows, heads_local, HD),
        values_new.reshape(block_rows, heads_local, HD),
        block_allowed,
    )
    own_keys = cache_keys[0].reshape(cache_rows, heads_local, HD)
    own_values = cache_values[0].reshape(cache_rows, heads_local, HD)
    own_blocks = (my_cache + BLK - 1) // BLK
    soft_state = cache_pass(soft_state, head_queries, own_keys, own_values, 0, own_blocks, my_cache)
    attn_mixed = (
        (soft_state[2] / soft_state[1][..., None])
        .astype(jnp.bfloat16)
        .reshape(block_rows, local_width)
    )
    attn_sum = lax.psum(
        jnp.dot(attn_mixed, w_out, preferred_element_type=jnp.float32).astype(jnp.bfloat16), "tp"
    ).astype(jnp.float32)
    middle = normalize(tokens.astype(jnp.float32) + attn_sum, ln_gains[0], ln_biases[0]).astype(
        jnp.bfloat16
    )
    active = jax.nn.gelu(
        jnp.dot(middle, w_up, preferred_element_type=jnp.float32), approximate=False
    ).astype(jnp.bfloat16)
    ffn_sum = lax.psum(
        jnp.dot(active, w_down, preferred_element_type=jnp.float32).astype(jnp.bfloat16), "tp"
    ).astype(jnp.float32)
    layer_out = normalize(middle.astype(jnp.float32) + ffn_sum, ln_gains[1], ln_biases[1]).astype(
        jnp.bfloat16
    )
    last_row = lax.dynamic_slice_in_dim(layer_out, my_valid - 1, 1, 0)
    logits = jnp.einsum(
        "rd,vd->rv",
        lax.all_gather(last_row, "req", axis=0, tiled=True),
        embed,
        preferred_element_type=jnp.float32,
    )
    slice_best = jnp.max(logits, axis=1)
    best_logit = lax.pmax(slice_best, ("req", "tp"))
    return (layer_out, lax.dynamic_slice_in_dim(best_logit, my_index, 1, 0), slice_best[:, None])


def solution(mesh):
    placed = (
        P("req", None),
        P("req"),
        P(),
        P("req", None, "tp"),
        P("req", None, "tp"),
        P(None, "tp"),
        P(None, "tp"),
        P(None, "tp"),
        P("tp", None),
        P(None, "tp"),
        P("tp", None),
        P(),
        P(),
        P(("req", "tp"), None),
    )
    return jax.shard_map(
        shards,
        mesh=mesh,
        in_specs=placed,
        out_specs=(P("req", None), P("req"), P(None, ("req", "tp"))),
        check_vma=False,
    )
```

profile of v0, /device:TPU:1, one launch (start us, length us, event | category | flops | bytes accessed | tf_op | source)
XLA Modules:
  0.0 564.3 jit_solution(3807487911290846801)
XLA Ops:
  7.2 0.0 copy-start
  7.2 0.0 copy-start.3
  7.2 0.0 all-reduce.3.cloned.1.call-start
  7.2 1.5 dynamic_slice.16
  9.4 0.0 copy-start.12
  10.2 0.1 fusion.79
  10.3 2.3 convolution_convert_fusion.4
  12.6 0.0 copy-done.3
  12.6 0.0 copy-done.12
  12.6 0.8 convolution_convert_fusion.3
  13.4 0.0 copy-start.2
  13.4 1.5 fusion.24
  14.9 0.0 copy-done.2
  14.9 0.0 copy-start.1
  14.9 0.0 copy-start.13
  14.9 1.7 fusion.23
  16.7 1.5 copy-done.1
  18.1 0.0 copy-done.13
  18.1 1.6 convolution_convert_fusion.2
  19.7 0.0 copy-start.9
  19.7 2.4 copy.27
  22.1 0.0 copy-done.9
  22.1 1.4 copy.28
  23.4 5.7 %fusion.45 = f32[512,8,64]{0,2,1:T(8,128)S(1)} fusion(bf16[512,8,64]{0,2,1:T(8,128)(2,1)} %bitcast.92, f32[8,512,512]{2,1,0:T(8,128)} %copy-done.1, f32[512,8]{0,1:T(8,128)S(1)} %broadcast_maximum_fusion, pred[512,512]{0,1:T(8,128)(4,1)S(1)} %fusion.79, f32[512,8]{0,1:T(8,128)S(1)} %get-tuple-element.76), kind=kOutput, calls=%fused_computation.62 | convolution fusion | flops 277086208 | bytes 10256384 | tf_op jit(solution)/shard_map/qhk,khd->qhd/dot_general | solution.py:30
  29.2 6.1 %while.14 = (s32[]{:T(128)}, f32[512,8]{0,1:T(8,128)S(1)}, f32[512,8]{0,1:T(8,128)S(1)}, f32[512,8,64]{0,2,1:T(8,128)S(1)}, s32[]{:T(128)}, /*index=5*/s32[]{:T(...) while((s32[]{:T(128)}, f32[512,8]{0,1:T(8,128)S(1)}, ...), condition=%wide.region_5.6_spmd, body=%wide.region_2.5_spmd.sunk | while | flops 280502784 | bytes 15992003 | solution.py:44
  29.2 0.7 add_compare_fusion.2
  29.9 2.1 bitcast_reduce_fusion.2
  32.0 0.9 fusion.143
  33.0 2.1 fusion.144
  35.3 0.1 divide_convert_fusion
  35.5 0.0 copy-start.10
  35.5 0.0 copy-start.11
  35.5 0.0 copy-start.4
  35.5 3.0 convolution_convert_fusion.1
  38.5 0.0 all-reduce.3.cloned.1.call-update
  38.5 0.0 all-reduce.5.cloned.1.call-start
  38.6 0.0 copy-done.10
  38.6 0.0 copy-done.11
  38.6 52.4 %all-reduce.3.cloned.1.call-done = bf16[512,1024]{1,0:T(8,128)(2,1)} async-done(((bf16[512,1024]{1,0:T(8,128)(2,1)}), bf16[512,1024]{1,0:T(8,128)(2,1)}) %all-reduce.3.cloned.1.call-update) | async-done | bytes 1048592 | tf_op jit(solution)/shard_map/psum | solution.py:97
  91.0 0.0 copy-done.4
  91.0 0.0 copy-start.7
  91.0 0.0 copy-start.5
  91.0 1.7 fusion.39
  92.8 0.0 copy-done.7
  92.8 0.5 multiply_reduce_fusion.1
  93.3 0.0 copy-done.5
  93.3 0.5 add_convert_fusion.1
  93.8 0.0 copy-done
  93.9 8.8 %convolution_convert_fusion = bf16[512,1024]{1,0:T(8,128)(2,1)} fusion(bf16[1024,1024]{1,0:T(8,128)(2,1)S(1)} %copy-done, bf16[512,1024]{1,0:T(8,128)(2,1)S(1)} %add_convert_fusion.1, bf16[1024,1024]{1,0:T(8,128)(2,1)} %param.25), kind=kOutput, calls=%fused_computation.59 | convolution fusion | flops 2182086656 | bytes 6291456 | tf_op jit(solution)/shard_map/dot_general | solution.py:107
  102.7 0.0 all-reduce.5.cloned.1.call-update
  102.7 31.7 %all-reduce.5.cloned.1.call-done = bf16[512,1024]{1,0:T(8,128)(2,1)} async-done(((bf16[512,1024]{1,0:T(8,128)(2,1)}), bf16[512,1024]{1,0:T(8,128)(2,1)}) %all-reduce.5.cloned.1.call-update) | async-done | bytes 1048592 | tf_op jit(solution)/shard_map/psum | solution.py:106
  134.4 1.7 fusion.41
  136.0 0.0 copy-done.6
  136.0 0.5 multiply_reduce_fusion
  136.6 0.6 add_convert_fusion
  137.1 0.0 copy-start.8
  137.1 1.0 copy-done.8
  138.1 292.9 %all-gather = bf16[128,1,1024]{2,1,0:T(2,128)(2,1)S(1)} all-gather(bf16[1,1,1024]{2,1,0:T(2,128)(2,1)S(1)} %dynamic-slice_bitcast_fusion), channel_id=1, replica_groups=mesh['req'=128,'tp'=2] {'req'}, dimensions={0}, use_global_device_ids=true | all-gather | bytes 264192 | tf_op jit(solution)/shard_map/all_gather | solution.py:115
  431.0 0.0 copy-done.14
  431.0 0.3 convolution_reduce_fusion
  431.3 0.0 copy-start.15
  431.3 125.6 %pmax.7 = f32[128]{0:T(128)S(1)} all-reduce(f32[128]{0:T(128)S(1)} %convolution_reduce_fusion), channel_id=1, replica_groups=mesh['req'=128,'tp'=2] {'req','tp'}, use_global_device_ids=true, to_apply=%region_13.14 | all-reduce | flops 128 | bytes 1024 | tf_op jit(solution)/shard_map/pmax | solution.py:120
  556.9 0.6 dynamic_slice.18
  557.5 0.0 copy-done.15
  (15 shorter events, 0.1 us)
Async XLA Ops:
  7.2 86.7 %copy-start = (bf16[1024,1024]{1,0:T(8,128)(2,1)S(1)}, bf16[1024,1024]{1,0:T(8,128)(2,1)}, u32[]{:S(2)}) copy-start(bf16[1024,1024]{1,0:T(8,128)(2,1)} %param.26) | copy-start | bytes 6291460
  7.2 5.4 copy-start.3
  7.2 83.8 %all-reduce.3.cloned.1.call-start = ((), (), s32[]{:S(2)}) async-start(), calls=%async_computation | async-start | bytes 2097152 | tf_op jit(solution)/shard_map/psum | solution.py:97
  9.4 3.2 copy-start.12
  13.4 1.5 copy-start.2
  14.9 3.2 copy-start.1
  14.9 3.2 copy-start.13
  19.7 2.4 copy-start.9
  35.5 3.1 copy-start.10
  35.5 3.1 copy-start.11
  35.5 55.5 %copy-start.4 = (bf16[512,1024]{1,0:T(8,128)(2,1)S(1)}, bf16[512,1024]{1,0:T(8,128)(2,1)}, u32[]{:S(2)}) copy-start(bf16[512,1024]{1,0:T(8,128)(2,1)} %param.16) | copy-start | bytes 3145732
  38.5 95.8 %all-reduce.5.cloned.1.call-start = ((), (), s32[]{:S(2)}) async-start(), calls=%async_computation.1 | async-start | bytes 2097152 | tf_op jit(solution)/shard_map/psum | solution.py:106
  91.0 1.7 copy-start.7
  91.0 2.2 copy-start.5
  134.4 1.7 copy-start.6
  136.5 294.4 %copy-start.14 = (bf16[192,1024]{1,0:T(8,128)(2,1)S(1)}, bf16[192,1024]{1,0:T(8,128)(2,1)}, u32[]{:S(2)}) copy-start(bf16[192,1024]{1,0:T(8,128)(2,1)} %param.29) | copy-start | bytes 1179652
  137.1 1.0 copy-start.8
  431.3 126.2 %copy-start.15 = (f32[128]{0:T(128)}, f32[128]{0:T(128)S(1)}, u32[]{:S(2)}) copy-start(f32[128]{0:T(128)S(1)} %convolution_reduce_fusion) | copy-start | bytes 1540
Sparse Core Ops, SparseCore 0:
  38.7 52.3 all-reduce.2
  102.8 31.5 all-reduce.4
where the time goes:
time: 565 us; the launch traced here: 564 us
  blocking collectives  419 us (74%)
  waiting for transfers between devices  84.1 us (15%)
  matrix products  28.2 us (5%)
  between operations  15.8 us (3%)
  other arithmetic  9.14 us (2%)
  local copies, waits for them, and re-layouts  8.33 us (1%)
    all_gather x1, blocking collectives, shards(): lax.all_gather(last_row, 'req', axis=0, tiled=True)  293 us
    pmax x1, blocking collectives, shards(): best_logit = lax.pmax(slice_best, ('req', 'tp'))  126 us
    psum x1, waiting for transfers between devices, shards(): lax.psum(jnp.dot(attn_mixed, w_out, preferred_element_type=jnp.float32).a...  52.4 us
    psum x1, waiting for transfers between devices, shards(): lax.psum(jnp.dot(active, w_down, preferred_element_type=jnp.float32).asty...  31.7 us
  transfers between devices with their start and end apart: 2, of which 2 were waited for; matrix products, arithmetic and copies ran while one was open for 0% of the time, Pallas kernels for 0%

commit v1 on v0

--- a/solution.py
+++ b/solution.py
@@ -14,6 +14,12 @@
     center = rows - jnp.mean(rows, axis=-1, keepdims=True)
     spread = jnp.mean(center * center, axis=-1, keepdims=True)
     return center * lax.rsqrt(spread + 1e-05) * gain + bias
+
+
+def pair_sum(partial):
+    own = partial.astype(jnp.bfloat16)
+    other = lax.ppermute(own, "tp", [(0, 1), (1, 0)])
+    return own.astype(jnp.float32) + other.astype(jnp.float32)
 
 
 def attend(soft_state, queries, keys_blk, values_blk, allowed):
@@ -94,31 +100,27 @@
         .astype(jnp.bfloat16)
         .reshape(block_rows, local_width)
     )
-    attn_sum = lax.psum(
-        jnp.dot(attn_mixed, w_out, preferred_element_type=jnp.float32).astype(jnp.bfloat16), "tp"
-    ).astype(jnp.float32)
+    attn_sum = pair_sum(jnp.dot(attn_mixed, w_out, preferred_element_type=jnp.float32))
     middle = normalize(tokens.astype(jnp.float32) + attn_sum, ln_gains[0], ln_biases[0]).astype(
         jnp.bfloat16
     )
     active = jax.nn.gelu(
         jnp.dot(middle, w_up, preferred_element_type=jnp.float32), approximate=False
     ).astype(jnp.bfloat16)
-    ffn_sum = lax.psum(
-        jnp.dot(active, w_down, preferred_element_type=jnp.float32).astype(jnp.bfloat16), "tp"
-    ).astype(jnp.float32)
+    ffn_sum = pair_sum(jnp.dot(active, w_down, preferred_element_type=jnp.float32))
     layer_out = normalize(middle.astype(jnp.float32) + ffn_sum, ln_gains[1], ln_biases[1]).astype(
         jnp.bfloat16
     )
     last_row = lax.dynamic_slice_in_dim(layer_out, my_valid - 1, 1, 0)
-    logits = jnp.einsum(
-        "rd,vd->rv",
-        lax.all_gather(last_row, "req", axis=0, tiled=True),
-        embed,
-        preferred_element_type=jnp.float32,
+    reqs = cache_len.shape[0]
+    all_rows = lax.all_to_all(
+        jnp.broadcast_to(last_row, (reqs, last_row.shape[1])), "req", 0, 0, tiled=True
     )
+    logits = jnp.einsum("rd,vd->rv", all_rows, embed, preferred_element_type=jnp.float32)
     slice_best = jnp.max(logits, axis=1)
-    best_logit = lax.pmax(slice_best, ("req", "tp"))
-    return (layer_out, lax.dynamic_slice_in_dim(best_logit, my_index, 1, 0), slice_best[:, None])
+    mine = jnp.max(lax.all_to_all(slice_best[:, None], "req", 0, 0, tiled=True), axis=0)
+    best_logit = jnp.maximum(mine, lax.ppermute(mine, "tp", [(0, 1), (1, 0)]))
+    return (layer_out, best_logit, slice_best[:, None])
 
 
 def solution(mesh):

time: 565 us -> 130 us (0.23)
  blocking collectives: 419 us -> 62 us
  waiting for transfers between devices: 84.1 us -> 5.83 us
  between operations: 15.8 us -> 4.81 us
  starting transfers between devices: 0.08 us -> 6.43 us
    all_gather x1 -> x0, blocking collectives: 293 us -> none  [shards(): lax.all_gather(last_row, 'req', axis=0, tiled=True)]
    pmax x1 -> x0, blocking collectives: 126 us -> none  [shards(): best_logit = lax.pmax(slice_best, ('req', 'tp'))]
    psum x2 -> x0, waiting for transfers between devices: 84.1 us -> none  [the longest x1 52.4 us: shards(): lax.psum(jnp.dot(attn_mixed, w_out, preferred_element_type=jnp.float32).a...]
    all_to_all x0 -> x2, blocking collectives: none -> 62 us  [the longest x1 45.4 us: shards(): lax.all_to_all(jnp.broadcast_to(last_row, (reqs, last_row.shape[1])), 're...]
    ppermute x0 -> x3, starting transfers between devices: none -> 6.43 us  [the longest x2 3.83 us: pair_sum(): other = lax.ppermute(own, 'tp', [(0, 1), (1, 0)])]
    ppermute x0 -> x3, waiting for transfers between devices: none -> 5.83 us  [the longest x2 4.88 us: pair_sum(): other = lax.ppermute(own, 'tp', [(0, 1), (1, 0)])]
  transfers between devices with their start and end apart: 2 -> 3, of which waited for: 2 -> 3; matrix products, arithmetic and copies ran while one was open for 0% -> 0% of each run, Pallas kernels for 0% -> 0%
where the time goes in v1:
time: 130 us; the launch traced here: 129 us
  blocking collectives  62 us (48%)
  matrix products  27.2 us (21%)
  other arithmetic  14.1 us (11%)
  local copies, waits for them, and re-layouts  9.04 us (7%)
  starting transfers between devices  6.43 us (5%)
  waiting for transfers between devices  5.83 us (4%)
  between operations  4.81 us (4%)
    all_to_all x1, blocking collectives, shards(): lax.all_to_all(jnp.broadcast_to(last_row, (reqs, last_row.shape[1])), 're...  45.4 us
    all_to_all x1, blocking collectives, shards(): lax.all_to_all(slice_best[:, None], 'req', 0, 0, tiled=True)  16.6 us
    dot_general x1, matrix products, shards(): jnp.dot(active, w_down, preferred_element_type=jnp.float32)  8.81 us
    dot_general x2, matrix products, attend(): jnp.einsum('qhk,khd->qhd', raised.astype(jnp.bfloat16), values_blk, prefe...  7.89 us
    unnamed x32, local copies, waits for them, and re-layouts  6.63 us
    ppermute x2, waiting for transfers between devices, pair_sum(): other = lax.ppermute(own, 'tp', [(0, 1), (1, 0)])  4.88 us
    ppermute x2, starting transfers between devices, pair_sum(): other = lax.ppermute(own, 'tp', [(0, 1), (1, 0)])  3.83 us
    dot_general x2, matrix products, attend(): jnp.einsum('qhd,khd->qhk', queries, keys_blk, preferred_element_type=jnp....  3.58 us
  transfers between devices with their start and end apart: 3, of which 3 were waited for; matrix products, arithmetic and copies ran while one was open for 0% of the time, Pallas kernels for 0%

profile of v1, /device:TPU:1, one launch (start us, length us, event | category | flops | bytes accessed | tf_op | source)
XLA Modules:
  0.0 129.5 jit_solution(10395022064388145117)
XLA Ops:
  0.6 0.0 copy-start
  0.6 0.0 copy-start.3
  0.7 1.5 %dynamic_slice.15 = s32[1]{0:T(128)} dynamic-slice(s32[128]{0:T(128)} %param.18, s32[]{:T(128)S(6)} %select_n.28), dynamic_slice_sizes={1} | dynamic-slice | bytes 12 | tf_op jit(solution)/shard_map/jit(dynamic_index_in_dim)/dynamic_slice | solution.py:74
  2.8 0.0 copy-start.11
  3.6 0.1 fusion.75
  3.7 2.3 %convolution_convert_fusion.3 = bf16[512,512]{0,1:T(8,128)(2,1)S(1)} fusion(bf16[512,1024]{1,0:T(8,128)(2,1)} %param.16, bf16[1024,512]{1,0:T(8,128)(2,1)} %param.21), kind=kOutput, calls=%fused_computation.60 | convolution fusion | flops 537133056 | bytes 2621440 | tf_op jit(solution)/shard_map/dot_general | solution.py:76
  6.0 0.0 copy-done.3
  6.0 0.0 copy-done.11
  6.0 0.0 copy-start.2
  6.0 0.8 convolution_convert_fusion.4
  6.8 1.5 %fusion.24 = (f32[512,8]{0,1:T(8,128)S(1)}, f32[8,512,512]{2,1,0:T(8,128)S(1)}) fusion(pred[512,512]{0,1:T(8,128)(4,1)S(1)} %fusion.75, bf16[512,8,64]{0,2,1:T(8,128)(2,1)S(1)} %bitcast.86, bf16[512,8,64]{0,2,1:T(8,128)(2,1)S(1)} %bitcast.82), kind=kOutput, calls=%fused_computation.27 | convolution fusion | flops 274722816 | bytes 9715712 | tf_op jit(solution)/shard_map/qhd,khd->qhk/dot_general | solution.py:29
  8.3 0.0 copy-done.2
  8.3 0.0 copy-start.1
  8.3 0.0 copy-start.12
  8.3 1.7 %fusion.23 = f32[512,8]{0,1:T(8,128)S(1)} fusion(f32[8,512,512]{2,1,0:T(8,128)S(1)} %get-tuple-element.83, f32[512,8]{0,1:T(8,128)S(1)} %broadcast_maximum_fusion, pred[512,512]{0,1:T(8,128)(4,1)S(1)} %fusion.75), kind=kLoop, calls=%fused_computation.26 | loop fusion | flops 8384512 | bytes 8683520 | tf_op jit(solution)/shard_map/reduce_sum | solution.py:35
  10.1 1.5 %copy-done.1 = f32[8,512,512]{2,1,0:T(8,128)} copy-done((f32[8,512,512]{2,1,0:T(8,128)}, f32[8,512,512]{2,1,0:T(8,128)S(1)}, u32[]{:S(2)}) %copy-start.1) | copy-done | bytes 8388632
  11.5 0.0 copy-done.12
  11.6 1.6 %convolution_convert_fusion.2 = bf16[512,512]{0,1:T(8,128)(2,1)} fusion(bf16[512,1024]{1,0:T(8,128)(2,1)S(1)} %copy-done.3, bf16[1024,512]{1,0:T(8,128)(2,1)S(1)} %copy-done.12), kind=kOutput, calls=%fused_computation.59 | convolution fusion | flops 537133056 | bytes 2621440 | tf_op jit(solution)/shard_map/dot_general | solution.py:78
  13.1 2.4 %copy.28 = bf16[1,1024,512]{1,2,0:T(8,128)(2,1)} copy(bf16[1,1024,512]{2,1,0:T(8,128)(2,1)} %param.20) | data formatting | bytes 2097152 | tf_op args[4]
  15.5 0.0 copy-done.7
  15.6 1.3 %copy.27 = bf16[1,1024,512]{1,2,0:T(8,128)(2,1)} copy(bf16[1,1024,512]{2,1,0:T(8,128)(2,1)S(1)} %copy-done.7) | data formatting | bytes 2097152 | tf_op args[3]
  16.9 5.7 %fusion.41 = f32[512,8,64]{0,2,1:T(8,128)S(1)} fusion(bf16[512,8,64]{0,2,1:T(8,128)(2,1)} %bitcast.94, f32[8,512,512]{2,1,0:T(8,128)} %copy-done.1, f32[512,8]{0,1:T(8,128)S(1)} %broadcast_maximum_fusion, pred[512,512]{0,1:T(8,128)(4,1)S(1)} %fusion.75, f32[512,8]{0,1:T(8,128)S(1)} %get-tuple-element.76), kind=kOutput, calls=%fused_computation.58 | convolution fusion | flops 277086208 | bytes 10256384 | tf_op jit(solution)/shard_map/qhk,khd->qhd/dot_general | solution.py:36
  22.6 5.9 %while.14 = (s32[]{:T(128)}, f32[512,8]{0,1:T(8,128)S(1)}, f32[512,8]{0,1:T(8,128)S(1)}, f32[512,8,64]{0,2,1:T(8,128)S(1)}, s32[]{:T(128)}, /*index=5*/s32[]{:T(...) while((s32[]{:T(128)}, f32[512,8]{0,1:T(8,128)S(1)}, ...), condition=%wide.region_5.6_spmd, body=%wide.region_2.5_spmd.sunk | while | flops 280502784 | bytes 15991995 | solution.py:50
  22.6 0.7 add_compare_fusion.2
  23.3 2.1 %bitcast_reduce_fusion.2 = (f32[512,8]{0,1:T(8,128)S(1)}, f32[8,256,512]{2,1,0:T(8,128)S(1)}) fusion(pred[256]{0:T(512)(128)(4,1)S(1)} %add_compare_fusion.2, bf16[512,8,64]{0,2,1:T(8,128)(2,1)} %get-tuple-element.181, bf16[1024,8,64]{0,2,1:T(8,128)(2,1)} %get-tuple-element.180, s32[]{:T(128)S(6)} %select_n.64), kind=kOutput, calls=%fused_computation.1.clone.1 | convolution fusion | flops 137359360 | bytes 4997380 | tf_op jit(solution)/shard_map/while/body/qhd,khd->qhk/dot_general | solution.py:29
  25.4 0.9 fusion.141
  26.4 2.1 %fusion.142 = f32[512,8,64]{0,2,1:T(8,128)S(1)} fusion(f32[8,256,512]{2,1,0:T(8,128)S(1)} %get-tuple-element.145, f32[512,8]{0,1:T(8,128)S(1)} %max.8, pred[256]{0:T(512)(128)(4,1)S(1)} %add_compare_fusion.2, f32[512,8,64]{0,2,1:T(8,128)S(1)} %get-tuple-element.164, f32[512,8]{0,1:T(8,128)S(1)} %get-tuple-element.147, ...), kind=kOutput, calls=%fused_computation.12.clone.1 | convolution fusion | flops 138936320 | bytes 6586628 | tf_op jit(solution)/shard_map/while/body/qhk,khd->qhd/dot_general | solution.py:36
  28.6 0.0 copy-start.8
  28.6 0.0 copy-start.9
  28.6 0.0 copy-start.4
  28.6 0.1 divide_convert_fusion
  28.7 2.0 %convolution_convert_fusion.1 = bf16[512,1024]{1,0:T(8,128)(2,1)S(1)} fusion(bf16[512,512]{0,1:T(8,128)(2,1)S(1)} %bitcast.87, bf16[512,1024]{1,0:T(8,128)(2,1)} %param.24), kind=kOutput, calls=%fused_computation.56 | convolution fusion | flops 537395200 | bytes 2621440 | tf_op jit(solution)/shard_map/dot_general | solution.py:103
  30.8 3.5 %collective-permute-start = (bf16[512,1024]{1,0:T(8,128)(2,1)S(1)}, bf16[512,1024]{1,0:T(8,128)(2,1)S(1)}, u32[]{:S(2)}, u32[]{:S(2)}) collective-permute-start(bf16[512,1024]{1,0:T(8,128)(2,1)S(1)} %convolution_convert_fusion.1), channel_id=1, source_target_pairs={{0,1},{1,0},{2,3},{3,2},{4,5},{5,4},{6,7},{7,6},{8,9},{9,8},{10,11... | collective-permute-start | bytes 3145736 | tf_op jit(solution)/shard_map/ppermute | solution.py:21
  34.2 0.0 copy-done.8
  34.2 0.0 copy-done.9
  34.3 2.2 %collective-permute-done = bf16[512,1024]{1,0:T(8,128)(2,1)S(1)} collective-permute-done((bf16[512,1024]{1,0:T(8,128)(2,1)S(1)}, bf16[512,1024]{1,0:T(8,128)(2,1)S(1)}, u32[]{:S(2)}, u32[]{:S(2)}) %collective-permute-start) | collective-permute-done | bytes 1048608 | tf_op jit(solution)/shard_map/ppermute | solution.py:21
  36.5 0.0 copy-done.4
  36.5 0.5 fusion.76
  37.0 0.6 multiply_reduce_fusion.1
  37.6 0.7 add_convert_fusion.1
  38.3 0.0 copy-done
  38.3 8.8 %convolution_convert_fusion = bf16[512,1024]{1,0:T(8,128)(2,1)} fusion(bf16[1024,1024]{1,0:T(8,128)(2,1)S(1)} %copy-done, bf16[512,1024]{1,0:T(8,128)(2,1)S(1)} %add_convert_fusion.1, bf16[1024,1024]{1,0:T(8,128)(2,1)} %param.25), kind=kOutput, calls=%fused_computation.55 | convolution fusion | flops 2182086656 | bytes 6291456 | tf_op jit(solution)/shard_map/dot_general | solution.py:110
  47.1 0.4 collective-permute-start.1
  47.5 2.6 %collective-permute-done.1 = bf16[512,1024]{1,0:T(8,128)(2,1)} collective-permute-done((bf16[512,1024]{1,0:T(8,128)(2,1)}, bf16[512,1024]{1,0:T(8,128)(2,1)}, u32[]{:S(2)}, u32[]{:S(2)}) %collective-permute-start.1) | collective-permute-done | bytes 1048608 | tf_op jit(solution)/shard_map/ppermute | solution.py:21
  50.1 2.0 %fusion.77 = f32[512]{0:T(512)S(1)} fusion(bf16[512,1024]{1,0:T(8,128)(2,1)} %collective-permute-done.1, bf16[512,1024]{1,0:T(8,128)(2,1)} %convolution_convert_fusion, bf16[512,1024]{1,0:T(8,128)(2,1)S(1)} %add_convert_fusion.1), kind=kLoop, calls=%fused_computation.97 | loop fusion | flops 3145216 | bytes 3147776 | tf_op jit(solution)/shard_map/reduce_sum | solution.py:14
  52.2 0.0 copy-done.5
  52.2 1.8 %multiply_reduce_fusion = f32[512]{0:T(512)S(1)} fusion(f32[512]{0:T(512)S(1)} %broadcast_multiply_fusion, bf16[512,1024]{1,0:T(8,128)(2,1)} %collective-permute-done.1, bf16[512,1024]{1,0:T(8,128)(2,1)S(1)} %copy-done.5, bf16[512,1024]{1,0:T(8,128)(2,1)S(1)} %add_convert_fusion.1), kind=kLoop, calls=%fused_computation.35 | loop fusion | flops 4193792 | bytes 3149824 | tf_op jit(solution)/shard_map/reduce_sum | solution.py:15
  54.0 1.9 %add_convert_fusion = bf16[512,1024]{1,0:T(8,128)(2,1)S(1)} fusion(f32[1024]{0:T(1024)S(1)} %bitcast.89, f32[1024]{0:T(1024)S(1)} %bitcast.88, f32[512]{0:T(512)S(1)} %add_rsqrt_fusion, f32[512]{0:T(512)S(1)} %broadcast_multiply_fusion, bf16[512,1024]{1,0:T(8,128)(2,1)} %collective-permute-done.1, bf16[512,1024]{1,0:T(8,128)(2,1)S(1)} %copy-done.5, ...), kind=kLoop, calls=%fused_computation.34 | loop fusion | flops 5242880 | bytes 4206592 | tf_op jit(solution)/shard_map/convert_element_type | solution.py:111
  56.0 0.0 copy-start.6
  56.0 1.0 copy-done.6
  57.0 0.3 broadcast_in_dim.39
  57.2 0.5 broadcast.122
  57.7 2.1 %reduce.4 = bf16[128,1024]{1,0:T(8,128)(2,1)S(1)} reduce(bf16[128,1,1024]{2,1,0:T(2,128)(2,1)S(1)} %broadcast_in_dim.39, bf16[]{:T(256)} %broadcast.122), dimensions={1}, to_apply=%broadcast_in_dim.39.reduce_sub_computation | reduce | bytes 524290 | tf_op jit(solution)/shard_map/broadcast_in_dim | solution.py:117
  59.9 0.2 reshape.99
  60.1 45.4 %all_to_all.18 = bf16[128,2,512]{2,1,0:T(2,128)(2,1)S(1)} all-to-all(bf16[128,2,512]{2,1,0:T(2,128)(2,1)S(1)} %reshape.99), channel_id=1, replica_groups=mesh['req'=128,'tp'=2] {'req'}, dimensions={0} | all-to-all | bytes 524288 | tf_op jit(solution)/shard_map/all_to_all | solution.py:116
  105.4 0.2 reshape.100
  105.7 0.3 convolution_reduce_fusion
  106.0 0.0 copy-start.10
  106.0 0.1 copy.29
  106.1 16.6 %all_to_all.19 = f32[128,1,1]{2,1,0:T(1,128)S(1)} all-to-all(f32[128,1,1]{2,1,0:T(1,128)S(1)} %copy.29), channel_id=1, replica_groups=mesh['req'=128,'tp'=2] {'req'}, dimensions={0} | all-to-all | bytes 1024 | tf_op jit(solution)/shard_map/all_to_all | solution.py:121
  122.7 0.7 reduce_max.40
  123.4 2.6 %collective-permute-start.2 = (f32[1]{0:T(128)}, f32[1]{0:T(128)}, u32[]{:S(2)}, u32[]{:S(2)}) collective-permute-start(f32[1]{0:T(128)} %bitcast.17), channel_id=1, source_target_pairs={{0,1},{1,0},{2,3},{3,2},{4,5},{5,4},{6,7},{7,6},{8,9},{9,8},{10,11... | collective-permute-start | bytes 20 | tf_op jit(solution)/shard_map/ppermute | solution.py:122
  126.0 1.0 collective-permute-done.2
  128.3 0.0 copy-done.10
  (17 shorter events, 0.1 us)
Async XLA Ops:
  0.6 37.7 %copy-start = (bf16[1024,1024]{1,0:T(8,128)(2,1)S(1)}, bf16[1024,1024]{1,0:T(8,128)(2,1)}, u32[]{:S(2)}) copy-start(bf16[1024,1024]{1,0:T(8,128)(2,1)} %param.26) | copy-start | bytes 6291460
  0.6 5.4 %copy-start.3 = (bf16[512,1024]{1,0:T(8,128)(2,1)S(1)}, bf16[512,1024]{1,0:T(8,128)(2,1)}, u32[]{:S(2)}) copy-start(bf16[512,1024]{1,0:T(8,128)(2,1)} %param.16) | copy-start | bytes 3145732
  2.8 3.2 %copy-start.11 = (bf16[1024,512]{1,0:T(8,128)(2,1)S(1)}, bf16[1024,512]{1,0:T(8,128)(2,1)}, u32[]{:S(2)}) copy-start(bf16[1024,512]{1,0:T(8,128)(2,1)} %param.22) | copy-start | bytes 3145732
  6.0 2.3 %copy-start.2 = (bf16[512,512]{0,1:T(8,128)(2,1)}, bf16[512,512]{0,1:T(8,128)(2,1)S(1)}, u32[]{:S(2)}) copy-start(bf16[512,512]{0,1:T(8,128)(2,1)S(1)} %convolution_convert_fusion.3) | copy-start | bytes 1572868
  8.3 3.2 %copy-start.1 = (f32[8,512,512]{2,1,0:T(8,128)}, f32[8,512,512]{2,1,0:T(8,128)S(1)}, u32[]{:S(2)}) copy-start(f32[8,512,512]{2,1,0:T(8,128)S(1)} %get-tuple-element.83) | copy-start | bytes 25165828
  8.3 3.2 %copy-start.12 = (bf16[1024,512]{1,0:T(8,128)(2,1)S(1)}, bf16[1024,512]{1,0:T(8,128)(2,1)}, u32[]{:S(2)}) copy-start(bf16[1024,512]{1,0:T(8,128)(2,1)} %param.23) | copy-start | bytes 3145732
  13.1 2.4 %copy-start.7 = (bf16[1,1024,512]{2,1,0:T(8,128)(2,1)S(1)}, bf16[1,1024,512]{2,1,0:T(8,128)(2,1)}, u32[]{:S(2)}) copy-start(bf16[1,1024,512]{2,1,0:T(8,128)(2,1)} %param.19) | copy-start | bytes 3145732
  28.6 5.7 %copy-start.8 = (f32[2,1024]{1,0:T(2,128)S(1)}, f32[2,1024]{1,0:T(2,128)}, u32[]{:S(2)}) copy-start(f32[2,1024]{1,0:T(2,128)} %param.27) | copy-start | bytes 24580
  28.6 5.7 %copy-start.9 = (f32[2,1024]{1,0:T(2,128)S(1)}, f32[2,1024]{1,0:T(2,128)}, u32[]{:S(2)}) copy-start(f32[2,1024]{1,0:T(2,128)} %param.28) | copy-start | bytes 24580
  28.6 8.0 %copy-start.4 = (bf16[512,1024]{1,0:T(8,128)(2,1)S(1)}, bf16[512,1024]{1,0:T(8,128)(2,1)}, u32[]{:S(2)}) copy-start(bf16[512,1024]{1,0:T(8,128)(2,1)} %param.16) | copy-start | bytes 3145732
  30.8 5.7 %collective-permute-start = (bf16[512,1024]{1,0:T(8,128)(2,1)S(1)}, bf16[512,1024]{1,0:T(8,128)(2,1)S(1)}, u32[]{:S(2)}, u32[]{:S(2)}) collective-permute-start(bf16[512,1024]{1,0:T(8,128)(2,1)S(1)} %convolution_convert_fusion.1), channel_id=1, source_target_pairs={{0,1},{1,0},{2,3},{3,2},{4,5},{5,4},{6,7},{7,6},{8,9},{9,8},{10,11... | collective-permute-start | bytes 3145736 | tf_op jit(solution)/shard_map/ppermute | solution.py:21
  47.1 3.0 %collective-permute-start.1 = (bf16[512,1024]{1,0:T(8,128)(2,1)}, bf16[512,1024]{1,0:T(8,128)(2,1)}, u32[]{:S(2)}, u32[]{:S(2)}) collective-permute-start(bf16[512,1024]{1,0:T(8,128)(2,1)} %convolution_convert_fusion), channel_id=1, source_target_pairs={{0,1},{1,0},{2,3},{3,2},{4,5},{5,4},{6,7},{7,6},{8,9},{9,8},{10,11... | collective-permute-start | bytes 3145736 | tf_op jit(solution)/shard_map/ppermute | solution.py:21
  47.5 4.7 %copy-start.5 = (bf16[512,1024]{1,0:T(8,128)(2,1)S(1)}, bf16[512,1024]{1,0:T(8,128)(2,1)}, u32[]{:S(2)}) copy-start(bf16[512,1024]{1,0:T(8,128)(2,1)} %convolution_convert_fusion) | copy-start | bytes 3145732
  56.0 1.0 copy-start.6
  56.9 48.7 %copy-start.13 = (bf16[192,1024]{1,0:T(8,128)(2,1)S(1)}, bf16[192,1024]{1,0:T(8,128)(2,1)}, u32[]{:S(2)}) copy-start(bf16[192,1024]{1,0:T(8,128)(2,1)} %param.29) | copy-start | bytes 1179652
  106.0 22.4 %copy-start.10 = (f32[128]{0:T(128)}, f32[128]{0:T(128)S(1)}, u32[]{:S(2)}) copy-start(f32[128]{0:T(128)S(1)} %convolution_reduce_fusion) | copy-start | bytes 1540
  123.4 3.6 %collective-permute-start.2 = (f32[1]{0:T(128)}, f32[1]{0:T(128)}, u32[]{:S(2)}, u32[]{:S(2)}) collective-permute-start(f32[1]{0:T(128)} %bitcast.17), channel_id=1, source_target_pairs={{0,1},{1,0},{2,3},{3,2},{4,5},{5,4},{6,7},{7,6},{8,9},{9,8},{10,11... | collective-permute-start | bytes 20 | tf_op jit(solution)/shard_map/ppermute | solution.py:122

commit v2 on v1

--- a/solution.py
+++ b/solution.py
@@ -100,6 +100,37 @@
         .astype(jnp.bfloat16)
         .reshape(block_rows, local_width)
     )
+    layer_out = finish_rows(attn_mixed, tokens, w_out, w_up, w_down, ln_gains, ln_biases)
+
+    reqs = cache_len.shape[0]
+    last = my_valid - 1
+    q_last = lax.dynamic_slice_in_dim(head_queries, last, 1, 0)[0].astype(jnp.float32)
+    keys_all = jnp.concatenate([own_keys, keys_new.reshape(block_rows, heads_local, HD)], axis=0)
+    values_all = jnp.concatenate([own_values, values_new.reshape(block_rows, heads_local, HD)], axis=0)
+    scale = 1.0 / jnp.sqrt(jnp.float32(HD))
+    scores = jnp.einsum("hd,khd->hk", q_last, keys_all.astype(jnp.float32)) * scale
+    places = jnp.arange(cache_rows + block_rows, dtype=jnp.int32)
+    allowed = jnp.where(places < cache_rows, places < my_cache, places - cache_rows < my_valid)
+    scores = jnp.where(allowed[None, :], scores, -jnp.inf)
+    peak = jnp.max(scores, axis=-1, keepdims=True)
+    raised = jnp.exp(scores - peak)
+    total = jnp.sum(raised, axis=-1, keepdims=True)
+    rounded = raised.astype(jnp.bfloat16).astype(jnp.float32)
+    row_mixed = (jnp.einsum("hk,khd->hd", rounded, values_all.astype(jnp.float32)) / total).astype(
+        jnp.bfloat16
+    ).reshape(1, local_width)
+    token_row = lax.dynamic_slice_in_dim(tokens, last, 1, 0)
+    last_row = finish_rows(row_mixed, token_row, w_out, w_up, w_down, ln_gains, ln_biases)
+
+    all_rows = gather_rows(last_row, reqs)
+    logits = jnp.einsum("rd,vd->rv", all_rows, embed, preferred_element_type=jnp.float32)
+    slice_best = jnp.max(logits, axis=1)
+    best_all = max_everywhere(slice_best, reqs)
+    best_logit = lax.dynamic_slice_in_dim(best_all, my_index, 1, 0)
+    return (layer_out, best_logit, slice_best[:, None])
+
+
+def finish_rows(attn_mixed, tokens, w_out, w_up, w_down, ln_gains, ln_biases):
     attn_sum = pair_sum(jnp.dot(attn_mixed, w_out, preferred_element_type=jnp.float32))
     middle = normalize(tokens.astype(jnp.float32) + attn_sum, ln_gains[0], ln_biases[0]).astype(
         jnp.bfloat16
@@ -108,19 +139,32 @@
         jnp.dot(middle, w_up, preferred_element_type=jnp.float32), approximate=False
     ).astype(jnp.bfloat16)
     ffn_sum = pair_sum(jnp.dot(active, w_down, preferred_element_type=jnp.float32))
-    layer_out = normalize(middle.astype(jnp.float32) + ffn_sum, ln_gains[1], ln_biases[1]).astype(
+    return normalize(middle.astype(jnp.float32) + ffn_sum, ln_gains[1], ln_biases[1]).astype(
         jnp.bfloat16
     )
-    last_row = lax.dynamic_slice_in_dim(layer_out, my_valid - 1, 1, 0)
-    reqs = cache_len.shape[0]
-    all_rows = lax.all_to_all(
-        jnp.broadcast_to(last_row, (reqs, last_row.shape[1])), "req", 0, 0, tiled=True
-    )
-    logits = jnp.einsum("rd,vd->rv", all_rows, embed, preferred_element_type=jnp.float32)
-    slice_best = jnp.max(logits, axis=1)
-    mine = jnp.max(lax.all_to_all(slice_best[:, None], "req", 0, 0, tiled=True), axis=0)
-    best_logit = jnp.maximum(mine, lax.ppermute(mine, "tp", [(0, 1), (1, 0)]))
-    return (layer_out, best_logit, slice_best[:, None])
+
+
+def gather_rows(row, count):
+    me = lax.axis_index("req")
+    held = row
+    step = 1
+    while step < count:
+        other = lax.ppermute(held, "req", [(i, i ^ step) for i in range(count)])
+        low = (me // step) % 2 == 0
+        held = jnp.where(
+            low, jnp.concatenate([held, other], axis=0), jnp.concatenate([other, held], axis=0)
+        )
+        step *= 2
+    return held
+
+
+def max_everywhere(values, count):
+    values = jnp.maximum(values, lax.ppermute(values, "tp", [(0, 1), (1, 0)]))
+    step = 1
+    while step < count:
+        values = jnp.maximum(values, lax.ppermute(values, "req", [(i, i ^ step) for i in range(count)]))
+        step *= 2
+    return values
 
 
 def solution(mesh):

time: 130 us -> 157 us (1.21)
  the two profiles are of different devices: /device:TPU:1 before, /device:TPU:2 now
where the time goes in v2:
time: 157 us; the launch traced here: 156 us
  waiting for transfers between devices  42.8 us (27%)
  matrix products  40.8 us (26%)
  starting transfers between devices  34.8 us (22%)
  other arithmetic  24.2 us (15%)
  local copies, waits for them, and re-layouts  7.55 us (5%)
  between operations  5.24 us (3%)
    ppermute x7, waiting for transfers between devices, gather_rows(): other = lax.ppermute(held, 'req', [(i, i ^ step) for i in range(count)])  21.4 us
    ppermute x7, starting transfers between devices, gather_rows(): other = lax.ppermute(held, 'req', [(i, i ^ step) for i in range(count)])  19.8 us
    ppermute x7, waiting for transfers between devices, max_everywhere(): lax.ppermute(values, 'req', [(i, i ^ step) for i in range(count)])  19.1 us
    ppermute x7, starting transfers between devices, max_everywhere(): lax.ppermute(values, 'req', [(i, i ^ step) for i in range(count)])  14.1 us
    dot_general x2, matrix products, finish_rows(): jnp.dot(active, w_down, preferred_element_type=jnp.float32)  9.2 us
    dot_general x4, matrix products, attend(): jnp.einsum('qhk,khd->qhd', raised.astype(jnp.bfloat16), values_blk, prefe...  8.7 us
    dot_general x4, matrix products, attend(): jnp.einsum('qhd,khd->qhk', queries, keys_blk, preferred_element_type=jnp....  7.78 us
    unnamed x29, local copies, waits for them, and re-layouts  6.14 us
  transfers between devices with their start and end apart: 19, of which 15 were waited for; matrix products, arithmetic and copies ran while one was open for 31% of the time, Pallas kernels for 0%

profile of v2, /device:TPU:2, one launch (start us, length us, event | category | flops | bytes accessed | tf_op | source)
XLA Modules:
  0.0 155.8 jit_solution(17043761491736558627)
XLA Ops:
  1.4 2.3 %convolution_convert_fusion.3 = bf16[512,512]{0,1:T(8,128)(2,1)S(1)} fusion(bf16[512,1024]{1,0:T(8,128)(2,1)} %param.16, bf16[1024,512]{1,0:T(8,128)(2,1)} %param.21), kind=kOutput, calls=%fused_computation.68 | convolution fusion | flops 537133056 | bytes 2621440 | tf_op jit(solution)/shard_map/dot_general | solution.py:76
  4.0 2.3 %copy.28 = bf16[1,1024,512]{1,2,0:T(8,128)(2,1)} copy(bf16[1,1024,512]{2,1,0:T(8,128)(2,1)} %param.19) | data formatting | bytes 2097152 | tf_op args[3]
  6.3 2.3 %convolution_convert_fusion.4 = bf16[512,512]{0,1:T(8,128)(2,1)S(1)} fusion(bf16[512,1024]{1,0:T(8,128)(2,1)} %param.16, bf16[1024,512]{1,0:T(8,128)(2,1)} %param.22), kind=kOutput, calls=%fused_computation.69 | convolution fusion | flops 537133056 | bytes 2621440 | tf_op jit(solution)/shard_map/dot_general | solution.py:77
  8.6 0.6 dynamic_slice.19
  9.2 0.7 fusion.98
  9.9 1.5 fusion.38
  11.7 2.3 %copy.29 = bf16[1,1024,512]{1,2,0:T(8,128)(2,1)} copy(bf16[1,1024,512]{2,1,0:T(8,128)(2,1)} %param.20) | data formatting | bytes 2097152 | tf_op args[4]
  14.0 2.4 %convolution_convert_fusion.2 = bf16[512,512]{0,1:T(8,128)(2,1)S(1)} fusion(bf16[512,1024]{1,0:T(8,128)(2,1)} %param.16, bf16[1024,512]{1,0:T(8,128)(2,1)} %param.23), kind=kOutput, calls=%fused_computation.67 | convolution fusion | flops 537133056 | bytes 2621440 | tf_op jit(solution)/shard_map/dot_general | solution.py:78
  17.4 1.5 fusion.153
  19.8 1.5 fusion.24
  21.3 1.7 %fusion.23 = f32[512,8]{0,1:T(8,128)S(1)} fusion(f32[8,512,512]{2,1,0:T(8,128)S(1)} %get-tuple-element.90, f32[512,8]{0,1:T(8,128)S(1)} %broadcast_maximum_fusion, pred[512,512]{0,1:T(8,128)(4,1)S(1)} %fusion.83), kind=kLoop, calls=%fused_computation.26 | loop fusion | flops 8384512 | bytes 8683520 | tf_op jit(solution)/shard_map/reduce_sum | solution.py:35
  23.1 2.3 %fusion.49 = f32[512,8,64]{0,2,1:T(8,128)S(1)} fusion(bf16[512,8,64]{0,2,1:T(8,128)(2,1)S(1)} %bitcast.128, f32[8,512,512]{2,1,0:T(8,128)S(1)} %get-tuple-element.90, f32[512,8]{0,1:T(8,128)S(1)} %broadcast_maximum_fusion, pred[512,512]{0,1:T(8,128)(4,1)S(1)} %fusion.83, f32[512,8]{0,1:T(8,128)S(1)} %get-tuple-element.82), kind=kOutput, calls=%fused_computation.66 | convolution fusion | flops 277086208 | bytes 10256384 | tf_op jit(solution)/shard_map/qhk,khd->qhd/dot_general | solution.py:36
  25.3 17.9 %while.14 = (s32[]{:T(128)}, f32[512,8]{0,1:T(8,128)S(1)}, f32[512,8]{0,1:T(8,128)S(1)}, f32[512,8,64]{0,2,1:T(8,128)S(1)}, s32[]{:T(128)}, /*index=5*/s32[]{:T(...) while((s32[]{:T(128)}, f32[512,8]{0,1:T(8,128)S(1)}, ...), condition=%wide.region_5.6_spmd, body=%wide.region_2.5_spmd.sunk | while | flops 280502784 | bytes 15991995 | solution.py:50
  25.4 0.7 add_compare_fusion.3
  26.0 2.1 %bitcast_reduce_fusion.2 = (f32[512,8]{0,1:T(8,128)S(1)}, f32[8,256,512]{2,1,0:T(8,128)S(1)}) fusion(pred[256]{0:T(512)(128)(4,1)S(1)} %add_compare_fusion.3, bf16[512,8,64]{0,2,1:T(8,128)(2,1)} %get-tuple-element.188, bf16[1024,8,64]{0,2,1:T(8,128)(2,1)} %get-tuple-element.187, s32[]{:T(128)S(6)} %select_n.240), kind=kOutput, calls=%fused_computation.1.clone.1 | convolution fusion | flops 137359360 | bytes 4997380 | tf_op jit(solution)/shard_map/while/body/qhd,khd->qhk/dot_general | solution.py:29
  28.1 0.9 fusion.184
  29.1 2.1 %fusion.185 = f32[512,8,64]{0,2,1:T(8,128)S(1)} fusion(f32[8,256,512]{2,1,0:T(8,128)S(1)} %get-tuple-element.152, f32[512,8]{0,1:T(8,128)S(1)} %max.36, pred[256]{0:T(512)(128)(4,1)S(1)} %add_compare_fusion.3, f32[512,8,64]{0,2,1:T(8,128)S(1)} %get-tuple-element.171, f32[512,8]{0,1:T(8,128)S(1)} %get-tuple-element.154, ...), kind=kOutput, calls=%fused_computation.12.clone.1 | convolution fusion | flops 138936320 | bytes 6586628 | tf_op jit(solution)/shard_map/while/body/qhk,khd->qhd/dot_general | solution.py:36
  31.3 0.7 add_compare_fusion.3
  31.9 2.1 %bitcast_reduce_fusion.2 = (f32[512,8]{0,1:T(8,128)S(1)}, f32[8,256,512]{2,1,0:T(8,128)S(1)}) fusion(pred[256]{0:T(512)(128)(4,1)S(1)} %add_compare_fusion.3, bf16[512,8,64]{0,2,1:T(8,128)(2,1)} %get-tuple-element.188, bf16[1024,8,64]{0,2,1:T(8,128)(2,1)} %get-tuple-element.187, s32[]{:T(128)S(6)} %select_n.240), kind=kOutput, calls=%fused_computation.1.clone.1 | convolution fusion | flops 137359360 | bytes 4997380 | tf_op jit(solution)/shard_map/while/body/qhd,khd->qhk/dot_general | solution.py:29
  34.1 0.9 fusion.184
  35.0 2.1 %fusion.185 = f32[512,8,64]{0,2,1:T(8,128)S(1)} fusion(f32[8,256,512]{2,1,0:T(8,128)S(1)} %get-tuple-element.152, f32[512,8]{0,1:T(8,128)S(1)} %max.36, pred[256]{0:T(512)(128)(4,1)S(1)} %add_compare_fusion.3, f32[512,8,64]{0,2,1:T(8,128)S(1)} %get-tuple-element.171, f32[512,8]{0,1:T(8,128)S(1)} %get-tuple-element.154, ...), kind=kOutput, calls=%fused_computation.12.clone.1 | convolution fusion | flops 138936320 | bytes 6586628 | tf_op jit(solution)/shard_map/while/body/qhk,khd->qhd/dot_general | solution.py:36
  37.2 0.7 add_compare_fusion.3
  37.9 2.1 %bitcast_reduce_fusion.2 = (f32[512,8]{0,1:T(8,128)S(1)}, f32[8,256,512]{2,1,0:T(8,128)S(1)}) fusion(pred[256]{0:T(512)(128)(4,1)S(1)} %add_compare_fusion.3, bf16[512,8,64]{0,2,1:T(8,128)(2,1)} %get-tuple-element.188, bf16[1024,8,64]{0,2,1:T(8,128)(2,1)} %get-tuple-element.187, s32[]{:T(128)S(6)} %select_n.240), kind=kOutput, calls=%fused_computation.1.clone.1 | convolution fusion | flops 137359360 | bytes 4997380 | tf_op jit(solution)/shard_map/while/body/qhd,khd->qhk/dot_general | solution.py:29
  40.0 0.9 fusion.184
  40.9 2.1 %fusion.185 = f32[512,8,64]{0,2,1:T(8,128)S(1)} fusion(f32[8,256,512]{2,1,0:T(8,128)S(1)} %get-tuple-element.152, f32[512,8]{0,1:T(8,128)S(1)} %max.36, pred[256]{0:T(512)(128)(4,1)S(1)} %add_compare_fusion.3, f32[512,8,64]{0,2,1:T(8,128)S(1)} %get-tuple-element.171, f32[512,8]{0,1:T(8,128)S(1)} %get-tuple-element.154, ...), kind=kOutput, calls=%fused_computation.12.clone.1 | convolution fusion | flops 138936320 | bytes 6586628 | tf_op jit(solution)/shard_map/while/body/qhk,khd->qhd/dot_general | solution.py:36
  43.4 2.9 %convolution_convert_fusion.1 = bf16[512,1024]{1,0:T(8,128)(2,1)} fusion(bf16[512,512]{0,1:T(8,128)(2,1)S(1)} %bitcast.116, bf16[512,1024]{1,0:T(8,128)(2,1)} %param.24), kind=kOutput, calls=%fused_computation.64 | convolution fusion | flops 537395200 | bytes 2621440 | tf_op jit(solution)/shard_map/dot_general | solution.py:134
  46.9 1.3 fusion.150
  48.9 0.6 multiply_reduce_fusion.3
  50.7 1.1 copy-done.6
  52.3 1.1 collective-permute-done.3
  53.4 0.6 fusion.149
  54.7 0.6 multiply_reduce_fusion.2
  56.1 2.0 %fusion.84 = f32[512]{0:T(512)S(1)} fusion(bf16[512,1024]{1,0:T(8,128)(2,1)} %collective-permute-done, bf16[512,1024]{1,0:T(8,128)(2,1)} %convolution_convert_fusion.1, bf16[512,1024]{1,0:T(8,128)(2,1)S(1)} %copy-done.2), kind=kLoop, calls=%fused_computation.104 | loop fusion | flops 3145216 | bytes 3147776 | tf_op jit(solution)/shard_map/reduce_sum | solution.py:14
  58.2 2.2 %multiply_reduce_fusion.1 = f32[512]{0:T(512)S(1)} fusion(f32[512]{0:T(512)S(1)} %broadcast_multiply_fusion.1, bf16[512,1024]{1,0:T(8,128)(2,1)} %collective-permute-done, bf16[512,1024]{1,0:T(8,128)(2,1)} %convolution_convert_fusion.1, bf16[512,1024]{1,0:T(8,128)(2,1)S(1)} %copy-done.2), kind=kLoop, calls=%fused_computation.51 | loop fusion | flops 4193792 | bytes 3149824 | tf_op jit(solution)/shard_map/reduce_sum | solution.py:15
  60.5 2.2 %add_convert_fusion.1 = bf16[512,1024]{1,0:T(8,128)(2,1)S(1)} fusion(f32[1024]{0:T(1024)S(1)} %bitcast.123, f32[1024]{0:T(1024)S(1)} %bitcast.122, f32[512]{0:T(512)S(1)} %add_rsqrt_fusion.1, f32[512]{0:T(512)S(1)} %broadcast_multiply_fusion.1, bf16[512,1024]{1,0:T(8,128)(2,1)} %collective-permute-done, bf16[512,1024]{1,0:T(8,128)(2,1)} %convolution_convert_fusion.1, ...), kind=kLoop, calls=%fused_computation.50 | loop fusion | flops 5242880 | bytes 4206592 | tf_op jit(solution)/shard_map/convert_element_type | solution.py:135
  62.7 8.8 %convolution_convert_fusion = bf16[512,1024]{1,0:T(8,128)(2,1)} fusion(bf16[1024,1024]{1,0:T(8,128)(2,1)} %param.26, bf16[512,1024]{1,0:T(8,128)(2,1)S(1)} %add_convert_fusion.1, bf16[1024,1024]{1,0:T(8,128)(2,1)S(1)} %copy-done), kind=kOutput, calls=%fused_computation.63 | convolution fusion | flops 2182086656 | bytes 6291456 | tf_op jit(solution)/shard_map/dot_general | solution.py:141
  72.0 4.5 %collective-permute-done.5 = bf16[2,1024]{1,0:T(2,128)(2,1)S(1)} collective-permute-done((bf16[2,1024]{1,0:T(2,128)(2,1)S(1)}, bf16[2,1024]{1,0:T(2,128)(2,1)S(1)}, u32[]{:S(2)}, u32[]{:S(2)}) %collective-permute-start.5) | collective-permute-done | bytes 4128 | tf_op jit(solution)/shard_map/ppermute | solution.py:152
  76.5 14.0 %collective-permute-start.6 = (bf16[4,1024]{1,0:T(4,128)(2,1)S(1)}, bf16[4,1024]{1,0:T(4,128)(2,1)S(1)}, u32[]{:S(2)}, u32[]{:S(2)}) collective-permute-start(bf16[4,1024]{1,0:T(4,128)(2,1)S(1)} %maximum_select_fusion.6), channel_id=1, source_target_pairs={{0,8},{2,10},{4,12},{6,14},{8,0},{10,2},{12,4},{14,6},{16,24},{18,... | collective-permute-start | bytes 24584 | tf_op jit(solution)/shard_map/ppermute | solution.py:152
  90.6 1.6 %collective-permute-done.6 = bf16[4,1024]{1,0:T(4,128)(2,1)S(1)} collective-permute-done((bf16[4,1024]{1,0:T(4,128)(2,1)S(1)}, bf16[4,1024]{1,0:T(4,128)(2,1)S(1)}, u32[]{:S(2)}, u32[]{:S(2)}) %collective-permute-start.6) | collective-permute-done | bytes 8224 | tf_op jit(solution)/shard_map/ppermute | solution.py:152
  92.2 1.6 %collective-permute-start.7 = (bf16[8,1024]{1,0:T(8,128)(2,1)S(1)}, bf16[8,1024]{1,0:T(8,128)(2,1)S(1)}, u32[]{:S(2)}, u32[]{:S(2)}) collective-permute-start(bf16[8,1024]{1,0:T(8,128)(2,1)S(1)} %maximum_select_fusion.5), channel_id=1, source_target_pairs={{0,16},{2,18},{4,20},{6,22},{8,24},{10,26},{12,28},{14,30},{16,0},... | collective-permute-start | bytes 49160 | tf_op jit(solution)/shard_map/ppermute | solution.py:152
  93.9 2.2 %collective-permute-done.7 = bf16[8,1024]{1,0:T(8,128)(2,1)S(1)} collective-permute-done((bf16[8,1024]{1,0:T(8,128)(2,1)S(1)}, bf16[8,1024]{1,0:T(8,128)(2,1)S(1)}, u32[]{:S(2)}, u32[]{:S(2)}) %collective-permute-start.7) | collective-permute-done | bytes 16416 | tf_op jit(solution)/shard_map/ppermute | solution.py:152
  96.1 2.2 %collective-permute-start.8 = (bf16[16,1024]{1,0:T(8,128)(2,1)S(1)}, bf16[16,1024]{1,0:T(8,128)(2,1)S(1)}, u32[]{:S(2)}, u32[]{:S(2)}) collective-permute-start(bf16[16,1024]{1,0:T(8,128)(2,1)S(1)} %maximum_select_fusion.4), channel_id=1, source_target_pairs={{0,32},{2,34},{4,36},{6,38},{8,40},{10,42},{12,44},{14,46},{16,48}... | collective-permute-start | bytes 98312 | tf_op jit(solution)/shard_map/ppermute | solution.py:152
  98.2 3.3 %collective-permute-done.8 = bf16[16,1024]{1,0:T(8,128)(2,1)S(1)} collective-permute-done((bf16[16,1024]{1,0:T(8,128)(2,1)S(1)}, bf16[16,1024]{1,0:T(8,128)(2,1)S(1)}, u32[]{:S(2)}, u32[]{:S(2)}) %collective-permute-start.8) | collective-permute-done | bytes 32800 | tf_op jit(solution)/shard_map/ppermute | solution.py:152
  101.8 4.5 %collective-permute-done.9 = bf16[32,1024]{1,0:T(8,128)(2,1)S(1)} collective-permute-done((bf16[32,1024]{1,0:T(8,128)(2,1)S(1)}, bf16[32,1024]{1,0:T(8,128)(2,1)S(1)}, u32[]{:S(2)}, u32[]{:S(2)}) %collective-permute-start.9) | collective-permute-done | bytes 65568 | tf_op jit(solution)/shard_map/ppermute | solution.py:152
  106.4 1.3 collective-permute-start.10
  107.7 5.3 %collective-permute-done.10 = bf16[64,1024]{1,0:T(8,128)(2,1)S(1)} collective-permute-done((bf16[64,1024]{1,0:T(8,128)(2,1)S(1)}, bf16[64,1024]{1,0:T(8,128)(2,1)S(1)}, u32[]{:S(2)}, u32[]{:S(2)}) %collective-permute-start.10) | collective-permute-done | bytes 131104 | tf_op jit(solution)/shard_map/ppermute | solution.py:152
  113.0 1.3 convolution_reduce_fusion
  114.3 1.1 collective-permute-done.11
  115.5 1.3 collective-permute-start.12
  116.8 2.2 %collective-permute-done.12 = f32[128]{0:T(128)S(1)} collective-permute-done((f32[128]{0:T(128)S(1)}, f32[128]{0:T(128)S(1)}, u32[]{:S(2)}, u32[]{:S(2)}) %collective-permute-start.12) | collective-permute-done | bytes 544 | tf_op jit(solution)/shard_map/ppermute | solution.py:165
  119.1 2.7 %collective-permute-start.13 = (f32[128]{0:T(128)S(1)}, f32[128]{0:T(128)S(1)}, u32[]{:S(2)}, u32[]{:S(2)}) collective-permute-start(f32[128]{0:T(128)S(1)} %max.28), channel_id=1, source_target_pairs={{0,4},{2,6},{4,0},{6,2},{8,12},{10,14},{12,8},{14,10},{16,20},{18,... | collective-permute-start | bytes 1544 | tf_op jit(solution)/shard_map/ppermute | solution.py:165
  121.8 1.8 %collective-permute-done.13 = f32[128]{0:T(128)S(1)} collective-permute-done((f32[128]{0:T(128)S(1)}, f32[128]{0:T(128)S(1)}, u32[]{:S(2)}, u32[]{:S(2)}) %collective-permute-start.13) | collective-permute-done | bytes 544 | tf_op jit(solution)/shard_map/ppermute | solution.py:165
  123.5 6.4 %collective-permute-start.14 = (f32[128]{0:T(128)S(1)}, f32[128]{0:T(128)S(1)}, u32[]{:S(2)}, u32[]{:S(2)}) collective-permute-start(f32[128]{0:T(128)S(1)} %max.29), channel_id=1, source_target_pairs={{0,8},{2,10},{4,12},{6,14},{8,0},{10,2},{12,4},{14,6},{16,24},{18,... | collective-permute-start | bytes 1544 | tf_op jit(solution)/shard_map/ppermute | solution.py:165
  129.9 1.5 collective-permute-done.14
  131.5 1.4 collective-permute-start.15
  132.8 2.2 %collective-permute-done.15 = f32[128]{0:T(128)S(1)} collective-permute-done((f32[128]{0:T(128)S(1)}, f32[128]{0:T(128)S(1)}, u32[]{:S(2)}, u32[]{:S(2)}) %collective-permute-start.15) | collective-permute-done | bytes 544 | tf_op jit(solution)/shard_map/ppermute | solution.py:165
  135.0 1.5 collective-permute-start.16
  136.5 3.6 %collective-permute-done.16 = f32[128]{0:T(128)S(1)} collective-permute-done((f32[128]{0:T(128)S(1)}, f32[128]{0:T(128)S(1)}, u32[]{:S(2)}, u32[]{:S(2)}) %collective-permute-start.16) | collective-permute-done | bytes 544 | tf_op jit(solution)/shard_map/ppermute | solution.py:165
  140.1 3.6 %collective-permute-done.17 = f32[128]{0:T(128)S(1)} collective-permute-done((f32[128]{0:T(128)S(1)}, f32[128]{0:T(128)S(1)}, u32[]{:S(2)}, u32[]{:S(2)}) %collective-permute-start.17) | collective-permute-done | bytes 544 | tf_op jit(solution)/shard_map/ppermute | solution.py:165
  143.7 0.8 collective-permute-start.18
  144.5 4.3 %collective-permute-done.18 = f32[128]{0:T(128)S(1)} collective-permute-done((f32[128]{0:T(128)S(1)}, f32[128]{0:T(128)S(1)}, u32[]{:S(2)}, u32[]{:S(2)}) %collective-permute-start.18) | collective-permute-done | bytes 544 | tf_op jit(solution)/shard_map/ppermute | solution.py:165
  149.4 1.7 %fusion.85 = f32[512]{0:T(512)S(1)} fusion(bf16[512,1024]{1,0:T(8,128)(2,1)} %collective-permute-done.1, bf16[512,1024]{1,0:T(8,128)(2,1)S(1)} %copy-done.4, bf16[512,1024]{1,0:T(8,128)(2,1)S(1)} %add_convert_fusion.1), kind=kLoop, calls=%fused_computation.105 | loop fusion | flops 3145216 | bytes 3147776 | tf_op jit(solution)/shard_map/reduce_sum | solution.py:14
  151.1 1.8 %multiply_reduce_fusion = f32[512]{0:T(512)S(1)} fusion(f32[512]{0:T(512)S(1)} %broadcast_multiply_fusion, bf16[512,1024]{1,0:T(8,128)(2,1)} %collective-permute-done.1, bf16[512,1024]{1,0:T(8,128)(2,1)S(1)} %copy-done.4, bf16[512,1024]{1,0:T(8,128)(2,1)S(1)} %add_convert_fusion.1), kind=kLoop, calls=%fused_computation.35 | loop fusion | flops 4193792 | bytes 3149824 | tf_op jit(solution)/shard_map/reduce_sum | solution.py:15
  152.9 2.9 %add_convert_fusion = bf16[512,1024]{1,0:T(8,128)(2,1)} fusion(f32[1024]{0:T(1024)S(1)} %bitcast.121, f32[1024]{0:T(1024)S(1)} %bitcast.120, f32[512]{0:T(512)S(1)} %add_rsqrt_fusion, f32[512]{0:T(512)S(1)} %broadcast_multiply_fusion, bf16[512,1024]{1,0:T(8,128)(2,1)} %collective-permute-done.1, bf16[512,1024]{1,0:T(8,128)(2,1)S(1)} %copy-done.4, ...), kind=kLoop, calls=%fused_computation.34 | loop fusion | flops 5242880 | bytes 4206592 | tf_op jit(solution)/shard_map/convert_element_type | solution.py:142
  (88 shorter events, 5.2 us)
Async XLA Ops:
  0.6 49.6 %copy-start = (bf16[1024,1024]{1,0:T(8,128)(2,1)S(1)}, bf16[1024,1024]{1,0:T(8,128)(2,1)}, u32[]{:S(2)}) copy-start(bf16[1024,1024]{1,0:T(8,128)(2,1)} %param.25) | copy-start | bytes 6291460
  3.8 16.0 %copy-start.1 = (bf16[512,512]{0,1:T(8,128)(2,1)}, bf16[512,512]{0,1:T(8,128)(2,1)S(1)}, u32[]{:S(2)}) copy-start(bf16[512,512]{0,1:T(8,128)(2,1)S(1)} %convolution_convert_fusion.3) | copy-start | bytes 1572868
  6.3 2.3 %copy-start.9 = (s32[128]{0:T(128)S(1)}, s32[128]{0:T(128)}, u32[]{:S(2)}) copy-start(s32[128]{0:T(128)} %param.18) | copy-start | bytes 1540
  14.0 2.4 %copy-start.5 = (bf16[1,1024,512]{1,2,0:T(8,128)(2,1)S(1)}, bf16[1,1024,512]{1,2,0:T(8,128)(2,1)}, u32[]{:S(2)}) copy-start(bf16[1,1024,512]{1,2,0:T(8,128)(2,1)} %copy.29) | copy-start | bytes 3145732
  16.4 0.8 copy-start.11
  18.9 28.0 %collective-permute-start.2 = (bf16[1,1024]{1,0:T(2,128)(2,1)S(1)}, bf16[1,1024]{1,0:T(2,128)(2,1)S(1)}, u32[]{:S(2)}, u32[]{:S(2)}) collective-permute-start(bf16[1,1024]{1,0:T(2,128)(2,1)S(1)} %convert_element_type.123), channel_id=1, source_target_pairs={{0,1},{1,0},{2,3},{3,2},{4,5},{5,4},{6,7},{7,6},{8,9},{9,8},{10,11... | collective-permute-start | bytes 6152 | tf_op jit(solution)/shard_map/ppermute | solution.py:21
  21.3 1.8 %copy-start.12 = (bf16[512,512]{0,1:T(8,128)(2,1)S(1)}, bf16[512,512]{0,1:T(8,128)(2,1)}, u32[]{:S(2)}) copy-start(bf16[512,512]{0,1:T(8,128)(2,1)} %copy-done.11) | copy-start | bytes 1572868
  43.3 6.9 %copy-start.7 = (f32[2,1024]{1,0:T(2,128)S(1)}, f32[2,1024]{1,0:T(2,128)}, u32[]{:S(2)}) copy-start(f32[2,1024]{1,0:T(2,128)} %param.28) | copy-start | bytes 24580
  43.3 6.9 %copy-start.8 = (f32[2,1024]{1,0:T(2,128)S(1)}, f32[2,1024]{1,0:T(2,128)}, u32[]{:S(2)}) copy-start(f32[2,1024]{1,0:T(2,128)} %param.27) | copy-start | bytes 24580
  46.4 9.8 %collective-permute-start = (bf16[512,1024]{1,0:T(8,128)(2,1)}, bf16[512,1024]{1,0:T(8,128)(2,1)}, u32[]{:S(2)}, u32[]{:S(2)}) collective-permute-start(bf16[512,1024]{1,0:T(8,128)(2,1)} %convolution_convert_fusion.1), channel_id=1, source_target_pairs={{0,1},{1,0},{2,3},{3,2},{4,5},{5,4},{6,7},{7,6},{8,9},{9,8},{10,11... | collective-permute-start | bytes 3145736 | tf_op jit(solution)/shard_map/ppermute | solution.py:21
  50.2 1.6 %copy-start.6 = (bf16[1024,1024]{1,0:T(8,128)(2,1)S(1)}, bf16[1024,1024]{1,0:T(8,128)(2,1)}, u32[]{:S(2)}) copy-start(bf16[1024,1024]{1,0:T(8,128)(2,1)} %param.26) | copy-start | bytes 6291460
  50.2 5.9 %copy-start.2 = (bf16[512,1024]{1,0:T(8,128)(2,1)S(1)}, bf16[512,1024]{1,0:T(8,128)(2,1)}, u32[]{:S(2)}) copy-start(bf16[512,1024]{1,0:T(8,128)(2,1)} %param.16) | copy-start | bytes 3145732
  52.2 1.3 collective-permute-start.3
  56.0 15.6 %collective-permute-start.4 = (bf16[1,1024]{1,0:T(2,128)(2,1)S(1)}, bf16[1,1024]{1,0:T(2,128)(2,1)S(1)}, u32[]{:S(2)}, u32[]{:S(2)}) collective-permute-start(bf16[1,1024]{1,0:T(2,128)(2,1)S(1)} %get-tuple-element.84), channel_id=1, source_target_pairs={{0,2},{2,0},{4,6},{6,4},{8,10},{10,8},{12,14},{14,12},{16,18},{18,... | collective-permute-start | bytes 6152 | tf_op jit(solution)/shard_map/ppermute | solution.py:152
  58.2 2.3 %copy-start.3 = (bf16[512,1024]{1,0:T(8,128)(2,1)S(1)}, bf16[512,1024]{1,0:T(8,128)(2,1)}, u32[]{:S(2)}) copy-start(bf16[512,1024]{1,0:T(8,128)(2,1)} %param.16) | copy-start | bytes 3145732
  71.5 77.9 %collective-permute-start.1 = (bf16[512,1024]{1,0:T(8,128)(2,1)}, bf16[512,1024]{1,0:T(8,128)(2,1)}, u32[]{:S(2)}, u32[]{:S(2)}) collective-permute-start(bf16[512,1024]{1,0:T(8,128)(2,1)} %convolution_convert_fusion), channel_id=1, source_target_pairs={{0,1},{1,0},{2,3},{3,2},{4,5},{5,4},{6,7},{7,6},{8,9},{9,8},{10,11... | collective-permute-start | bytes 3145736 | tf_op jit(solution)/shard_map/ppermute | solution.py:21
  71.7 4.8 %collective-permute-start.5 = (bf16[2,1024]{1,0:T(2,128)(2,1)S(1)}, bf16[2,1024]{1,0:T(2,128)(2,1)S(1)}, u32[]{:S(2)}, u32[]{:S(2)}) collective-permute-start(bf16[2,1024]{1,0:T(2,128)(2,1)S(1)} %broadcast_select_fusion), channel_id=1, source_target_pairs={{0,4},{2,6},{4,0},{6,2},{8,12},{10,14},{12,8},{14,10},{16,20},{18,... | collective-permute-start | bytes 12296 | tf_op jit(solution)/shard_map/ppermute | solution.py:152
  76.5 15.7 %collective-permute-start.6 = (bf16[4,1024]{1,0:T(4,128)(2,1)S(1)}, bf16[4,1024]{1,0:T(4,128)(2,1)S(1)}, u32[]{:S(2)}, u32[]{:S(2)}) collective-permute-start(bf16[4,1024]{1,0:T(4,128)(2,1)S(1)} %maximum_select_fusion.6), channel_id=1, source_target_pairs={{0,8},{2,10},{4,12},{6,14},{8,0},{10,2},{12,4},{14,6},{16,24},{18,... | collective-permute-start | bytes 24584 | tf_op jit(solution)/shard_map/ppermute | solution.py:152
  92.2 3.8 %collective-permute-start.7 = (bf16[8,1024]{1,0:T(8,128)(2,1)S(1)}, bf16[8,1024]{1,0:T(8,128)(2,1)S(1)}, u32[]{:S(2)}, u32[]{:S(2)}) collective-permute-start(bf16[8,1024]{1,0:T(8,128)(2,1)S(1)} %maximum_select_fusion.5), channel_id=1, source_target_pairs={{0,16},{2,18},{4,20},{6,22},{8,24},{10,26},{12,28},{14,30},{16,0},... | collective-permute-start | bytes 49160 | tf_op jit(solution)/shard_map/ppermute | solution.py:152
  96.1 5.5 %collective-permute-start.8 = (bf16[16,1024]{1,0:T(8,128)(2,1)S(1)}, bf16[16,1024]{1,0:T(8,128)(2,1)S(1)}, u32[]{:S(2)}, u32[]{:S(2)}) collective-permute-start(bf16[16,1024]{1,0:T(8,128)(2,1)S(1)} %maximum_select_fusion.4), channel_id=1, source_target_pairs={{0,32},{2,34},{4,36},{6,38},{8,40},{10,42},{12,44},{14,46},{16,48}... | collective-permute-start | bytes 98312 | tf_op jit(solution)/shard_map/ppermute | solution.py:152
  101.6 4.8 %collective-permute-start.9 = (bf16[32,1024]{1,0:T(8,128)(2,1)S(1)}, bf16[32,1024]{1,0:T(8,128)(2,1)S(1)}, u32[]{:S(2)}, u32[]{:S(2)}) collective-permute-start(bf16[32,1024]{1,0:T(8,128)(2,1)S(1)} %maximum_select_fusion.3), channel_id=1, source_target_pairs={{0,64},{2,66},{4,68},{6,70},{8,72},{10,74},{12,76},{14,78},{16,80}... | collective-permute-start | bytes 196616 | tf_op jit(solution)/shard_map/ppermute | solution.py:152
  106.4 6.6 %collective-permute-start.10 = (bf16[64,1024]{1,0:T(8,128)(2,1)S(1)}, bf16[64,1024]{1,0:T(8,128)(2,1)S(1)}, u32[]{:S(2)}, u32[]{:S(2)}) collective-permute-start(bf16[64,1024]{1,0:T(8,128)(2,1)S(1)} %maximum_select_fusion.2), channel_id=1, source_target_pairs={{0,128},{2,130},{4,132},{6,134},{8,136},{10,138},{12,140},{14,142}... | collective-permute-start | bytes 393224 | tf_op jit(solution)/shard_map/ppermute | solution.py:152
  107.7 41.7 %copy-start.4 = (bf16[512,1024]{1,0:T(8,128)(2,1)S(1)}, bf16[512,1024]{1,0:T(8,128)(2,1)}, u32[]{:S(2)}) copy-start(bf16[512,1024]{1,0:T(8,128)(2,1)} %convolution_convert_fusion) | copy-start | bytes 3145732
  114.2 38.7 %copy-start.10 = (f32[128]{0:T(128)}, f32[128]{0:T(128)S(1)}, u32[]{:S(2)}) copy-start(f32[128]{0:T(128)S(1)} %convolution_reduce_fusion) | copy-start | bytes 1540
  114.2 1.2 collective-permute-start.11
  115.5 3.6 %collective-permute-start.12 = (f32[128]{0:T(128)S(1)}, f32[128]{0:T(128)S(1)}, u32[]{:S(2)}, u32[]{:S(2)}) collective-permute-start(f32[128]{0:T(128)S(1)} %max.27), channel_id=1, source_target_pairs={{0,2},{2,0},{4,6},{6,4},{8,10},{10,8},{12,14},{14,12},{16,18},{18,... | collective-permute-start | bytes 1544 | tf_op jit(solution)/shard_map/ppermute | solution.py:165
  119.1 4.5 %collective-permute-start.13 = (f32[128]{0:T(128)S(1)}, f32[128]{0:T(128)S(1)}, u32[]{:S(2)}, u32[]{:S(2)}) collective-permute-start(f32[128]{0:T(128)S(1)} %max.28), channel_id=1, source_target_pairs={{0,4},{2,6},{4,0},{6,2},{8,12},{10,14},{12,8},{14,10},{16,20},{18,... | collective-permute-start | bytes 1544 | tf_op jit(solution)/shard_map/ppermute | solution.py:165
  123.5 7.9 %collective-permute-start.14 = (f32[128]{0:T(128)S(1)}, f32[128]{0:T(128)S(1)}, u32[]{:S(2)}, u32[]{:S(2)}) collective-permute-start(f32[128]{0:T(128)S(1)} %max.29), channel_id=1, source_target_pairs={{0,8},{2,10},{4,12},{6,14},{8,0},{10,2},{12,4},{14,6},{16,24},{18,... | collective-permute-start | bytes 1544 | tf_op jit(solution)/shard_map/ppermute | solution.py:165
  131.5 3.6 %collective-permute-start.15 = (f32[128]{0:T(128)S(1)}, f32[128]{0:T(128)S(1)}, u32[]{:S(2)}, u32[]{:S(2)}) collective-permute-start(f32[128]{0:T(128)S(1)} %max.30), channel_id=1, source_target_pairs={{0,16},{2,18},{4,20},{6,22},{8,24},{10,26},{12,28},{14,30},{16,0},... | collective-permute-start | bytes 1544 | tf_op jit(solution)/shard_map/ppermute | solution.py:165
  135.0 5.1 %collective-permute-start.16 = (f32[128]{0:T(128)S(1)}, f32[128]{0:T(128)S(1)}, u32[]{:S(2)}, u32[]{:S(2)}) collective-permute-start(f32[128]{0:T(128)S(1)} %max.31), channel_id=1, source_target_pairs={{0,32},{2,34},{4,36},{6,38},{8,40},{10,42},{12,44},{14,46},{16,48}... | collective-permute-start | bytes 1544 | tf_op jit(solution)/shard_map/ppermute | solution.py:165
  140.1 3.6 %collective-permute-start.17 = (f32[128]{0:T(128)S(1)}, f32[128]{0:T(128)S(1)}, u32[]{:S(2)}, u32[]{:S(2)}) collective-permute-start(f32[128]{0:T(128)S(1)} %max.32), channel_id=1, source_target_pairs={{0,64},{2,66},{4,68},{6,70},{8,72},{10,74},{12,76},{14,78},{16,80}... | collective-permute-start | bytes 1544 | tf_op jit(solution)/shard_map/ppermute | solution.py:165
  143.7 5.1 %collective-permute-start.18 = (f32[128]{0:T(128)S(1)}, f32[128]{0:T(128)S(1)}, u32[]{:S(2)}, u32[]{:S(2)}) collective-permute-start(f32[128]{0:T(128)S(1)} %max.33), channel_id=1, source_target_pairs={{0,128},{2,130},{4,132},{6,134},{8,136},{10,138},{12,140},{14,142}... | collective-permute-start | bytes 1544 | tf_op jit(solution)/shard_map/ppermute | solution.py:165

commit v3 on v1

v3 whole, which is shorter than its diff:
```python
import jax
import jax.numpy as jnp
from jax import lax
from jax.experimental import pallas as pl
from jax.experimental.pallas import tpu as pltpu
from jax.sharding import PartitionSpec as P

HD = 64


def normalize(rows, gain, bias):
    center = rows - jnp.mean(rows, axis=-1, keepdims=True)
    spread = jnp.mean(center * center, axis=-1, keepdims=True)
    return center * lax.rsqrt(spread + 1e-05) * gain + bias


def pair_sum(partial):
    own = partial.astype(jnp.bfloat16)
    other = lax.ppermute(own, "tp", [(0, 1), (1, 0)])
    return own.astype(jnp.float32) + other.astype(jnp.float32)


PAIR = 2 * HD
ROWS = 256


def attention_kernel(lens_ref, q_ref, kc_ref, vc_ref, kn_ref, vn_ref, out_ref):
    cached = lens_ref[0]
    valid = lens_ref[1]
    row0 = pl.program_id(1) * ROWS
    q = q_ref[...]
    kc = kc_ref[...]
    vc = vc_ref[...]
    kn = kn_ref[...]
    vn = vn_ref[...]
    lanes = lax.broadcasted_iota(jnp.int32, q.shape, 1)
    cache_cols = lax.broadcasted_iota(jnp.int32, (q.shape[0], kc.shape[0]), 1)
    cache_ok = cache_cols < cached
    new_cols = lax.broadcasted_iota(jnp.int32, (q.shape[0], kn.shape[0]), 1)
    new_rows = lax.broadcasted_iota(jnp.int32, (q.shape[0], kn.shape[0]), 0) + row0
    new_ok = (new_cols <= new_rows) & (new_cols < valid)
    scale = 1.0 / float(HD) ** 0.5
    dims = (((1,), (1,)), ((), ()))
    result = jnp.zeros(q.shape, jnp.float32)
    for head in range(2):
        mine = (lanes // HD) == head
        qh = jnp.where(mine, q, jnp.zeros_like(q))
        s_c = lax.dot_general(qh, kc, dims, preferred_element_type=jnp.float32) * scale
        s_n = lax.dot_general(qh, kn, dims, preferred_element_type=jnp.float32) * scale
        s_c = jnp.where(cache_ok, s_c, -jnp.inf)
        s_n = jnp.where(new_ok, s_n, -jnp.inf)
        peak = jnp.maximum(jnp.max(s_c, axis=1, keepdims=True), jnp.max(s_n, axis=1, keepdims=True))
        e_c = jnp.exp(s_c - peak)
        e_n = jnp.exp(s_n - peak)
        total = jnp.sum(e_c, axis=1, keepdims=True) + jnp.sum(e_n, axis=1, keepdims=True)
        mixed = jnp.dot(e_c.astype(jnp.bfloat16), vc, preferred_element_type=jnp.float32) + jnp.dot(
            e_n.astype(jnp.bfloat16), vn, preferred_element_type=jnp.float32
        )
        result = jnp.where(mine, mixed / total, result)
    out_ref[...] = result.astype(out_ref.dtype)


def attention(lens, queries, cache_k, cache_v, keys_new, values_new):
    rows, width = queries.shape
    cache_rows = cache_k.shape[0]
    pairs = width // PAIR
    chunks = rows // ROWS
    flops = 4 * rows * (cache_rows + rows) * width * 2
    return pl.pallas_call(
        attention_kernel,
        out_shape=jax.ShapeDtypeStruct((rows, width), jnp.bfloat16),
        grid_spec=pltpu.PrefetchScalarGridSpec(
            num_scalar_prefetch=1,
            grid=(pairs, chunks),
            in_specs=[
                pl.BlockSpec((ROWS, PAIR), lambda p, r, lens: (r, p)),
                pl.BlockSpec((cache_rows, PAIR), lambda p, r, lens: (0, p)),
                pl.BlockSpec((cache_rows, PAIR), lambda p, r, lens: (0, p)),
                pl.BlockSpec((rows, PAIR), lambda p, r, lens: (0, p)),
                pl.BlockSpec((rows, PAIR), lambda p, r, lens: (0, p)),
            ],
            out_specs=pl.BlockSpec((ROWS, PAIR), lambda p, r, lens: (r, p)),
        ),
        cost_estimate=pl.CostEstimate(
            flops=flops,
            transcendentals=rows * (cache_rows + rows) * width // HD,
            bytes_accessed=2 * (2 * rows * width + 2 * cache_rows * width + 2 * rows * width),
        ),
    )(lens, queries, cache_k, cache_v, keys_new, values_new)


def shards(
    tokens,
    group_len,
    cache_len,
    cache_keys,
    cache_values,
    w_query,
    w_key,
    w_value,
    w_out,
    w_up,
    w_down,
    ln_gains,
    ln_biases,
    embed,
):
    block_rows = tokens.shape[0]
    local_width = w_query.shape[1]
    my_index = lax.axis_index("req")
    my_cache = lax.dynamic_index_in_dim(cache_len, my_index, 0, keepdims=False)
    my_valid = group_len[0]
    queries = jnp.dot(tokens, w_query, preferred_element_type=jnp.float32).astype(jnp.bfloat16)
    keys_new = jnp.dot(tokens, w_key, preferred_element_type=jnp.float32).astype(jnp.bfloat16)
    values_new = jnp.dot(tokens, w_value, preferred_element_type=jnp.float32).astype(jnp.bfloat16)
    lens = jnp.stack([my_cache, my_valid]).astype(jnp.int32)
    attn_mixed = attention(lens, queries, cache_keys[0], cache_values[0], keys_new, values_new)
    attn_sum = pair_sum(jnp.dot(attn_mixed, w_out, preferred_element_type=jnp.float32))
    middle = normalize(tokens.astype(jnp.float32) + attn_sum, ln_gains[0], ln_biases[0]).astype(
        jnp.bfloat16
    )
    active = jax.nn.gelu(
        jnp.dot(middle, w_up, preferred_element_type=jnp.float32), approximate=False
    ).astype(jnp.bfloat16)
    ffn_sum = pair_sum(jnp.dot(active, w_down, preferred_element_type=jnp.float32))
    layer_out = normalize(middle.astype(jnp.float32) + ffn_sum, ln_gains[1], ln_biases[1]).astype(
        jnp.bfloat16
    )
    last_row = lax.dynamic_slice_in_dim(layer_out, my_valid - 1, 1, 0)
    reqs = cache_len.shape[0]
    all_rows = lax.all_to_all(
        jnp.broadcast_to(last_row, (reqs, last_row.shape[1])), "req", 0, 0, tiled=True
    )
    logits = jnp.einsum("rd,vd->rv", all_rows, embed, preferred_element_type=jnp.float32)
    slice_best = jnp.max(logits, axis=1)
    mine = jnp.max(lax.all_to_all(slice_best[:, None], "req", 0, 0, tiled=True), axis=0)
    best_logit = jnp.maximum(mine, lax.ppermute(mine, "tp", [(0, 1), (1, 0)]))
    return (layer_out, best_logit, slice_best[:, None])


def solution(mesh):
    placed = (
        P("req", None),
        P("req"),
        P(),
        P("req", None, "tp"),
        P("req", None, "tp"),
        P(None, "tp"),
        P(None, "tp"),
        P(None, "tp"),
        P("tp", None),
        P(None, "tp"),
        P("tp", None),
        P(),
        P(),
        P(("req", "tp"), None),
    )
    return jax.shard_map(
        shards,
        mesh=mesh,
        in_specs=placed,
        out_specs=(P("req", None), P("req"), P(None, ("req", "tp"))),
        check_vma=False,
    )
```

time: 130 us -> 109 us (0.84)
  blocking collectives: 62 us -> 44.3 us
  Pallas kernels: 0 us -> 15.5 us
  matrix products: 27.2 us -> 17.4 us
  local copies, waits for them, and re-layouts: 9.04 us -> 3.52 us
  other arithmetic: 14.1 us -> 11.7 us
    all_to_all x1, blocking collectives: 45.4 us -> 27.7 us  [shards(): lax.all_to_all(jnp.broadcast_to(last_row, (reqs, last_row.shape[1])), 're...]
    pallas_call x0 -> x1, Pallas kernels: none -> 15.5 us  [attention(): pl.pallas_call(attention_kernel, out_shape=jax.ShapeDtypeStruct((rows, wi...]
    dot_general x4 -> x0, matrix products: 11.5 us -> none  [the longest x2 7.89 us: attend(): jnp.einsum('qhk,khd->qhd', raised.astype(jnp.bfloat16), values_blk, prefe...]
    unnamed x32 -> x26, local copies, waits for them, and re-layouts: 6.63 us -> 1.99 us
    reduce_sum x2 -> x0, other arithmetic: 2.65 us -> none  [attend(): new_total = row_total * factor + jnp.sum(raised, axis=-1)]
where the time goes in v3:
time: 109 us
  blocking collectives  44.3 us (41%)
  matrix products  17.4 us (16%)
  Pallas kernels  15.5 us (14%)
  other arithmetic  11.7 us (11%)
  starting transfers between devices  6.43 us (6%)
  waiting for transfers between devices  5.83 us (5%)
  between operations  4.06 us (4%)
  local copies, waits for them, and re-layouts  3.52 us (3%)
    all_to_all x1, blocking collectives, shards(): lax.all_to_all(jnp.broadcast_to(last_row, (reqs, last_row.shape[1])), 're...  27.7 us
    all_to_all x1, blocking collectives, shards(): lax.all_to_all(slice_best[:, None], 'req', 0, 0, tiled=True)  16.6 us
    pallas_call x1, Pallas kernels, attention(): pl.pallas_call(attention_kernel, out_shape=jax.ShapeDtypeStruct((rows, wi...  15.5 us
    dot_general x1, matrix products, shards(): jnp.dot(active, w_down, preferred_element_type=jnp.float32)  8.8 us
    ppermute x2, waiting for transfers between devices, pair_sum(): other = lax.ppermute(own, 'tp', [(0, 1), (1, 0)])  4.87 us
    ppermute x2, starting transfers between devices, pair_sum(): other = lax.ppermute(own, 'tp', [(0, 1), (1, 0)])  3.84 us
    dot_general x1, matrix products, shards(): jnp.dot(tokens, w_query, preferred_element_type=jnp.float32)  3.16 us
    ppermute x1, starting transfers between devices, shards(): best_logit = jnp.maximum(mine, lax.ppermute(mine, 'tp', [(0, 1), (1, 0)]))  2.59 us
  transfers between devices with their start and end apart: 3, of which 3 were waited for; matrix products, arithmetic and copies ran while one was open for 0% of the time, Pallas kernels for 0%

profile of v3, /device:TPU:1, one launch (start us, length us, event | category | flops | bytes accessed | tf_op | source)
XLA Modules:
  0.0 108.7 jit_solution(14320274016092913409)
XLA Ops:
  0.6 0.0 copy-start
  0.6 0.0 copy-start.1
  1.5 0.0 copy-start.8
  1.5 3.2 %convolution_convert_fusion.4.q_ref = bf16[512,512]{1,0:T(8,128)(2,1)} fusion(bf16[512,1024]{1,0:T(8,128)(2,1)} %param.14, bf16[1024,512]{1,0:T(8,128)(2,1)} %param.19), kind=kOutput, calls=%fused_computation.29 | convolution fusion | flops 537133056 | bytes 2621440 | tf_op jit(solution)/shard_map/dot_general | solution.py:113
  4.6 0.0 copy-done.1
  4.6 0.0 copy-done.8
  4.6 0.0 copy-start.9
  4.6 1.5 %convolution_convert_fusion.3.kn_ref = bf16[512,512]{1,0:T(8,128)(2,1)} fusion(bf16[512,1024]{1,0:T(8,128)(2,1)S(1)} %copy-done.1, bf16[1024,512]{1,0:T(8,128)(2,1)S(1)} %copy-done.8), kind=kOutput, calls=%fused_computation.28 | convolution fusion | flops 537133056 | bytes 2621440 | tf_op jit(solution)/shard_map/dot_general | solution.py:114
  6.1 0.0 copy-done.9
  6.1 0.0 copy-start.11
  6.1 1.5 %convolution_convert_fusion.2.vn_ref = bf16[512,512]{1,0:T(8,128)(2,1)} fusion(bf16[512,1024]{1,0:T(8,128)(2,1)S(1)} %copy-done.1, bf16[1024,512]{1,0:T(8,128)(2,1)S(1)} %copy-done.9), kind=kOutput, calls=%fused_computation.27 | convolution fusion | flops 537133056 | bytes 2621440 | tf_op jit(solution)/shard_map/dot_general | solution.py:115
  7.7 0.0 copy-done.11
  7.7 0.6 dynamic_slice.9
  8.2 1.2 %pad_add_fusion.lens_ref = s32[2]{0:T(128)} fusion(s32[1]{0:T(128)S(6)} %copy.23, s32[1]{0:T(128)} %dynamic_slice.9), kind=kLoop, calls=%fused_computation.70 | loop fusion | flops 2 | bytes 16 | tf_op jit(solution)/shard_map/stack | solution.py:116
  9.5 15.5 %shard_map.157 = bf16[512,512]{1,0:T(8,128)(2,1)} custom-call(s32[2]{0:T(128)} %pad_add_fusion.lens_ref, bf16[512,512]{1,0:T(8,128)(2,1)} %convolution_convert_fusion.4.q_ref, bf16[1024,512]{1,0:T(8,128)(2,1)} %bitcast.32, bf16[1024,512]{1,0:T(8,128)(2,1)} %bitcast.33, bf16[512,512]{1,0:T(8,128)(2,1)} %convolution_convert_fusion.3.kn_ref, ...), custom_call_target="tpu_custom_call" | custom-call | flops 3221225472 | bytes 4194304 | tf_op jit(solution)/shard_map/pallas_call | solution.py:69
  25.0 0.0 copy-start.5
  25.0 0.0 copy-start.6
  25.0 2.1 %convolution_convert_fusion.1 = bf16[512,1024]{1,0:T(8,128)(2,1)S(1)} fusion(bf16[512,512]{1,0:T(8,128)(2,1)} %shard_map.157, bf16[512,1024]{1,0:T(8,128)(2,1)} %param.22), kind=kOutput, calls=%fused_computation.26 | convolution fusion | flops 537395200 | bytes 2621440 | tf_op jit(solution)/shard_map/dot_general | solution.py:118
  27.1 3.5 %collective-permute-start = (bf16[512,1024]{1,0:T(8,128)(2,1)S(1)}, bf16[512,1024]{1,0:T(8,128)(2,1)S(1)}, u32[]{:S(2)}, u32[]{:S(2)}) collective-permute-start(bf16[512,1024]{1,0:T(8,128)(2,1)S(1)} %convolution_convert_fusion.1), channel_id=1, source_target_pairs={{0,1},{1,0},{2,3},{3,2},{4,5},{5,4},{6,7},{7,6},{8,9},{9,8},{10,11... | collective-permute-start | bytes 3145736 | tf_op jit(solution)/shard_map/ppermute | solution.py:19
  30.5 0.0 copy-done.5
  30.6 0.0 copy-done.6
  30.6 2.2 %collective-permute-done = bf16[512,1024]{1,0:T(8,128)(2,1)S(1)} collective-permute-done((bf16[512,1024]{1,0:T(8,128)(2,1)S(1)}, bf16[512,1024]{1,0:T(8,128)(2,1)S(1)}, u32[]{:S(2)}, u32[]{:S(2)}) %collective-permute-start) | collective-permute-done | bytes 1048608 | tf_op jit(solution)/shard_map/ppermute | solution.py:19
  32.8 0.5 fusion.41
  33.3 0.0 copy-start.2
  33.3 0.6 multiply_reduce_fusion.1
  34.0 0.6 copy-done.2
  34.5 0.7 add_convert_fusion.1
  35.2 0.0 copy-done
  35.2 8.8 %convolution_convert_fusion = bf16[512,1024]{1,0:T(8,128)(2,1)} fusion(bf16[1024,1024]{1,0:T(8,128)(2,1)S(1)} %copy-done, bf16[512,1024]{1,0:T(8,128)(2,1)S(1)} %add_convert_fusion.1, bf16[1024,1024]{1,0:T(8,128)(2,1)} %param.23), kind=kOutput, calls=%fused_computation.25 | convolution fusion | flops 2182086656 | bytes 6291456 | tf_op jit(solution)/shard_map/dot_general | solution.py:125
  44.0 0.4 collective-permute-start.1
  44.4 0.0 copy-start.3
  44.4 2.6 %collective-permute-done.1 = bf16[512,1024]{1,0:T(8,128)(2,1)} collective-permute-done((bf16[512,1024]{1,0:T(8,128)(2,1)}, bf16[512,1024]{1,0:T(8,128)(2,1)}, u32[]{:S(2)}, u32[]{:S(2)}) %collective-permute-start.1) | collective-permute-done | bytes 1048608 | tf_op jit(solution)/shard_map/ppermute | solution.py:19
  47.0 2.0 %fusion.42 = f32[512]{0:T(512)S(1)} fusion(bf16[512,1024]{1,0:T(8,128)(2,1)} %collective-permute-done.1, bf16[512,1024]{1,0:T(8,128)(2,1)} %convolution_convert_fusion, bf16[512,1024]{1,0:T(8,128)(2,1)S(1)} %add_convert_fusion.1), kind=kLoop, calls=%fused_computation.62 | loop fusion | flops 3145216 | bytes 3147776 | tf_op jit(solution)/shard_map/reduce_sum | solution.py:12
  49.1 0.0 copy-done.3
  49.1 1.8 %multiply_reduce_fusion = f32[512]{0:T(512)S(1)} fusion(f32[512]{0:T(512)S(1)} %broadcast_multiply_fusion, bf16[512,1024]{1,0:T(8,128)(2,1)} %collective-permute-done.1, bf16[512,1024]{1,0:T(8,128)(2,1)S(1)} %copy-done.3, bf16[512,1024]{1,0:T(8,128)(2,1)S(1)} %add_convert_fusion.1), kind=kLoop, calls=%fused_computation.5 | loop fusion | flops 4193792 | bytes 3149824 | tf_op jit(solution)/shard_map/reduce_sum | solution.py:13
  50.9 1.9 %add_convert_fusion = bf16[512,1024]{1,0:T(8,128)(2,1)S(1)} fusion(f32[1024]{0:T(1024)S(1)} %bitcast.26, f32[1024]{0:T(1024)S(1)} %bitcast.27, f32[512]{0:T(512)S(1)} %add_rsqrt_fusion, f32[512]{0:T(512)S(1)} %broadcast_multiply_fusion, bf16[512,1024]{1,0:T(8,128)(2,1)} %collective-permute-done.1, bf16[512,1024]{1,0:T(8,128)(2,1)S(1)} %copy-done.3, ...), kind=kLoop, calls=%fused_computation.4 | loop fusion | flops 5242880 | bytes 4206592 | tf_op jit(solution)/shard_map/convert_element_type | solution.py:126
  52.8 0.0 copy-start.4
  52.9 1.0 copy-done.4
  53.8 0.0 copy-start.10
  53.8 0.3 broadcast_in_dim.4
  54.1 0.5 broadcast.61
  54.6 2.1 %reduce.4 = bf16[128,1024]{1,0:T(8,128)(2,1)S(1)} reduce(bf16[128,1,1024]{2,1,0:T(2,128)(2,1)S(1)} %broadcast_in_dim.4, bf16[]{:T(256)} %broadcast.61), dimensions={1}, to_apply=%broadcast_in_dim.4.reduce_sub_computation | reduce | bytes 524290 | tf_op jit(solution)/shard_map/broadcast_in_dim | solution.py:132
  56.8 0.2 reshape.45
  57.0 27.7 %all_to_all.18 = bf16[128,2,512]{2,1,0:T(2,128)(2,1)S(1)} all-to-all(bf16[128,2,512]{2,1,0:T(2,128)(2,1)S(1)} %reshape.45), channel_id=1, replica_groups=mesh['req'=128,'tp'=2] {'req'}, dimensions={0} | all-to-all | bytes 524288 | tf_op jit(solution)/shard_map/all_to_all | solution.py:131
  84.7 0.2 reshape.46
  84.9 0.0 copy-done.10
  84.9 0.3 convolution_reduce_fusion
  85.2 0.0 copy-start.7
  85.3 0.1 copy.17
  85.4 16.6 %all_to_all.19 = f32[128,1,1]{2,1,0:T(1,128)S(1)} all-to-all(f32[128,1,1]{2,1,0:T(1,128)S(1)} %copy.17), channel_id=1, replica_groups=mesh['req'=128,'tp'=2] {'req'}, dimensions={0} | all-to-all | bytes 1024 | tf_op jit(solution)/shard_map/all_to_all | solution.py:136
  102.0 0.7 reduce_max.21
  102.7 2.6 %collective-permute-start.2 = (f32[1]{0:T(128)}, f32[1]{0:T(128)}, u32[]{:S(2)}, u32[]{:S(2)}) collective-permute-start(f32[1]{0:T(128)} %bitcast.9), channel_id=1, source_target_pairs={{0,1},{1,0},{2,3},{3,2},{4,5},{5,4},{6,7},{7,6},{8,9},{9,8},{10,11... | collective-permute-start | bytes 20 | tf_op jit(solution)/shard_map/ppermute | solution.py:137
  105.3 1.0 collective-permute-done.2
  107.6 0.0 copy-done.7
  (7 shorter events, 0.1 us)
Async XLA Ops:
  0.6 34.6 %copy-start = (bf16[1024,1024]{1,0:T(8,128)(2,1)S(1)}, bf16[1024,1024]{1,0:T(8,128)(2,1)}, u32[]{:S(2)}) copy-start(bf16[1024,1024]{1,0:T(8,128)(2,1)} %param.24) | copy-start | bytes 6291460
  0.6 4.0 %copy-start.1 = (bf16[512,1024]{1,0:T(8,128)(2,1)S(1)}, bf16[512,1024]{1,0:T(8,128)(2,1)}, u32[]{:S(2)}) copy-start(bf16[512,1024]{1,0:T(8,128)(2,1)} %param.14) | copy-start | bytes 3145732
  1.5 3.2 %copy-start.8 = (bf16[1024,512]{1,0:T(8,128)(2,1)S(1)}, bf16[1024,512]{1,0:T(8,128)(2,1)}, u32[]{:S(2)}) copy-start(bf16[1024,512]{1,0:T(8,128)(2,1)} %param.20) | copy-start | bytes 3145732
  4.6 1.5 %copy-start.9 = (bf16[1024,512]{1,0:T(8,128)(2,1)S(1)}, bf16[1024,512]{1,0:T(8,128)(2,1)}, u32[]{:S(2)}) copy-start(bf16[1024,512]{1,0:T(8,128)(2,1)} %param.21) | copy-start | bytes 3145732
  6.1 1.5 %copy-start.11 = (s32[128]{0:T(128)S(1)}, s32[128]{0:T(128)}, u32[]{:S(2)}) copy-start(s32[128]{0:T(128)} %param.16) | copy-start | bytes 1540
  25.0 5.6 %copy-start.5 = (f32[2,1024]{1,0:T(2,128)S(1)}, f32[2,1024]{1,0:T(2,128)}, u32[]{:S(2)}) copy-start(f32[2,1024]{1,0:T(2,128)} %param.26) | copy-start | bytes 24580
  25.0 5.6 %copy-start.6 = (f32[2,1024]{1,0:T(2,128)S(1)}, f32[2,1024]{1,0:T(2,128)}, u32[]{:S(2)}) copy-start(f32[2,1024]{1,0:T(2,128)} %param.25) | copy-start | bytes 24580
  27.1 5.7 %collective-permute-start = (bf16[512,1024]{1,0:T(8,128)(2,1)S(1)}, bf16[512,1024]{1,0:T(8,128)(2,1)S(1)}, u32[]{:S(2)}, u32[]{:S(2)}) collective-permute-start(bf16[512,1024]{1,0:T(8,128)(2,1)S(1)} %convolution_convert_fusion.1), channel_id=1, source_target_pairs={{0,1},{1,0},{2,3},{3,2},{4,5},{5,4},{6,7},{7,6},{8,9},{9,8},{10,11... | collective-permute-start | bytes 3145736 | tf_op jit(solution)/shard_map/ppermute | solution.py:19
  33.3 1.2 %copy-start.2 = (bf16[512,1024]{1,0:T(8,128)(2,1)S(1)}, bf16[512,1024]{1,0:T(8,128)(2,1)}, u32[]{:S(2)}) copy-start(bf16[512,1024]{1,0:T(8,128)(2,1)} %param.14) | copy-start | bytes 3145732
  44.0 3.0 %collective-permute-start.1 = (bf16[512,1024]{1,0:T(8,128)(2,1)}, bf16[512,1024]{1,0:T(8,128)(2,1)}, u32[]{:S(2)}, u32[]{:S(2)}) collective-permute-start(bf16[512,1024]{1,0:T(8,128)(2,1)} %convolution_convert_fusion), channel_id=1, source_target_pairs={{0,1},{1,0},{2,3},{3,2},{4,5},{5,4},{6,7},{7,6},{8,9},{9,8},{10,11... | collective-permute-start | bytes 3145736 | tf_op jit(solution)/shard_map/ppermute | solution.py:19
  44.4 4.7 %copy-start.3 = (bf16[512,1024]{1,0:T(8,128)(2,1)S(1)}, bf16[512,1024]{1,0:T(8,128)(2,1)}, u32[]{:S(2)}) copy-start(bf16[512,1024]{1,0:T(8,128)(2,1)} %convolution_convert_fusion) | copy-start | bytes 3145732
  52.8 1.0 copy-start.4
  53.8 31.1 %copy-start.10 = (bf16[192,1024]{1,0:T(8,128)(2,1)S(1)}, bf16[192,1024]{1,0:T(8,128)(2,1)}, u32[]{:S(2)}) copy-start(bf16[192,1024]{1,0:T(8,128)(2,1)} %param.27) | copy-start | bytes 1179652
  85.2 22.4 %copy-start.7 = (f32[128]{0:T(128)}, f32[128]{0:T(128)S(1)}, u32[]{:S(2)}) copy-start(f32[128]{0:T(128)S(1)} %convolution_reduce_fusion) | copy-start | bytes 1540
  102.7 3.5 %collective-permute-start.2 = (f32[1]{0:T(128)}, f32[1]{0:T(128)}, u32[]{:S(2)}, u32[]{:S(2)}) collective-permute-start(f32[1]{0:T(128)} %bitcast.9), channel_id=1, source_target_pairs={{0,1},{1,0},{2,3},{3,2},{4,5},{5,4},{6,7},{7,6},{8,9},{9,8},{10,11... | collective-permute-start | bytes 20 | tf_op jit(solution)/shard_map/ppermute | solution.py:137

commit v4 on v3

--- a/solution.py
+++ b/solution.py
@@ -89,6 +89,58 @@
     )(lens, queries, cache_k, cache_v, keys_new, values_new)
 
 
+HIDDEN_CHUNK = 256
+
+
+def ffn_kernel(x_ref, wu_ref, wd_ref, out_ref, acc_ref):
+    step = pl.program_id(0)
+
+    @pl.when(step == 0)
+    def _():
+        acc_ref[...] = jnp.zeros_like(acc_ref)
+
+    hidden = jnp.dot(x_ref[...], wu_ref[...], preferred_element_type=jnp.float32)
+    active = (hidden * (0.5 + 0.5 * lax.erf(hidden * (0.5**0.5)))).astype(jnp.bfloat16)
+    acc_ref[...] += jnp.dot(active, wd_ref[...], preferred_element_type=jnp.float32)
+
+    @pl.when(step == pl.num_programs(0) - 1)
+    def _():
+        out_ref[...] = acc_ref[...].astype(out_ref.dtype)
+
+
+def ffn(middle, w_up, w_down):
+    rows, width = middle.shape
+    hidden = w_up.shape[1]
+    return pl.pallas_call(
+        ffn_kernel,
+        out_shape=jax.ShapeDtypeStruct((rows, width), jnp.bfloat16),
+        grid=(hidden // HIDDEN_CHUNK,),
+        in_specs=[
+            pl.BlockSpec((rows, width), lambda c: (0, 0)),
+            pl.BlockSpec((width, HIDDEN_CHUNK), lambda c: (0, c)),
+            pl.BlockSpec((HIDDEN_CHUNK, width), lambda c: (c, 0)),
+        ],
+        out_specs=pl.BlockSpec((rows, width), lambda c: (0, 0)),
+        scratch_shapes=[pltpu.VMEM((rows, width), jnp.float32)],
+        cost_estimate=pl.CostEstimate(
+            flops=4 * rows * width * hidden,
+            transcendentals=rows * hidden,
+            bytes_accessed=2 * (2 * rows * width + 2 * width * hidden),
+        ),
+    )(middle, w_up, w_down)
+
+
+def finish_rows(attn_mixed, tokens, w_out, w_up, w_down, ln_gains, ln_biases):
+    attn_sum = pair_sum(jnp.dot(attn_mixed, w_out, preferred_element_type=jnp.float32))
+    middle = normalize(tokens.astype(jnp.float32) + attn_sum, ln_gains[0], ln_biases[0]).astype(
+        jnp.bfloat16
+    )
+    ffn_sum = pair_sum(ffn(middle, w_up, w_down))
+    return normalize(middle.astype(jnp.float32) + ffn_sum, ln_gains[1], ln_biases[1]).astype(
+        jnp.bfloat16
+    )
+
+
 def shards(
     tokens,
     group_len,
@@ -115,16 +167,13 @@
     values_new = jnp.dot(tokens, w_value, preferred_element_type=jnp.float32).astype(jnp.bfloat16)
     lens = jnp.stack([my_cache, my_valid]).astype(jnp.int32)
     attn_mixed = attention(lens, queries, cache_keys[0], cache_values[0], keys_new, values_new)
-    attn_sum = pair_sum(jnp.dot(attn_mixed, w_out, preferred_element_type=jnp.float32))
-    middle = normalize(tokens.astype(jnp.float32) + attn_sum, ln_gains[0], ln_biases[0]).astype(
-        jnp.bfloat16
-    )
-    active = jax.nn.gelu(
-        jnp.dot(middle, w_up, preferred_element_type=jnp.float32), approximate=False
-    ).astype(jnp.bfloat16)
-    ffn_sum = pair_sum(jnp.dot(active, w_down, preferred_element_type=jnp.float32))
-    layer_out = normalize(middle.astype(jnp.float32) + ffn_sum, ln_gains[1], ln_biases[1]).astype(
-        jnp.bfloat16
+    half = block_rows // 2
+    layer_out = jnp.concatenate(
+        [
+            finish_rows(attn_mixed[:half], tokens[:half], w_out, w_up, w_down, ln_gains, ln_biases),
+            finish_rows(attn_mixed[half:], tokens[half:], w_out, w_up, w_down, ln_gains, ln_biases),
+        ],
+        axis=0,
     )
     last_row = lax.dynamic_slice_in_dim(layer_out, my_valid - 1, 1, 0)
     reqs = cache_len.shape[0]
@@ -133,8 +182,8 @@
     )
     logits = jnp.einsum("rd,vd->rv", all_rows, embed, preferred_element_type=jnp.float32)
     slice_best = jnp.max(logits, axis=1)
-    mine = jnp.max(lax.all_to_all(slice_best[:, None], "req", 0, 0, tiled=True), axis=0)
-    best_logit = jnp.maximum(mine, lax.ppermute(mine, "tp", [(0, 1), (1, 0)]))
+    spread = jnp.repeat(slice_best, 2)[:, None]
+    best_logit = jnp.max(lax.all_to_all(spread, ("req", "tp"), 0, 0, tiled=True), axis=0)
     return (layer_out, best_logit, slice_best[:, None])
 
 

time: 109 us -> 106 us (0.972)
  blocking collectives: 44.3 us -> 27.7 us
  Pallas kernels: 15.5 us -> 27.6 us
  waiting for transfers between devices: 5.83 us -> 14.9 us
  matrix products: 17.4 us -> 9.19 us
  starting transfers between devices: 6.43 us -> 10.8 us
  between operations: 4.06 us -> 1.64 us
  other arithmetic: 11.7 us -> 10 us
    all_to_all x1 -> x0, blocking collectives: 16.6 us -> none  [shards(): lax.all_to_all(slice_best[:, None], 'req', 0, 0, tiled=True)]
    pallas_call x0 -> x2, Pallas kernels: none -> 12.2 us  [ffn(): pl.pallas_call(ffn_kernel, out_shape=jax.ShapeDtypeStruct((rows, width),...]
    all_to_all x0 -> x1, waiting for transfers between devices: none -> 12 us  [shards(): lax.all_to_all(spread, ('req', 'tp'), 0, 0, tiled=True)]
    dot_general x2, matrix products: 10.9 us -> 2.79 us  [finish_rows(): jnp.dot(attn_mixed, w_out, preferred_element_type=jnp.float32)]
    all_to_all x0 -> x1, starting transfers between devices: none -> 6.93 us  [shards(): lax.all_to_all(spread, ('req', 'tp'), 0, 0, tiled=True)]
    ppermute x1 -> x0, starting transfers between devices: 2.59 us -> none  [shards(): best_logit = jnp.maximum(mine, lax.ppermute(mine, 'tp', [(0, 1), (1, 0)]))]
    ppermute x2 -> x4, waiting for transfers between devices: 4.87 us -> 2.92 us  [pair_sum(): other = lax.ppermute(own, 'tp', [(0, 1), (1, 0)])]
    reduce_sum x2 -> x3, other arithmetic: 2.5 us -> 1.05 us  [normalize(): center = rows - jnp.mean(rows, axis=-1, keepdims=True)]
  transfers between devices with their start and end apart: 3 -> 5, of which waited for: 3 -> 3; matrix products, arithmetic and copies ran while one was open for 0% -> 3% of each run, Pallas kernels for 0% -> 6%
where the time goes in v4:
time: 106 us
  blocking collectives  27.7 us (26%)
  Pallas kernels  27.6 us (26%)
  waiting for transfers between devices  14.9 us (14%)
  starting transfers between devices  10.8 us (10%)
  other arithmetic  10 us (9%)
  matrix products  9.19 us (9%)
  local copies, waits for them, and re-layouts  3.51 us (3%)
  between operations  1.64 us (2%)
    all_to_all x1, blocking collectives, shards(): lax.all_to_all(jnp.broadcast_to(last_row, (reqs, last_row.shape[1])), 're...  27.7 us
    pallas_call x1, Pallas kernels, attention(): pl.pallas_call(attention_kernel, out_shape=jax.ShapeDtypeStruct((rows, wi...  15.5 us
    pallas_call x2, Pallas kernels, ffn(): pl.pallas_call(ffn_kernel, out_shape=jax.ShapeDtypeStruct((rows, width),...  12.2 us
    all_to_all x1, waiting for transfers between devices, shards(): lax.all_to_all(spread, ('req', 'tp'), 0, 0, tiled=True)  12 us
    all_to_all x1, starting transfers between devices, shards(): lax.all_to_all(spread, ('req', 'tp'), 0, 0, tiled=True)  6.93 us
    ppermute x4, starting transfers between devices, pair_sum(): other = lax.ppermute(own, 'tp', [(0, 1), (1, 0)])  3.9 us
    dot_general x1, matrix products, shards(): jnp.dot(tokens, w_query, preferred_element_type=jnp.float32)  3.1 us
    ppermute x4, waiting for transfers between devices, pair_sum(): other = lax.ppermute(own, 'tp', [(0, 1), (1, 0)])  2.92 us
  transfers between devices with their start and end apart: 5, of which 3 were waited for; matrix products, arithmetic and copies ran while one was open for 3% of the time, Pallas kernels for 6%

profile of v4, /device:TPU:1, one launch (start us, length us, event | category | flops | bytes accessed | tf_op | source)
XLA Modules:
  0.0 105.5 jit_solution(3680319581419180568)
XLA Ops:
  0.6 0.0 copy-start
  0.6 0.0 copy-start.3
  0.7 0.0 copy-start.11
  1.5 3.1 %convolution_convert_fusion.4.q_ref = bf16[512,512]{1,0:T(8,128)(2,1)} fusion(bf16[512,1024]{1,0:T(8,128)(2,1)} %param.14, bf16[1024,512]{1,0:T(8,128)(2,1)} %param.19), kind=kOutput, calls=%fused_computation.4 | convolution fusion | flops 537133056 | bytes 2621440 | tf_op jit(solution)/shard_map/dot_general | solution.py:165
  4.6 0.0 copy-done.3
  4.6 0.0 copy-done.11
  4.6 0.0 copy-start.12
  4.6 1.5 %convolution_convert_fusion.3.kn_ref = bf16[512,512]{1,0:T(8,128)(2,1)} fusion(bf16[512,1024]{1,0:T(8,128)(2,1)S(1)} %copy-done.3, bf16[1024,512]{1,0:T(8,128)(2,1)S(1)} %copy-done.11), kind=kOutput, calls=%fused_computation.3 | convolution fusion | flops 537133056 | bytes 2621440 | tf_op jit(solution)/shard_map/dot_general | solution.py:166
  6.1 0.0 copy-done.12
  6.1 0.0 copy-start.14
  6.1 1.5 %convolution_convert_fusion.2.vn_ref = bf16[512,512]{1,0:T(8,128)(2,1)} fusion(bf16[512,1024]{1,0:T(8,128)(2,1)S(1)} %copy-done.3, bf16[1024,512]{1,0:T(8,128)(2,1)S(1)} %copy-done.12), kind=kOutput, calls=%fused_computation.2 | convolution fusion | flops 537133056 | bytes 2621440 | tf_op jit(solution)/shard_map/dot_general | solution.py:167
  7.6 0.0 copy-done.14
  7.6 0.6 dynamic_slice.9
  8.2 1.2 %pad_add_fusion.lens_ref = s32[2]{0:T(128)} fusion(s32[1]{0:T(128)S(6)} %copy.23, s32[1]{0:T(128)} %dynamic_slice.9), kind=kLoop, calls=%fused_computation.35 | loop fusion | flops 2 | bytes 16 | tf_op jit(solution)/shard_map/stack | solution.py:168
  9.4 15.5 %shard_map.157 = bf16[512,512]{1,0:T(8,128)(2,1)} custom-call(s32[2]{0:T(128)} %pad_add_fusion.lens_ref, bf16[512,512]{1,0:T(8,128)(2,1)} %convolution_convert_fusion.4.q_ref, bf16[1024,512]{1,0:T(8,128)(2,1)} %bitcast.27, bf16[1024,512]{1,0:T(8,128)(2,1)} %bitcast.28, bf16[512,512]{1,0:T(8,128)(2,1)} %convolution_convert_fusion.3.kn_ref, ...), custom_call_target="tpu_custom_call" | custom-call | flops 3221225472 | bytes 4194304 | tf_op jit(solution)/shard_map/pallas_call | solution.py:69
  24.9 0.0 copy-done
  24.9 0.0 copy-start.8
  24.9 0.0 copy-start.9
  24.9 1.4 %convolution_convert_fusion.1 = bf16[256,1024]{1,0:T(8,128)(2,1)S(1)} fusion(bf16[512,1024]{1,0:T(8,128)(2,1)S(1)} %copy-done, bf16[512,512]{1,0:T(8,128)(2,1)} %shard_map.157), kind=kOutput, calls=%fused_computation.1 | convolution fusion | flops 268697600 | bytes 1835008 | tf_op jit(solution)/shard_map/dot_general | solution.py:134
  26.3 3.3 %collective-permute-start = (bf16[256,1024]{1,0:T(8,128)(2,1)S(1)}, bf16[256,1024]{1,0:T(8,128)(2,1)S(1)}, u32[]{:S(2)}, u32[]{:S(2)}) collective-permute-start(bf16[256,1024]{1,0:T(8,128)(2,1)S(1)} %convolution_convert_fusion.1), channel_id=1, source_target_pairs={{0,1},{1,0},{2,3},{3,2},{4,5},{5,4},{6,7},{7,6},{8,9},{9,8},{10,11... | collective-permute-start | bytes 1572872 | tf_op jit(solution)/shard_map/ppermute | solution.py:19
  29.6 1.4 %convolution_convert_fusion = bf16[256,1024]{1,0:T(8,128)(2,1)S(1)} fusion(bf16[512,1024]{1,0:T(8,128)(2,1)S(1)} %copy-done, bf16[512,512]{1,0:T(8,128)(2,1)} %shard_map.157), kind=kOutput, calls=%fused_computation | convolution fusion | flops 268697600 | bytes 1835008 | tf_op jit(solution)/shard_map/dot_general | solution.py:134
  31.0 0.1 collective-permute-start.2
  31.1 0.0 copy-done.8
  31.1 0.0 copy-done.9
  31.2 0.0 collective-permute-done
  31.2 1.8 %collective-permute-done.2 = bf16[256,1024]{1,0:T(8,128)(2,1)S(1)} collective-permute-done((bf16[256,1024]{1,0:T(8,128)(2,1)S(1)}, bf16[256,1024]{1,0:T(8,128)(2,1)S(1)}, u32[]{:S(2)}, u32[]{:S(2)}) %collective-permute-start.2) | collective-permute-done | bytes 524320 | tf_op jit(solution)/shard_map/ppermute | solution.py:19
  33.0 0.5 fusion.6
  33.5 0.6 multiply_reduce_fusion.3
  34.1 1.6 %add_convert_fusion.3 = (bf16[256,1024]{1,0:T(8,128)(2,1)}, bf16[256,1024]{1,0:T(8,128)(2,1)}) fusion(f32[1024]{0:T(1024)S(1)} %bitcast.24, f32[1024]{0:T(1024)S(1)} %bitcast.25, f32[256]{0:T(256)S(1)} %add_rsqrt_fusion.3, f32[256]{0:T(256)S(1)} %get-tuple-element.16, bf16[256,1024]{1,0:T(8,128)(2,1)S(1)} %collective-permute-done, ...), kind=kLoop, calls=%fused_computation.18 | loop fusion | flops 5242880 | bytes 4206592 | tf_op jit(solution)/shard_map/convert_element_type | solution.py:135
  35.8 6.0 %shard_map.158 = bf16[256,1024]{1,0:T(8,128)(2,1)} custom-call(bf16[256,1024]{1,0:T(8,128)(2,1)} %get-tuple-element.7.x_ref, bf16[1024,1024]{1,0:T(8,128)(2,1)} %wu_ref.3, bf16[1024,1024]{1,0:T(8,128)(2,1)} %wd_ref.3), custom_call_target="tpu_custom_call" | custom-call | flops 1073741824 | bytes 5242880 | tf_op jit(solution)/shard_map/pallas_call | solution.py:114
  41.8 0.1 collective-permute-start.1
  41.9 0.0 copy-start.1
  41.9 6.1 %shard_map.159 = bf16[256,1024]{1,0:T(8,128)(2,1)} custom-call(bf16[256,1024]{1,0:T(8,128)(2,1)} %get-tuple-element.8.x_ref, bf16[1024,1024]{1,0:T(8,128)(2,1)} %wu_ref.3, bf16[1024,1024]{1,0:T(8,128)(2,1)} %wd_ref.3), custom_call_target="tpu_custom_call" | custom-call | flops 1073741824 | bytes 5242880 | tf_op jit(solution)/shard_map/pallas_call | solution.py:114
  48.1 0.4 collective-permute-start.3
  48.4 0.0 collective-permute-done.1
  48.4 0.0 copy-done.1
  48.4 0.0 copy-done.4
  48.4 0.3 fusion
  48.7 0.4 multiply_reduce_fusion.2
  49.1 1.1 %collective-permute-done.3 = bf16[256,1024]{1,0:T(8,128)(2,1)S(1)} collective-permute-done((bf16[256,1024]{1,0:T(8,128)(2,1)}, bf16[256,1024]{1,0:T(8,128)(2,1)S(1)}, u32[]{:S(2)}, u32[]{:S(2)}) %collective-permute-start.3) | collective-permute-done | bytes 524320 | tf_op jit(solution)/shard_map/ppermute | solution.py:19
  50.2 0.0 copy-done.2
  50.2 0.0 copy-done.5
  50.2 0.3 fusion.1
  50.5 0.4 multiply_reduce_fusion
  50.8 0.7 add_convert_fusion.2
  51.5 0.0 copy-start.6
  51.5 0.8 copy-done.6
  52.4 0.3 broadcast_in_dim.6
  52.6 0.5 broadcast.93
  53.2 2.1 %reduce.4 = bf16[128,1024]{1,0:T(8,128)(2,1)S(1)} reduce(bf16[128,1,1024]{2,1,0:T(2,128)(2,1)S(1)} %broadcast_in_dim.6, bf16[]{:T(256)} %broadcast.93), dimensions={1}, to_apply=%broadcast_in_dim.6.reduce_sub_computation | reduce | bytes 524290 | tf_op jit(solution)/shard_map/broadcast_in_dim | solution.py:181
  55.3 0.2 reshape.69
  55.5 27.7 %all_to_all.19 = bf16[128,2,512]{2,1,0:T(2,128)(2,1)S(1)} all-to-all(bf16[128,2,512]{2,1,0:T(2,128)(2,1)S(1)} %reshape.69), channel_id=1, replica_groups=mesh['req'=128,'tp'=2] {'req'}, dimensions={0} | all-to-all | bytes 524288 | tf_op jit(solution)/shard_map/all_to_all | solution.py:180
  83.2 0.2 reshape.70
  83.5 0.0 copy-done.13
  83.5 0.3 convolution_reduce_fusion
  83.8 0.0 copy-start.10
  83.8 0.1 broadcast_in_dim.7
  83.8 0.8 all_to_all.16
  84.6 6.9 %all-to-all-start.1 = ((f32[256,1,1]{2,1,0:T(1,128)}), f32[256,1,1]{2,1,0:T(1,128)S(1)}, u32[]{:S(2)}, u32[]{:S(2)}) async-start(f32[256,1,1]{2,1,0:T(1,128)} %all_to_all.16), calls=%async_computation.1 | async-start | bytes 262144 | tf_op jit(solution)/shard_map/all_to_all | solution.py:186
  91.6 0.0 copy-done.7
  91.6 1.0 pad_maximum_fusion
  92.6 12.0 %all-to-all-done.1 = f32[256,1,1]{2,1,0:T(1,128)S(1)} async-done(((f32[256,1,1]{2,1,0:T(1,128)}), f32[256,1,1]{2,1,0:T(1,128)S(1)}, u32[]{:S(2)}, u32[]{:S(2)}) %all-to-all-start.1) | async-done | bytes 1056 | tf_op jit(solution)/shard_map/all_to_all | solution.py:186
  104.7 0.9 reduce_max.21
  105.5 0.0 copy-done.10
  (15 shorter events, 0.1 us)
Async XLA Ops:
  0.6 24.3 %copy-start = (bf16[512,1024]{1,0:T(8,128)(2,1)S(1)}, bf16[512,1024]{1,0:T(8,128)(2,1)}, u32[]{:S(2)}) copy-start(bf16[512,1024]{1,0:T(8,128)(2,1)} %param.22) | copy-start | bytes 3145732
  0.6 3.9 %copy-start.3 = (bf16[512,1024]{1,0:T(8,128)(2,1)S(1)}, bf16[512,1024]{1,0:T(8,128)(2,1)}, u32[]{:S(2)}) copy-start(bf16[512,1024]{1,0:T(8,128)(2,1)} %param.14) | copy-start | bytes 3145732
  0.7 3.9 %copy-start.11 = (bf16[1024,512]{1,0:T(8,128)(2,1)S(1)}, bf16[1024,512]{1,0:T(8,128)(2,1)}, u32[]{:S(2)}) copy-start(bf16[1024,512]{1,0:T(8,128)(2,1)} %param.20) | copy-start | bytes 3145732
  4.6 1.5 %copy-start.12 = (bf16[1024,512]{1,0:T(8,128)(2,1)S(1)}, bf16[1024,512]{1,0:T(8,128)(2,1)}, u32[]{:S(2)}) copy-start(bf16[1024,512]{1,0:T(8,128)(2,1)} %param.21) | copy-start | bytes 3145732
  6.1 1.5 %copy-start.14 = (s32[128]{0:T(128)S(1)}, s32[128]{0:T(128)}, u32[]{:S(2)}) copy-start(s32[128]{0:T(128)} %param.16) | copy-start | bytes 1540
  24.9 6.2 %copy-start.8 = (f32[2,1024]{1,0:T(2,128)S(1)}, f32[2,1024]{1,0:T(2,128)}, u32[]{:S(2)}) copy-start(f32[2,1024]{1,0:T(2,128)} %param.26) | copy-start | bytes 24580
  24.9 6.2 %copy-start.9 = (f32[2,1024]{1,0:T(2,128)S(1)}, f32[2,1024]{1,0:T(2,128)}, u32[]{:S(2)}) copy-start(f32[2,1024]{1,0:T(2,128)} %param.25) | copy-start | bytes 24580
  26.3 4.8 %collective-permute-start = (bf16[256,1024]{1,0:T(8,128)(2,1)S(1)}, bf16[256,1024]{1,0:T(8,128)(2,1)S(1)}, u32[]{:S(2)}, u32[]{:S(2)}) collective-permute-start(bf16[256,1024]{1,0:T(8,128)(2,1)S(1)} %convolution_convert_fusion.1), channel_id=1, source_target_pairs={{0,1},{1,0},{2,3},{3,2},{4,5},{5,4},{6,7},{7,6},{8,9},{9,8},{10,11... | collective-permute-start | bytes 1572872 | tf_op jit(solution)/shard_map/ppermute | solution.py:19
  31.0 2.0 %collective-permute-start.2 = (bf16[256,1024]{1,0:T(8,128)(2,1)S(1)}, bf16[256,1024]{1,0:T(8,128)(2,1)S(1)}, u32[]{:S(2)}, u32[]{:S(2)}) collective-permute-start(bf16[256,1024]{1,0:T(8,128)(2,1)S(1)} %convolution_convert_fusion), channel_id=1, source_target_pairs={{0,1},{1,0},{2,3},{3,2},{4,5},{5,4},{6,7},{7,6},{8,9},{9,8},{10,11... | collective-permute-start | bytes 1572872 | tf_op jit(solution)/shard_map/ppermute | solution.py:19
  41.8 6.6 %collective-permute-start.1 = (bf16[256,1024]{1,0:T(8,128)(2,1)}, bf16[256,1024]{1,0:T(8,128)(2,1)S(1)}, u32[]{:S(2)}, u32[]{:S(2)}) collective-permute-start(bf16[256,1024]{1,0:T(8,128)(2,1)} %shard_map.158), channel_id=1, source_target_pairs={{0,1},{1,0},{2,3},{3,2},{4,5},{5,4},{6,7},{7,6},{8,9},{9,8},{10,11... | collective-permute-start | bytes 1572872 | tf_op jit(solution)/shard_map/ppermute | solution.py:19
  41.9 6.5 %copy-start.1 = (bf16[256,1024]{1,0:T(8,128)(2,1)S(1)}, bf16[256,1024]{1,0:T(8,128)(2,1)}, u32[]{:S(2)}) copy-start(bf16[256,1024]{1,0:T(8,128)(2,1)} %get-tuple-element.7.x_ref) | copy-start | bytes 1572868
  41.9 6.5 %copy-start.4 = (bf16[256,1024]{1,0:T(8,128)(2,1)S(1)}, bf16[256,1024]{1,0:T(8,128)(2,1)}, u32[]{:S(2)}) copy-start(bf16[256,1024]{1,0:T(8,128)(2,1)} %shard_map.158) | copy-start | bytes 1572868
  48.1 2.1 %copy-start.2 = (bf16[256,1024]{1,0:T(8,128)(2,1)S(1)}, bf16[256,1024]{1,0:T(8,128)(2,1)}, u32[]{:S(2)}) copy-start(bf16[256,1024]{1,0:T(8,128)(2,1)} %get-tuple-element.8.x_ref) | copy-start | bytes 1572868
  48.1 2.1 %copy-start.5 = (bf16[256,1024]{1,0:T(8,128)(2,1)S(1)}, bf16[256,1024]{1,0:T(8,128)(2,1)}, u32[]{:S(2)}) copy-start(bf16[256,1024]{1,0:T(8,128)(2,1)} %shard_map.159) | copy-start | bytes 1572868
  48.1 2.1 %collective-permute-start.3 = (bf16[256,1024]{1,0:T(8,128)(2,1)}, bf16[256,1024]{1,0:T(8,128)(2,1)S(1)}, u32[]{:S(2)}, u32[]{:S(2)}) collective-permute-start(bf16[256,1024]{1,0:T(8,128)(2,1)} %shard_map.159), channel_id=1, source_target_pairs={{0,1},{1,0},{2,3},{3,2},{4,5},{5,4},{6,7},{7,6},{8,9},{9,8},{10,11... | collective-permute-start | bytes 1572872 | tf_op jit(solution)/shard_map/ppermute | solution.py:19
  51.5 0.8 copy-start.6
  52.3 31.1 %copy-start.13 = (bf16[192,1024]{1,0:T(8,128)(2,1)S(1)}, bf16[192,1024]{1,0:T(8,128)(2,1)}, u32[]{:S(2)}) copy-start(bf16[192,1024]{1,0:T(8,128)(2,1)} %param.27) | copy-start | bytes 1179652
  52.4 39.2 %copy-start.7 = (bf16[256,1024]{1,0:T(8,128)(2,1)S(1)}, bf16[256,1024]{1,0:T(8,128)(2,1)}, u32[]{:S(2)}) copy-start(bf16[256,1024]{1,0:T(8,128)(2,1)} %copy-done.6) | copy-start | bytes 1572868
  83.8 21.8 %copy-start.10 = (f32[128]{0:T(128)}, f32[128]{0:T(128)S(1)}, u32[]{:S(2)}) copy-start(f32[128]{0:T(128)S(1)} %convolution_reduce_fusion) | copy-start | bytes 1540
  84.6 20.0 %all-to-all-start.1 = ((f32[256,1,1]{2,1,0:T(1,128)}), f32[256,1,1]{2,1,0:T(1,128)S(1)}, u32[]{:S(2)}, u32[]{:S(2)}) async-start(f32[256,1,1]{2,1,0:T(1,128)} %all_to_all.16), calls=%async_computation.1 | async-start | bytes 262144 | tf_op jit(solution)/shard_map/all_to_all | solution.py:186

commit v5 on v3

--- a/solution.py
+++ b/solution.py
@@ -89,6 +89,20 @@
     )(lens, queries, cache_k, cache_v, keys_new, values_new)
 
 
+def finish_rows(attn_mixed, tokens, w_out, w_up, w_down, ln_gains, ln_biases):
+    attn_sum = pair_sum(jnp.dot(attn_mixed, w_out, preferred_element_type=jnp.float32))
+    middle = normalize(tokens.astype(jnp.float32) + attn_sum, ln_gains[0], ln_biases[0]).astype(
+        jnp.bfloat16
+    )
+    active = jax.nn.gelu(
+        jnp.dot(middle, w_up, preferred_element_type=jnp.float32), approximate=False
+    ).astype(jnp.bfloat16)
+    ffn_sum = pair_sum(jnp.dot(active, w_down, preferred_element_type=jnp.float32))
+    return normalize(middle.astype(jnp.float32) + ffn_sum, ln_gains[1], ln_biases[1]).astype(
+        jnp.bfloat16
+    )
+
+
 def shards(
     tokens,
     group_len,
@@ -115,26 +129,25 @@
     values_new = jnp.dot(tokens, w_value, preferred_element_type=jnp.float32).astype(jnp.bfloat16)
     lens = jnp.stack([my_cache, my_valid]).astype(jnp.int32)
     attn_mixed = attention(lens, queries, cache_keys[0], cache_values[0], keys_new, values_new)
-    attn_sum = pair_sum(jnp.dot(attn_mixed, w_out, preferred_element_type=jnp.float32))
-    middle = normalize(tokens.astype(jnp.float32) + attn_sum, ln_gains[0], ln_biases[0]).astype(
-        jnp.bfloat16
-    )
-    active = jax.nn.gelu(
-        jnp.dot(middle, w_up, preferred_element_type=jnp.float32), approximate=False
-    ).astype(jnp.bfloat16)
-    ffn_sum = pair_sum(jnp.dot(active, w_down, preferred_element_type=jnp.float32))
-    layer_out = normalize(middle.astype(jnp.float32) + ffn_sum, ln_gains[1], ln_biases[1]).astype(
-        jnp.bfloat16
+    half = block_rows // 2
+    layer_out = jnp.concatenate(
+        [
+            finish_rows(attn_mixed[:half], tokens[:half], w_out, w_up, w_down, ln_gains, ln_biases),
+            finish_rows(attn_mixed[half:], tokens[half:], w_out, w_up, w_down, ln_gains, ln_biases),
+        ],
+        axis=0,
     )
     last_row = lax.dynamic_slice_in_dim(layer_out, my_valid - 1, 1, 0)
     reqs = cache_len.shape[0]
+    width = last_row.shape[1] // 2
+    my_half = lax.dynamic_slice_in_dim(last_row, lax.axis_index("tp") * width, width, 1)
     all_rows = lax.all_to_all(
-        jnp.broadcast_to(last_row, (reqs, last_row.shape[1])), "req", 0, 0, tiled=True
-    )
+        jnp.broadcast_to(my_half, (2 * reqs, width)), ("req", "tp"), 0, 0, tiled=True
+    ).reshape(reqs, 2 * width)
     logits = jnp.einsum("rd,vd->rv", all_rows, embed, preferred_element_type=jnp.float32)
     slice_best = jnp.max(logits, axis=1)
-    mine = jnp.max(lax.all_to_all(slice_best[:, None], "req", 0, 0, tiled=True), axis=0)
-    best_logit = jnp.maximum(mine, lax.ppermute(mine, "tp", [(0, 1), (1, 0)]))
+    spread = jnp.repeat(slice_best, 2)[:, None]
+    best_logit = jnp.max(lax.all_to_all(spread, ("req", "tp"), 0, 0, tiled=True), axis=0)
     return (layer_out, best_logit, slice_best[:, None])
 
 

time: 109 us -> 122 us (1.12)
  blocking collectives: 44.3 us -> 28.6 us
  other arithmetic: 11.7 us -> 21.5 us
  waiting for transfers between devices: 5.83 us -> 14.2 us
  matrix products: 17.4 us -> 24.6 us
  starting transfers between devices: 6.43 us -> 9.21 us
  between operations: 4.06 us -> 1.63 us
  local copies, waits for them, and re-layouts: 3.52 us -> 5.9 us
    all_to_all x2 -> x1, blocking collectives: 44.3 us -> 28.6 us  [shards(): lax.all_to_all(jnp.broadcast_to(my_half, (2 * reqs, width)), ('req', 'tp'...]
    all_to_all x0 -> x1, waiting for transfers between devices: none -> 12 us  [shards(): lax.all_to_all(spread, ('req', 'tp'), 0, 0, tiled=True)]
    dot_general x2 -> x4, matrix products: 10.9 us -> 17.1 us  [the longest x2 12 us: finish_rows(): jnp.dot(active, w_down, preferred_element_type=jnp.float32)]
    all_to_all x0 -> x1, starting transfers between devices: none -> 5.49 us  [shards(): lax.all_to_all(spread, ('req', 'tp'), 0, 0, tiled=True)]
    all_to_all x0 -> x1, other arithmetic: none -> 3.2 us  [shards(): lax.all_to_all(jnp.broadcast_to(my_half, (2 * reqs, width)), ('req', 'tp'...]
    ppermute x2 -> x4, waiting for transfers between devices: 4.87 us -> 2.21 us  [pair_sum(): other = lax.ppermute(own, 'tp', [(0, 1), (1, 0)])]
    ppermute x1 -> x0, starting transfers between devices: 2.59 us -> none  [shards(): best_logit = jnp.maximum(mine, lax.ppermute(mine, 'tp', [(0, 1), (1, 0)]))]
    convert_element_type x2, other arithmetic: 2.58 us -> 5.01 us  [the longest x1 3.14 us: finish_rows(): normalize(tokens.astype(jnp.float32) + attn_sum, ln_gains[0], ln_biases[0])]
  transfers between devices with their start and end apart: 3 -> 5, of which waited for: 3 -> 2; matrix products, arithmetic and copies ran while one was open for 0% -> 10% of each run, Pallas kernels for 0% -> 0%
where the time goes in v5:
time: 122 us; the launch traced here: 121 us
  blocking collectives  28.6 us (23%)
  matrix products  24.6 us (20%)
  other arithmetic  21.5 us (18%)
  Pallas kernels  15.5 us (13%)
  waiting for transfers between devices  14.2 us (12%)
  starting transfers between devices  9.21 us (8%)
  local copies, waits for them, and re-layouts  5.9 us (5%)
  between operations  1.63 us (1%)
    all_to_all x1, blocking collectives, shards(): lax.all_to_all(jnp.broadcast_to(my_half, (2 * reqs, width)), ('req', 'tp'...  28.6 us
    pallas_call x1, Pallas kernels, attention(): pl.pallas_call(attention_kernel, out_shape=jax.ShapeDtypeStruct((rows, wi...  15.5 us
    all_to_all x1, waiting for transfers between devices, shards(): lax.all_to_all(spread, ('req', 'tp'), 0, 0, tiled=True)  12 us
    dot_general x2, matrix products, finish_rows(): jnp.dot(active, w_down, preferred_element_type=jnp.float32)  12 us
    all_to_all x1, starting transfers between devices, shards(): lax.all_to_all(spread, ('req', 'tp'), 0, 0, tiled=True)  5.49 us
    dot_general x2, matrix products, finish_rows(): jnp.dot(attn_mixed, w_out, preferred_element_type=jnp.float32)  5.14 us
    reduce_sum x3, other arithmetic, normalize(): spread = jnp.mean(center * center, axis=-1, keepdims=True)  4.04 us
    reduce_sum x3, other arithmetic, normalize(): center = rows - jnp.mean(rows, axis=-1, keepdims=True)  3.76 us
  transfers between devices with their start and end apart: 5, of which 2 were waited for; matrix products, arithmetic and copies ran while one was open for 10% of the time, Pallas kernels for 0%

profile of v5, /device:TPU:1, one launch (start us, length us, event | category | flops | bytes accessed | tf_op | source)
XLA Modules:
  0.0 121.0 jit_solution(16733030732206363271)
XLA Ops:
  0.6 0.0 copy-start
  0.6 0.0 copy-start.1
  1.5 0.0 copy-start.12
  1.5 3.2 %convolution_convert_fusion.6.q_ref = bf16[512,512]{1,0:T(8,128)(2,1)} fusion(bf16[512,1024]{1,0:T(8,128)(2,1)} %param.14, bf16[1024,512]{1,0:T(8,128)(2,1)} %param.19), kind=kOutput, calls=%fused_computation.8 | convolution fusion | flops 537133056 | bytes 2621440 | tf_op jit(solution)/shard_map/dot_general | solution.py:127
  4.6 0.0 copy-done.1
  4.6 0.0 copy-done.12
  4.6 1.5 %convolution_convert_fusion.5.kn_ref = bf16[512,512]{1,0:T(8,128)(2,1)} fusion(bf16[512,1024]{1,0:T(8,128)(2,1)S(1)} %copy-done.1, bf16[1024,512]{1,0:T(8,128)(2,1)S(1)} %copy-done.12), kind=kOutput, calls=%fused_computation.7 | convolution fusion | flops 537133056 | bytes 2621440 | tf_op jit(solution)/shard_map/dot_general | solution.py:128
  6.1 0.0 copy-done.13
  6.1 1.5 %convolution_convert_fusion.4.vn_ref = bf16[512,512]{1,0:T(8,128)(2,1)} fusion(bf16[512,1024]{1,0:T(8,128)(2,1)S(1)} %copy-done.1, bf16[1024,512]{1,0:T(8,128)(2,1)S(1)} %copy-done.13), kind=kOutput, calls=%fused_computation.6 | convolution fusion | flops 537133056 | bytes 2621440 | tf_op jit(solution)/shard_map/dot_general | solution.py:129
  7.7 0.0 copy-done.14
  7.7 0.6 dynamic_slice.10
  8.3 1.2 %pad_add_fusion.lens_ref = s32[2]{0:T(128)} fusion(s32[1]{0:T(128)S(6)} %copy.18, s32[1]{0:T(128)} %dynamic_slice.10), kind=kLoop, calls=%fused_computation.133 | loop fusion | flops 2 | bytes 16 | tf_op jit(solution)/shard_map/stack | solution.py:130
  9.5 15.5 %shard_map.157 = bf16[512,512]{1,0:T(8,128)(2,1)} custom-call(s32[2]{0:T(128)} %pad_add_fusion.lens_ref, bf16[512,512]{1,0:T(8,128)(2,1)} %convolution_convert_fusion.6.q_ref, bf16[1024,512]{1,0:T(8,128)(2,1)} %bitcast.31, bf16[1024,512]{1,0:T(8,128)(2,1)} %bitcast.32, bf16[512,512]{1,0:T(8,128)(2,1)} %convolution_convert_fusion.5.kn_ref, ...), custom_call_target="tpu_custom_call" | custom-call | flops 3221225472 | bytes 4194304 | tf_op jit(solution)/shard_map/pallas_call | solution.py:69
  25.0 2.6 %convolution_convert_fusion.1 = bf16[256,1024]{1,0:T(8,128)(2,1)} fusion(bf16[512,1024]{1,0:T(8,128)(2,1)} %param.22, bf16[512,512]{1,0:T(8,128)(2,1)} %shard_map.157), kind=kOutput, calls=%fused_computation.3 | convolution fusion | flops 268697600 | bytes 1835008 | tf_op jit(solution)/shard_map/dot_general | solution.py:93
  27.5 3.2 %collective-permute-start = (bf16[256,1024]{1,0:T(8,128)(2,1)}, bf16[256,1024]{1,0:T(8,128)(2,1)}, u32[]{:S(2)}, u32[]{:S(2)}) collective-permute-start(bf16[256,1024]{1,0:T(8,128)(2,1)} %convolution_convert_fusion.1), channel_id=1, source_target_pairs={{0,1},{1,0},{2,3},{3,2},{4,5},{5,4},{6,7},{7,6},{8,9},{9,8},{10,11... | collective-permute-start | bytes 1572872 | tf_op jit(solution)/shard_map/ppermute | solution.py:19
  30.7 2.6 %convolution_convert_fusion = bf16[256,1024]{1,0:T(8,128)(2,1)} fusion(bf16[512,1024]{1,0:T(8,128)(2,1)} %param.22, bf16[512,512]{1,0:T(8,128)(2,1)} %shard_map.157), kind=kOutput, calls=%fused_computation.2 | convolution fusion | flops 268697600 | bytes 1835008 | tf_op jit(solution)/shard_map/dot_general | solution.py:93
  33.3 0.0 collective-permute-start.2
  33.3 0.0 copy-done.9
  33.3 0.0 copy-done.10
  33.3 0.0 collective-permute-done
  33.3 2.2 %collective-permute-done.2 = bf16[256,1024]{1,0:T(8,128)(2,1)} collective-permute-done((bf16[256,1024]{1,0:T(8,128)(2,1)}, bf16[256,1024]{1,0:T(8,128)(2,1)}, u32[]{:S(2)}, u32[]{:S(2)}) %collective-permute-start.2) | collective-permute-done | bytes 524320 | tf_op jit(solution)/shard_map/ppermute | solution.py:19
  35.5 2.0 %fusion.86 = (f32[256]{0:T(256)S(1)}, f32[256]{0:T(256)S(1)}) fusion(bf16[256,1024]{1,0:T(8,128)(2,1)} %collective-permute-done, bf16[256,1024]{1,0:T(8,128)(2,1)} %convolution_convert_fusion.1, bf16[512,1024]{1,0:T(8,128)(2,1)S(1)} %copy-done.1, bf16[256,1024]{1,0:T(8,128)(2,1)} %collective-permute-done.2, bf16[256,1024]{1,0:T(8,128)(2,1)} %convolution_convert_fusion), kind=kLoop, calls=%fused_computation.125 | loop fusion | flops 3145216 | bytes 3147776 | tf_op jit(solution)/shard_map/reduce_sum | solution.py:12
  37.5 2.1 %multiply_reduce_fusion.3 = (f32[256]{0:T(256)S(1)}, f32[256]{0:T(256)S(1)}) fusion(f32[256]{0:T(256)S(1)} %get-tuple-element.16, bf16[256,1024]{1,0:T(8,128)(2,1)} %collective-permute-done, bf16[256,1024]{1,0:T(8,128)(2,1)} %convolution_convert_fusion.1, bf16[512,1024]{1,0:T(8,128)(2,1)S(1)} %copy-done.1, f32[256]{0:T(256)S(1)} %get-tuple-element.15, ...), kind=kLoop, calls=%fused_computation.55 | loop fusion | flops 4193792 | bytes 3149824 | tf_op jit(solution)/shard_map/reduce_sum | solution.py:13
  39.7 3.1 %add_convert_fusion.3 = (bf16[256,1024]{1,0:T(8,128)(2,1)}, bf16[256,1024]{1,0:T(8,128)(2,1)}) fusion(f32[1024]{0:T(1024)S(1)} %bitcast.28, f32[1024]{0:T(1024)S(1)} %bitcast.29, f32[256]{0:T(256)S(1)} %add_rsqrt_fusion.3, f32[256]{0:T(256)S(1)} %get-tuple-element.16, bf16[256,1024]{1,0:T(8,128)(2,1)} %collective-permute-done, ...), kind=kLoop, calls=%fused_computation.54 | loop fusion | flops 5242880 | bytes 4206592 | tf_op jit(solution)/shard_map/convert_element_type | solution.py:94
  42.8 0.0 copy-done
  42.8 6.0 %convolution_convert_fusion.3 = bf16[256,1024]{1,0:T(8,128)(2,1)} fusion(bf16[1024,1024]{1,0:T(8,128)(2,1)S(1)} %copy-done, bf16[256,1024]{1,0:T(8,128)(2,1)} %get-tuple-element.7, bf16[1024,1024]{1,0:T(8,128)(2,1)} %param.23), kind=kOutput, calls=%fused_computation.5 | convolution fusion | flops 1091043328 | bytes 5242880 | tf_op jit(solution)/shard_map/dot_general | solution.py:100
  48.9 0.1 collective-permute-start.1
  49.0 0.0 copy-done.3
  49.0 5.9 %convolution_convert_fusion.2 = bf16[256,1024]{1,0:T(8,128)(2,1)} fusion(bf16[1024,1024]{1,0:T(8,128)(2,1)S(1)} %copy-done, bf16[256,1024]{1,0:T(8,128)(2,1)S(1)} %copy-done.3, bf16[1024,1024]{1,0:T(8,128)(2,1)} %param.23), kind=kOutput, calls=%fused_computation.4 | convolution fusion | flops 1091043328 | bytes 5242880 | tf_op jit(solution)/shard_map/dot_general | solution.py:100
  55.0 0.4 collective-permute-start.3
  55.3 0.0 collective-permute-done.1
  55.3 0.0 copy-done.2
  55.3 1.5 %fusion.82 = f32[256]{0:T(256)S(1)} fusion(bf16[256,1024]{1,0:T(8,128)(2,1)} %collective-permute-done.1, bf16[256,1024]{1,0:T(8,128)(2,1)} %convolution_convert_fusion.3, bf16[256,1024]{1,0:T(8,128)(2,1)S(1)} %copy-done.2), kind=kLoop, calls=%fused_computation.121 | loop fusion | flops 1572608 | bytes 1573888 | tf_op jit(solution)/shard_map/reduce_sum | solution.py:12
  56.8 1.6 %multiply_reduce_fusion.2 = f32[256]{0:T(256)S(1)} fusion(f32[256]{0:T(256)S(1)} %broadcast_multiply_fusion.2, bf16[256,1024]{1,0:T(8,128)(2,1)} %collective-permute-done.1, bf16[256,1024]{1,0:T(8,128)(2,1)} %convolution_convert_fusion.3, bf16[256,1024]{1,0:T(8,128)(2,1)S(1)} %copy-done.2), kind=kLoop, calls=%fused_computation.39 | loop fusion | flops 2096896 | bytes 1574912 | tf_op jit(solution)/shard_map/reduce_sum | solution.py:13
  58.4 0.0 collective-permute-done.3
  58.4 0.0 copy-done.8
  58.4 0.3 fusion.83
  58.7 0.4 multiply_reduce_fusion
  59.1 1.9 %add_convert_fusion.2 = (bf16[256,1024]{1,0:T(8,128)(2,1)S(1)}, bf16[256,1024]{1,0:T(8,128)(2,1)S(1)}) fusion(f32[1024]{0:T(1024)S(1)} %bitcast.26, f32[1024]{0:T(1024)S(1)} %bitcast.27, f32[256]{0:T(256)S(1)} %add_rsqrt_fusion.2, f32[256]{0:T(256)S(1)} %broadcast_multiply_fusion.2, bf16[256,1024]{1,0:T(8,128)(2,1)} %collective-permute-done.1, ...), kind=kLoop, calls=%fused_computation.38 | loop fusion | flops 5242880 | bytes 4206592 | tf_op jit(solution)/shard_map/convert_element_type | solution.py:101
  60.9 0.0 copy-start.4
  60.9 0.0 copy-start.6
  61.0 0.8 copy-done.4
  61.7 0.1 fusion.89
  61.8 0.1 copy-done.6
  61.9 0.3 broadcast_in_dim.6
  62.2 0.5 broadcast.454
  62.7 2.2 %reduce.5 = bf16[256,512]{1,0:T(8,128)(2,1)S(1)} reduce(bf16[256,1,512]{2,1,0:T(2,128)(2,1)S(1)} %broadcast_in_dim.6, bf16[]{:T(256)} %broadcast.454), dimensions={1}, to_apply=%broadcast_in_dim.6.reduce_sub_computation | reduce | bytes 524290 | tf_op jit(solution)/shard_map/broadcast_in_dim | solution.py:145
  64.9 0.0 copy-start.5
  64.9 0.0 copy-start.7
  64.9 0.8 reshape.75
  65.7 28.6 %all_to_all.16 = bf16[256,2,256]{2,1,0:T(2,128)(2,1)S(1)} all-to-all(bf16[256,2,256]{2,1,0:T(2,128)(2,1)} %reshape.75), channel_id=1, replica_groups=mesh['req'=128,'tp'=2] {'req','tp'}, dimensions={0} | all-to-all | bytes 524288 | tf_op jit(solution)/shard_map/all_to_all | solution.py:144
  94.2 0.9 reshape.76
  95.2 3.2 %reduce.3 = bf16[256,512]{1,0:T(8,128)(2,1)} reduce(bf16[256,1,512]{2,1,0:T(2,128)(2,1)} %reshape.76, bf16[]{:T(256)} %constant.116), dimensions={1}, to_apply=%all_to_all.10.reduce_sub_computation | reduce | bytes 524290 | tf_op jit(solution)/shard_map/all_to_all | solution.py:144
  98.4 1.0 reshape.72
  99.4 1.3 %convolution_reduce_fusion = f32[128]{0:T(128)S(1)} fusion(bf16[128,1024]{1,0:T(8,128)(2,1)S(1)} %reshape.72, bf16[192,1024]{1,0:T(8,128)(2,1)} %param.27), kind=kOutput, calls=%fused_computation.12 | convolution fusion | flops 50356096 | bytes 655872 | tf_op jit(solution)/shard_map/rd,vd->rv/dot_general | solution.py:147
  100.7 0.0 copy-start.11
  100.7 0.1 broadcast_in_dim.7
  100.8 0.8 all_to_all.13
  101.6 5.5 %all-to-all-start.1 = ((f32[256,1,1]{2,1,0:T(1,128)}), f32[256,1,1]{2,1,0:T(1,128)S(1)}, u32[]{:S(2)}, u32[]{:S(2)}) async-start(f32[256,1,1]{2,1,0:T(1,128)} %all_to_all.13), calls=%async_computation.1 | async-start | bytes 262144 | tf_op jit(solution)/shard_map/all_to_all | solution.py:150
  107.1 0.0 copy-done.5
  107.1 0.0 copy-done.7
  107.1 1.0 pad_maximum_fusion
  108.1 12.0 %all-to-all-done.1 = f32[256,1,1]{2,1,0:T(1,128)S(1)} async-done(((f32[256,1,1]{2,1,0:T(1,128)}), f32[256,1,1]{2,1,0:T(1,128)S(1)}, u32[]{:S(2)}, u32[]{:S(2)}) %all-to-all-start.1) | async-done | bytes 1056 | tf_op jit(solution)/shard_map/all_to_all | solution.py:150
  120.1 0.9 reduce_max.21
  (17 shorter events, 0.1 us)
Async XLA Ops:
  0.6 42.2 %copy-start = (bf16[1024,1024]{1,0:T(8,128)(2,1)S(1)}, bf16[1024,1024]{1,0:T(8,128)(2,1)}, u32[]{:S(2)}) copy-start(bf16[1024,1024]{1,0:T(8,128)(2,1)} %param.24) | copy-start | bytes 6291460
  0.6 4.0 %copy-start.1 = (bf16[512,1024]{1,0:T(8,128)(2,1)S(1)}, bf16[512,1024]{1,0:T(8,128)(2,1)}, u32[]{:S(2)}) copy-start(bf16[512,1024]{1,0:T(8,128)(2,1)} %param.14) | copy-start | bytes 3145732
  1.5 3.2 %copy-start.12 = (bf16[1024,512]{1,0:T(8,128)(2,1)S(1)}, bf16[1024,512]{1,0:T(8,128)(2,1)}, u32[]{:S(2)}) copy-start(bf16[1024,512]{1,0:T(8,128)(2,1)} %param.20) | copy-start | bytes 3145732
  4.6 1.5 %copy-start.13 = (bf16[1024,512]{1,0:T(8,128)(2,1)S(1)}, bf16[1024,512]{1,0:T(8,128)(2,1)}, u32[]{:S(2)}) copy-start(bf16[1024,512]{1,0:T(8,128)(2,1)} %param.21) | copy-start | bytes 3145732
  6.1 1.5 %copy-start.14 = (s32[128]{0:T(128)S(1)}, s32[128]{0:T(128)}, u32[]{:S(2)}) copy-start(s32[128]{0:T(128)} %param.16) | copy-start | bytes 1540
  24.9 8.3 %copy-start.9 = (f32[2,1024]{1,0:T(2,128)S(1)}, f32[2,1024]{1,0:T(2,128)}, u32[]{:S(2)}) copy-start(f32[2,1024]{1,0:T(2,128)} %param.26) | copy-start | bytes 24580
  24.9 8.4 %copy-start.10 = (f32[2,1024]{1,0:T(2,128)S(1)}, f32[2,1024]{1,0:T(2,128)}, u32[]{:S(2)}) copy-start(f32[2,1024]{1,0:T(2,128)} %param.25) | copy-start | bytes 24580
  27.5 5.8 %collective-permute-start = (bf16[256,1024]{1,0:T(8,128)(2,1)}, bf16[256,1024]{1,0:T(8,128)(2,1)}, u32[]{:S(2)}, u32[]{:S(2)}) collective-permute-start(bf16[256,1024]{1,0:T(8,128)(2,1)} %convolution_convert_fusion.1), channel_id=1, source_target_pairs={{0,1},{1,0},{2,3},{3,2},{4,5},{5,4},{6,7},{7,6},{8,9},{9,8},{10,11... | collective-permute-start | bytes 1572872 | tf_op jit(solution)/shard_map/ppermute | solution.py:19
  33.3 2.3 %collective-permute-start.2 = (bf16[256,1024]{1,0:T(8,128)(2,1)}, bf16[256,1024]{1,0:T(8,128)(2,1)}, u32[]{:S(2)}, u32[]{:S(2)}) collective-permute-start(bf16[256,1024]{1,0:T(8,128)(2,1)} %convolution_convert_fusion), channel_id=1, source_target_pairs={{0,1},{1,0},{2,3},{3,2},{4,5},{5,4},{6,7},{7,6},{8,9},{9,8},{10,11... | collective-permute-start | bytes 1572872 | tf_op jit(solution)/shard_map/ppermute | solution.py:19
  42.8 6.2 %copy-start.3 = (bf16[256,1024]{1,0:T(8,128)(2,1)S(1)}, bf16[256,1024]{1,0:T(8,128)(2,1)}, u32[]{:S(2)}) copy-start(bf16[256,1024]{1,0:T(8,128)(2,1)} %get-tuple-element.8) | copy-start | bytes 1572868
  48.9 6.4 %collective-permute-start.1 = (bf16[256,1024]{1,0:T(8,128)(2,1)}, bf16[256,1024]{1,0:T(8,128)(2,1)}, u32[]{:S(2)}, u32[]{:S(2)}) collective-permute-start(bf16[256,1024]{1,0:T(8,128)(2,1)} %convolution_convert_fusion.3), channel_id=1, source_target_pairs={{0,1},{1,0},{2,3},{3,2},{4,5},{5,4},{6,7},{7,6},{8,9},{9,8},{10,11... | collective-permute-start | bytes 1572872 | tf_op jit(solution)/shard_map/ppermute | solution.py:19
  49.0 6.3 %copy-start.2 = (bf16[256,1024]{1,0:T(8,128)(2,1)S(1)}, bf16[256,1024]{1,0:T(8,128)(2,1)}, u32[]{:S(2)}) copy-start(bf16[256,1024]{1,0:T(8,128)(2,1)} %get-tuple-element.7) | copy-start | bytes 1572868
  54.9 3.4 %copy-start.8 = (bf16[256,1024]{1,0:T(8,128)(2,1)S(1)}, bf16[256,1024]{1,0:T(8,128)(2,1)}, u32[]{:S(2)}) copy-start(bf16[256,1024]{1,0:T(8,128)(2,1)} %convolution_convert_fusion.2) | copy-start | bytes 1572868
  55.0 3.4 %collective-permute-start.3 = (bf16[256,1024]{1,0:T(8,128)(2,1)}, bf16[256,1024]{1,0:T(8,128)(2,1)S(1)}, u32[]{:S(2)}, u32[]{:S(2)}) collective-permute-start(bf16[256,1024]{1,0:T(8,128)(2,1)} %convolution_convert_fusion.2), channel_id=1, source_target_pairs={{0,1},{1,0},{2,3},{3,2},{4,5},{5,4},{6,7},{7,6},{8,9},{9,8},{10,11... | collective-permute-start | bytes 1572872 | tf_op jit(solution)/shard_map/ppermute | solution.py:19
  60.9 0.8 copy-start.4
  60.9 1.0 copy-start.6
  64.9 42.2 %copy-start.5 = (bf16[256,1024]{1,0:T(8,128)(2,1)S(1)}, bf16[256,1024]{1,0:T(8,128)(2,1)}, u32[]{:S(2)}) copy-start(bf16[256,1024]{1,0:T(8,128)(2,1)} %copy-done.4) | copy-start | bytes 1572868
  64.9 42.2 %copy-start.7 = (bf16[256,1024]{1,0:T(8,128)(2,1)S(1)}, bf16[256,1024]{1,0:T(8,128)(2,1)}, u32[]{:S(2)}) copy-start(bf16[256,1024]{1,0:T(8,128)(2,1)} %copy-done.6) | copy-start | bytes 1572868
  100.7 20.3 %copy-start.11 = (f32[128]{0:T(128)}, f32[128]{0:T(128)S(1)}, u32[]{:S(2)}) copy-start(f32[128]{0:T(128)S(1)} %convolution_reduce_fusion) | copy-start | bytes 1540
  101.6 18.6 %all-to-all-start.1 = ((f32[256,1,1]{2,1,0:T(1,128)}), f32[256,1,1]{2,1,0:T(1,128)S(1)}, u32[]{:S(2)}, u32[]{:S(2)}) async-start(f32[256,1,1]{2,1,0:T(1,128)} %all_to_all.13), calls=%async_computation.1 | async-start | bytes 262144 | tf_op jit(solution)/shard_map/all_to_all | solution.py:150

commit v6 on v3

--- a/solution.py
+++ b/solution.py
@@ -105,9 +105,12 @@
     ln_biases,
     embed,
 ):
+    xy_size = lax.psum(1, "xy")
+    z_size = lax.psum(1, "z")
+    tp_size = lax.psum(1, "tp")
     block_rows = tokens.shape[0]
     local_width = w_query.shape[1]
-    my_index = lax.axis_index("req")
+    my_index = lax.axis_index(("xy", "z"))
     my_cache = lax.dynamic_index_in_dim(cache_len, my_index, 0, keepdims=False)
     my_valid = group_len[0]
     queries = jnp.dot(tokens, w_query, preferred_element_type=jnp.float32).astype(jnp.bfloat16)
@@ -127,24 +130,39 @@
         jnp.bfloat16
     )
     last_row = lax.dynamic_slice_in_dim(layer_out, my_valid - 1, 1, 0)
-    reqs = cache_len.shape[0]
+    width = last_row.shape[1]
+    near = lax.all_to_all(jnp.broadcast_to(last_row, (z_size, width)), "z", 0, 0, tiled=True)
     all_rows = lax.all_to_all(
-        jnp.broadcast_to(last_row, (reqs, last_row.shape[1])), "req", 0, 0, tiled=True
-    )
+        jnp.broadcast_to(near[None], (xy_size, z_size, width)), "xy", 0, 0, tiled=True
+    ).reshape(xy_size * z_size, width)
     logits = jnp.einsum("rd,vd->rv", all_rows, embed, preferred_element_type=jnp.float32)
     slice_best = jnp.max(logits, axis=1)
-    mine = jnp.max(lax.all_to_all(slice_best[:, None], "req", 0, 0, tiled=True), axis=0)
-    best_logit = jnp.maximum(mine, lax.ppermute(mine, "tp", [(0, 1), (1, 0)]))
+    by_plane = lax.all_to_all(slice_best.reshape(xy_size, z_size), "xy", 0, 0, tiled=True)
+    plane_best = jnp.max(by_plane, axis=0)
+    spread = jnp.repeat(plane_best, tp_size)[:, None]
+    best_logit = jnp.max(lax.all_to_all(spread, ("z", "tp"), 0, 0, tiled=True), axis=0)
     return (layer_out, best_logit, slice_best[:, None])
 
 
+def z_extent(mesh):
+    devices = mesh.devices.reshape(-1)
+    coords = getattr(devices[0], "coords", None)
+    if coords is None:
+        return 8
+    return len({tuple(d.coords)[2] for d in devices})
+
+
 def solution(mesh):
+    reqs, cores = mesh.devices.shape
+    z = z_extent(mesh)
+    fine = jax.sharding.Mesh(mesh.devices.reshape(reqs // z, z, cores), ("xy", "z", "tp"))
+    R = ("xy", "z")
     placed = (
-        P("req", None),
-        P("req"),
+        P(R, None),
+        P(R),
         P(),
-        P("req", None, "tp"),
-        P("req", None, "tp"),
+        P(R, None, "tp"),
+        P(R, None, "tp"),
         P(None, "tp"),
         P(None, "tp"),
         P(None, "tp"),
@@ -153,12 +171,12 @@
         P("tp", None),
         P(),
         P(),
-        P(("req", "tp"), None),
+        P(("xy", "z", "tp"), None),
     )
     return jax.shard_map(
         shards,
-        mesh=mesh,
+        mesh=fine,
         in_specs=placed,
-        out_specs=(P("req", None), P("req"), P(None, ("req", "tp"))),
+        out_specs=(P(R, None), P(R), P(None, ("xy", "z", "tp"))),
         check_vma=False,
     )

time: 109 us -> 107 us (0.982)
  blocking collectives: 44.3 us -> 50.5 us
  starting transfers between devices: 6.43 us -> 3.85 us
  between operations: 4.06 us -> 1.6 us
  other arithmetic: 11.7 us -> 10.2 us
    all_to_all x2 -> x4, blocking collectives: 44.3 us -> 50.5 us  [the longest x1 13.9 us: shards(): lax.all_to_all(jnp.broadcast_to(near[None], (xy_size, z_size, width)), 'x...]
    ppermute x1 -> x0, starting transfers between devices: 2.59 us -> none  [shards(): best_logit = jnp.maximum(mine, lax.ppermute(mine, 'tp', [(0, 1), (1, 0)]))]
    broadcast_in_dim x1, other arithmetic: 2.15 us -> 0.73 us  [shards(): jnp.broadcast_to(last_row, (z_size, width))]
  transfers between devices with their start and end apart: 3 -> 2, of which waited for: 3 -> 2; matrix products, arithmetic and copies ran while one was open for 0% -> 0% of each run, Pallas kernels for 0% -> 0%
where the time goes in v6:
time: 107 us
  blocking collectives  50.5 us (47%)
  matrix products  17.4 us (16%)
  Pallas kernels  15.5 us (14%)
  other arithmetic  10.2 us (10%)
  waiting for transfers between devices  4.87 us (5%)
  starting transfers between devices  3.85 us (4%)
  local copies, waits for them, and re-layouts  3.05 us (3%)
  between operations  1.6 us (1%)
    pallas_call x1, Pallas kernels, attention(): pl.pallas_call(attention_kernel, out_shape=jax.ShapeDtypeStruct((rows, wi...  15.5 us
    all_to_all x1, blocking collectives, shards(): lax.all_to_all(jnp.broadcast_to(near[None], (xy_size, z_size, width)), 'x...  13.9 us
    all_to_all x1, blocking collectives, shards(): lax.all_to_all(spread, ('z', 'tp'), 0, 0, tiled=True)  13.8 us
    all_to_all x1, blocking collectives, shards(): lax.all_to_all(jnp.broadcast_to(last_row, (z_size, width)), 'z', 0, 0, ti...  12.9 us
    all_to_all x1, blocking collectives, shards(): lax.all_to_all(slice_best.reshape(xy_size, z_size), 'xy', 0, 0, tiled=True)  9.87 us
    dot_general x1, matrix products, shards(): jnp.dot(active, w_down, preferred_element_type=jnp.float32)  8.8 us
    ppermute x2, waiting for transfers between devices, pair_sum(): other = lax.ppermute(own, 'tp', [(0, 1), (1, 0)])  4.87 us
    ppermute x2, starting transfers between devices, pair_sum(): other = lax.ppermute(own, 'tp', [(0, 1), (1, 0)])  3.85 us
  transfers between devices with their start and end apart: 2, of which 2 were waited for; matrix products, arithmetic and copies ran while one was open for 0% of the time, Pallas kernels for 0%

profile of v6, /device:TPU:1, one launch (start us, length us, event | category | flops | bytes accessed | tf_op | source)
XLA Modules:
  0.0 107.0 jit_solution(16374159255001867738)
XLA Ops:
  0.6 0.0 copy-start
  0.6 0.0 copy-start.1
  1.5 0.0 copy-start.9
  1.5 3.2 %convolution_convert_fusion.4.q_ref = bf16[512,512]{1,0:T(8,128)(2,1)} fusion(bf16[512,1024]{1,0:T(8,128)(2,1)} %param.14, bf16[1024,512]{1,0:T(8,128)(2,1)} %param.19), kind=kOutput, calls=%fused_computation.29 | convolution fusion | flops 537133056 | bytes 2621440 | tf_op jit(solution)/shard_map/dot_general | solution.py:116
  4.6 0.0 copy-done.1
  4.6 0.0 copy-done.9
  4.6 0.0 copy-start.10
  4.6 1.5 %convolution_convert_fusion.3.kn_ref = bf16[512,512]{1,0:T(8,128)(2,1)} fusion(bf16[512,1024]{1,0:T(8,128)(2,1)S(1)} %copy-done.1, bf16[1024,512]{1,0:T(8,128)(2,1)S(1)} %copy-done.9), kind=kOutput, calls=%fused_computation.28 | convolution fusion | flops 537133056 | bytes 2621440 | tf_op jit(solution)/shard_map/dot_general | solution.py:117
  6.1 0.0 copy-done.10
  6.1 0.0 copy-start.11
  6.1 1.5 %convolution_convert_fusion.2.vn_ref = bf16[512,512]{1,0:T(8,128)(2,1)} fusion(bf16[512,1024]{1,0:T(8,128)(2,1)S(1)} %copy-done.1, bf16[1024,512]{1,0:T(8,128)(2,1)S(1)} %copy-done.10), kind=kOutput, calls=%fused_computation.27 | convolution fusion | flops 537133056 | bytes 2621440 | tf_op jit(solution)/shard_map/dot_general | solution.py:118
  7.7 0.0 copy-done.11
  7.7 0.6 dynamic_slice.9
  8.2 1.2 %pad_add_fusion.lens_ref = s32[2]{0:T(128)} fusion(s32[1]{0:T(128)S(6)} %copy.22, s32[1]{0:T(128)} %dynamic_slice.9), kind=kLoop, calls=%fused_computation.70 | loop fusion | flops 2 | bytes 16 | tf_op jit(solution)/shard_map/stack | solution.py:119
  9.5 15.5 %shard_map.157 = bf16[512,512]{1,0:T(8,128)(2,1)} custom-call(s32[2]{0:T(128)} %pad_add_fusion.lens_ref, bf16[512,512]{1,0:T(8,128)(2,1)} %convolution_convert_fusion.4.q_ref, bf16[1024,512]{1,0:T(8,128)(2,1)} %bitcast.36, bf16[1024,512]{1,0:T(8,128)(2,1)} %bitcast.37, bf16[512,512]{1,0:T(8,128)(2,1)} %convolution_convert_fusion.3.kn_ref, ...), custom_call_target="tpu_custom_call" | custom-call | flops 3221225472 | bytes 4194304 | tf_op jit(solution)/shard_map/pallas_call | solution.py:69
  24.9 0.0 copy-start.6
  24.9 0.0 copy-start.7
  24.9 2.1 %convolution_convert_fusion.1 = bf16[512,1024]{1,0:T(8,128)(2,1)S(1)} fusion(bf16[512,512]{1,0:T(8,128)(2,1)} %shard_map.157, bf16[512,1024]{1,0:T(8,128)(2,1)} %param.22), kind=kOutput, calls=%fused_computation.26 | convolution fusion | flops 537395200 | bytes 2621440 | tf_op jit(solution)/shard_map/dot_general | solution.py:121
  27.1 3.5 %collective-permute-start = (bf16[512,1024]{1,0:T(8,128)(2,1)S(1)}, bf16[512,1024]{1,0:T(8,128)(2,1)S(1)}, u32[]{:S(2)}, u32[]{:S(2)}) collective-permute-start(bf16[512,1024]{1,0:T(8,128)(2,1)S(1)} %convolution_convert_fusion.1), channel_id=1, source_target_pairs={{0,1},{1,0},{2,3},{3,2},{4,5},{5,4},{6,7},{7,6},{8,9},{9,8},{10,11... | collective-permute-start | bytes 3145736 | tf_op jit(solution)/shard_map/ppermute | solution.py:19
  30.5 0.0 copy-done.6
  30.6 0.0 copy-done.7
  30.6 2.2 %collective-permute-done = bf16[512,1024]{1,0:T(8,128)(2,1)S(1)} collective-permute-done((bf16[512,1024]{1,0:T(8,128)(2,1)S(1)}, bf16[512,1024]{1,0:T(8,128)(2,1)S(1)}, u32[]{:S(2)}, u32[]{:S(2)}) %collective-permute-start) | collective-permute-done | bytes 1048608 | tf_op jit(solution)/shard_map/ppermute | solution.py:19
  32.8 0.5 fusion.41
  33.3 0.0 copy-start.2
  33.3 0.6 multiply_reduce_fusion.1
  34.0 0.6 copy-done.2
  34.5 0.7 add_convert_fusion.1
  35.2 0.0 copy-done
  35.2 8.8 %convolution_convert_fusion = bf16[512,1024]{1,0:T(8,128)(2,1)} fusion(bf16[1024,1024]{1,0:T(8,128)(2,1)S(1)} %copy-done, bf16[512,1024]{1,0:T(8,128)(2,1)S(1)} %add_convert_fusion.1, bf16[1024,1024]{1,0:T(8,128)(2,1)} %param.23), kind=kOutput, calls=%fused_computation.25 | convolution fusion | flops 2182086656 | bytes 6291456 | tf_op jit(solution)/shard_map/dot_general | solution.py:128
  44.0 0.4 collective-permute-start.1
  44.4 0.0 copy-start.3
  44.4 2.6 %collective-permute-done.1 = bf16[512,1024]{1,0:T(8,128)(2,1)} collective-permute-done((bf16[512,1024]{1,0:T(8,128)(2,1)}, bf16[512,1024]{1,0:T(8,128)(2,1)}, u32[]{:S(2)}, u32[]{:S(2)}) %collective-permute-start.1) | collective-permute-done | bytes 1048608 | tf_op jit(solution)/shard_map/ppermute | solution.py:19
  47.0 2.0 %fusion.42 = f32[512]{0:T(512)S(1)} fusion(bf16[512,1024]{1,0:T(8,128)(2,1)} %collective-permute-done.1, bf16[512,1024]{1,0:T(8,128)(2,1)} %convolution_convert_fusion, bf16[512,1024]{1,0:T(8,128)(2,1)S(1)} %add_convert_fusion.1), kind=kLoop, calls=%fused_computation.62 | loop fusion | flops 3145216 | bytes 3147776 | tf_op jit(solution)/shard_map/reduce_sum | solution.py:12
  49.1 0.0 copy-done.3
  49.1 1.8 %multiply_reduce_fusion = f32[512]{0:T(512)S(1)} fusion(f32[512]{0:T(512)S(1)} %broadcast_multiply_fusion, bf16[512,1024]{1,0:T(8,128)(2,1)} %collective-permute-done.1, bf16[512,1024]{1,0:T(8,128)(2,1)S(1)} %copy-done.3, bf16[512,1024]{1,0:T(8,128)(2,1)S(1)} %add_convert_fusion.1), kind=kLoop, calls=%fused_computation.5 | loop fusion | flops 4193792 | bytes 3149824 | tf_op jit(solution)/shard_map/reduce_sum | solution.py:13
  50.9 0.0 copy-start.5
  50.9 2.0 %add_convert_fusion = bf16[512,1024]{1,0:T(8,128)(2,1)S(1)} fusion(f32[1024]{0:T(1024)S(1)} %bitcast.31, f32[1024]{0:T(1024)S(1)} %bitcast.32, f32[512]{0:T(512)S(1)} %add_rsqrt_fusion, f32[512]{0:T(512)S(1)} %broadcast_multiply_fusion, bf16[512,1024]{1,0:T(8,128)(2,1)} %collective-permute-done.1, bf16[512,1024]{1,0:T(8,128)(2,1)S(1)} %copy-done.3, ...), kind=kLoop, calls=%fused_computation.4 | loop fusion | flops 5242880 | bytes 4206592 | tf_op jit(solution)/shard_map/convert_element_type | solution.py:129
  52.9 0.0 copy-start.4
  52.9 1.0 copy-done.4
  53.9 0.5 broadcast.61
  54.4 0.7 reduce.5
  55.2 12.9 %all_to_all.30 = bf16[8,2,512]{2,1,0:T(2,128)(2,1)S(1)} all-to-all(bf16[8,2,512]{2,1,0:T(2,128)(2,1)S(1)} %reshape.55), channel_id=1, replica_groups=mesh['xy'=16,'z'=8,'tp'=2] {'z'}, dimensions={0} | all-to-all | bytes 32768 | tf_op jit(solution)/shard_map/all_to_all | solution.py:134
  68.2 13.9 %all_to_all.31 = bf16[16,8,1024]{2,1,0:T(8,128)(2,1)S(1)} all-to-all(bf16[16,8,1024]{2,1,0:T(8,128)(2,1)S(1)} %broadcast_in_dim.12), channel_id=1, replica_groups=mesh['xy'=16,'z'=8,'tp'=2] {'xy'}, dimensions={0} | all-to-all | bytes 524288 | tf_op jit(solution)/shard_map/all_to_all | solution.py:135
  82.1 0.0 copy-done.5
  82.1 0.3 convolution_reduce_fusion
  82.4 0.0 copy-start.8
  82.4 0.1 all_to_all.21
  82.5 9.9 %all_to_all.32 = f32[16,1,8]{2,1,0:T(1,128)S(1)} all-to-all(f32[16,1,8]{2,1,0:T(1,128)S(1)} %bitcast.30), channel_id=1, replica_groups=mesh['xy'=16,'z'=8,'tp'=2] {'xy'}, dimensions={0} | all-to-all | bytes 1024 | tf_op jit(solution)/shard_map/all_to_all | solution.py:140
  92.4 0.1 broadcast_in_dim.26
  92.5 0.1 all_to_all.25
  92.5 13.8 %all_to_all.33 = f32[16,1,1]{2,1,0:T(1,128)S(1)} all-to-all(f32[16,1,1]{2,1,0:T(1,128)S(1)} %all_to_all.25), channel_id=1, replica_groups=mesh['xy'=16,'z'=8,'tp'=2] {'z','tp'}, dimensions={0} | all-to-all | bytes 128 | tf_op jit(solution)/shard_map/all_to_all | solution.py:143
  106.4 0.6 reduce_max.31
  107.0 0.0 copy-done.8
  (13 shorter events, 0.2 us)
Async XLA Ops:
  0.6 34.6 %copy-start = (bf16[1024,1024]{1,0:T(8,128)(2,1)S(1)}, bf16[1024,1024]{1,0:T(8,128)(2,1)}, u32[]{:S(2)}) copy-start(bf16[1024,1024]{1,0:T(8,128)(2,1)} %param.24) | copy-start | bytes 6291460
  0.6 4.0 %copy-start.1 = (bf16[512,1024]{1,0:T(8,128)(2,1)S(1)}, bf16[512,1024]{1,0:T(8,128)(2,1)}, u32[]{:S(2)}) copy-start(bf16[512,1024]{1,0:T(8,128)(2,1)} %param.14) | copy-start | bytes 3145732
  1.5 3.2 %copy-start.9 = (bf16[1024,512]{1,0:T(8,128)(2,1)S(1)}, bf16[1024,512]{1,0:T(8,128)(2,1)}, u32[]{:S(2)}) copy-start(bf16[1024,512]{1,0:T(8,128)(2,1)} %param.20) | copy-start | bytes 3145732
  4.6 1.5 %copy-start.10 = (bf16[1024,512]{1,0:T(8,128)(2,1)S(1)}, bf16[1024,512]{1,0:T(8,128)(2,1)}, u32[]{:S(2)}) copy-start(bf16[1024,512]{1,0:T(8,128)(2,1)} %param.21) | copy-start | bytes 3145732
  6.1 1.5 %copy-start.11 = (s32[128]{0:T(128)S(1)}, s32[128]{0:T(128)}, u32[]{:S(2)}) copy-start(s32[128]{0:T(128)} %param.16) | copy-start | bytes 1540
  24.9 5.6 %copy-start.6 = (f32[2,1024]{1,0:T(2,128)S(1)}, f32[2,1024]{1,0:T(2,128)}, u32[]{:S(2)}) copy-start(f32[2,1024]{1,0:T(2,128)} %param.26) | copy-start | bytes 24580
  24.9 5.6 %copy-start.7 = (f32[2,1024]{1,0:T(2,128)S(1)}, f32[2,1024]{1,0:T(2,128)}, u32[]{:S(2)}) copy-start(f32[2,1024]{1,0:T(2,128)} %param.25) | copy-start | bytes 24580
  27.1 5.8 %collective-permute-start = (bf16[512,1024]{1,0:T(8,128)(2,1)S(1)}, bf16[512,1024]{1,0:T(8,128)(2,1)S(1)}, u32[]{:S(2)}, u32[]{:S(2)}) collective-permute-start(bf16[512,1024]{1,0:T(8,128)(2,1)S(1)} %convolution_convert_fusion.1), channel_id=1, source_target_pairs={{0,1},{1,0},{2,3},{3,2},{4,5},{5,4},{6,7},{7,6},{8,9},{9,8},{10,11... | collective-permute-start | bytes 3145736 | tf_op jit(solution)/shard_map/ppermute | solution.py:19
  33.3 1.2 %copy-start.2 = (bf16[512,1024]{1,0:T(8,128)(2,1)S(1)}, bf16[512,1024]{1,0:T(8,128)(2,1)}, u32[]{:S(2)}) copy-start(bf16[512,1024]{1,0:T(8,128)(2,1)} %param.14) | copy-start | bytes 3145732
  44.0 3.0 %collective-permute-start.1 = (bf16[512,1024]{1,0:T(8,128)(2,1)}, bf16[512,1024]{1,0:T(8,128)(2,1)}, u32[]{:S(2)}, u32[]{:S(2)}) collective-permute-start(bf16[512,1024]{1,0:T(8,128)(2,1)} %convolution_convert_fusion), channel_id=1, source_target_pairs={{0,1},{1,0},{2,3},{3,2},{4,5},{5,4},{6,7},{7,6},{8,9},{9,8},{10,11... | collective-permute-start | bytes 3145736 | tf_op jit(solution)/shard_map/ppermute | solution.py:19
  44.4 4.7 %copy-start.3 = (bf16[512,1024]{1,0:T(8,128)(2,1)S(1)}, bf16[512,1024]{1,0:T(8,128)(2,1)}, u32[]{:S(2)}) copy-start(bf16[512,1024]{1,0:T(8,128)(2,1)} %convolution_convert_fusion) | copy-start | bytes 3145732
  50.9 31.2 %copy-start.5 = (bf16[192,1024]{1,0:T(8,128)(2,1)S(1)}, bf16[192,1024]{1,0:T(8,128)(2,1)}, u32[]{:S(2)}) copy-start(bf16[192,1024]{1,0:T(8,128)(2,1)} %param.27) | copy-start | bytes 1179652
  52.9 1.0 copy-start.4
  82.4 24.6 %copy-start.8 = (f32[128]{0:T(128)}, f32[128]{0:T(128)S(1)}, u32[]{:S(2)}) copy-start(f32[128]{0:T(128)S(1)} %convolution_reduce_fusion) | copy-start | bytes 1540

commit v7 on v3

--- a/solution.py
+++ b/solution.py
@@ -133,8 +133,8 @@
     )
     logits = jnp.einsum("rd,vd->rv", all_rows, embed, preferred_element_type=jnp.float32)
     slice_best = jnp.max(logits, axis=1)
-    mine = jnp.max(lax.all_to_all(slice_best[:, None], "req", 0, 0, tiled=True), axis=0)
-    best_logit = jnp.maximum(mine, lax.ppermute(mine, "tp", [(0, 1), (1, 0)]))
+    spread = jnp.repeat(slice_best, 2)[:, None]
+    best_logit = jnp.max(lax.all_to_all(spread, ("req", "tp"), 0, 0, tiled=True), axis=0)
     return (layer_out, best_logit, slice_best[:, None])
 
 

time: 109 us -> 106 us (0.972)
  blocking collectives: 44.3 us -> 47.4 us
  starting transfers between devices: 6.43 us -> 3.84 us
  between operations: 4.06 us -> 1.59 us
    all_to_all x1, blocking collectives: 16.6 us -> 19.7 us  [shards(): lax.all_to_all(spread, ('req', 'tp'), 0, 0, tiled=True)]
    ppermute x1 -> x0, starting transfers between devices: 2.59 us -> none  [shards(): best_logit = jnp.maximum(mine, lax.ppermute(mine, 'tp', [(0, 1), (1, 0)]))]
  transfers between devices with their start and end apart: 3 -> 2, of which waited for: 3 -> 2; matrix products, arithmetic and copies ran while one was open for 0% -> 0% of each run, Pallas kernels for 0% -> 0%
where the time goes in v7:
time: 106 us
  blocking collectives  47.4 us (45%)
  matrix products  17.4 us (16%)
  Pallas kernels  15.5 us (15%)
  other arithmetic  11.8 us (11%)
  waiting for transfers between devices  4.87 us (5%)
  starting transfers between devices  3.84 us (4%)
  local copies, waits for them, and re-layouts  3.64 us (3%)
  between operations  1.59 us (2%)
    all_to_all x1, blocking collectives, shards(): lax.all_to_all(jnp.broadcast_to(last_row, (reqs, last_row.shape[1])), 're...  27.7 us
    all_to_all x1, blocking collectives, shards(): lax.all_to_all(spread, ('req', 'tp'), 0, 0, tiled=True)  19.7 us
    pallas_call x1, Pallas kernels, attention(): pl.pallas_call(attention_kernel, out_shape=jax.ShapeDtypeStruct((rows, wi...  15.5 us
    dot_general x1, matrix products, shards(): jnp.dot(active, w_down, preferred_element_type=jnp.float32)  8.8 us
    ppermute x2, waiting for transfers between devices, pair_sum(): other = lax.ppermute(own, 'tp', [(0, 1), (1, 0)])  4.87 us
    ppermute x2, starting transfers between devices, pair_sum(): other = lax.ppermute(own, 'tp', [(0, 1), (1, 0)])  3.84 us
    dot_general x1, matrix products, shards(): jnp.dot(tokens, w_query, preferred_element_type=jnp.float32)  3.16 us
    reduce_sum x2, other arithmetic, normalize(): center = rows - jnp.mean(rows, axis=-1, keepdims=True)  2.5 us
  transfers between devices with their start and end apart: 2, of which 2 were waited for; matrix products, arithmetic and copies ran while one was open for 0% of the time, Pallas kernels for 0%

profile of v7, /device:TPU:1, one launch (start us, length us, event | category | flops | bytes accessed | tf_op | source)
XLA Modules:
  0.0 106.0 jit_solution(12155752788709174087)
XLA Ops:
  0.6 0.0 copy-start
  0.6 0.0 copy-start.1
  1.5 0.0 copy-start.8
  1.5 3.2 %convolution_convert_fusion.4.q_ref = bf16[512,512]{1,0:T(8,128)(2,1)} fusion(bf16[512,1024]{1,0:T(8,128)(2,1)} %param.14, bf16[1024,512]{1,0:T(8,128)(2,1)} %param.19), kind=kOutput, calls=%fused_computation.29 | convolution fusion | flops 537133056 | bytes 2621440 | tf_op jit(solution)/shard_map/dot_general | solution.py:113
  4.6 0.0 copy-done.1
  4.6 0.0 copy-done.8
  4.6 0.0 copy-start.9
  4.6 1.5 %convolution_convert_fusion.3.kn_ref = bf16[512,512]{1,0:T(8,128)(2,1)} fusion(bf16[512,1024]{1,0:T(8,128)(2,1)S(1)} %copy-done.1, bf16[1024,512]{1,0:T(8,128)(2,1)S(1)} %copy-done.8), kind=kOutput, calls=%fused_computation.28 | convolution fusion | flops 537133056 | bytes 2621440 | tf_op jit(solution)/shard_map/dot_general | solution.py:114
  6.1 0.0 copy-done.9
  6.1 0.0 copy-start.11
  6.1 1.5 %convolution_convert_fusion.2.vn_ref = bf16[512,512]{1,0:T(8,128)(2,1)} fusion(bf16[512,1024]{1,0:T(8,128)(2,1)S(1)} %copy-done.1, bf16[1024,512]{1,0:T(8,128)(2,1)S(1)} %copy-done.9), kind=kOutput, calls=%fused_computation.27 | convolution fusion | flops 537133056 | bytes 2621440 | tf_op jit(solution)/shard_map/dot_general | solution.py:115
  7.7 0.0 copy-done.11
  7.7 0.6 dynamic_slice.9
  8.2 1.2 %pad_add_fusion.lens_ref = s32[2]{0:T(128)} fusion(s32[1]{0:T(128)S(6)} %copy.23, s32[1]{0:T(128)} %dynamic_slice.9), kind=kLoop, calls=%fused_computation.70 | loop fusion | flops 2 | bytes 16 | tf_op jit(solution)/shard_map/stack | solution.py:116
  9.5 15.5 %shard_map.157 = bf16[512,512]{1,0:T(8,128)(2,1)} custom-call(s32[2]{0:T(128)} %pad_add_fusion.lens_ref, bf16[512,512]{1,0:T(8,128)(2,1)} %convolution_convert_fusion.4.q_ref, bf16[1024,512]{1,0:T(8,128)(2,1)} %bitcast.30, bf16[1024,512]{1,0:T(8,128)(2,1)} %bitcast.31, bf16[512,512]{1,0:T(8,128)(2,1)} %convolution_convert_fusion.3.kn_ref, ...), custom_call_target="tpu_custom_call" | custom-call | flops 3221225472 | bytes 4194304 | tf_op jit(solution)/shard_map/pallas_call | solution.py:69
  25.0 0.0 copy-start.5
  25.0 0.0 copy-start.6
  25.0 2.1 %convolution_convert_fusion.1 = bf16[512,1024]{1,0:T(8,128)(2,1)S(1)} fusion(bf16[512,512]{1,0:T(8,128)(2,1)} %shard_map.157, bf16[512,1024]{1,0:T(8,128)(2,1)} %param.22), kind=kOutput, calls=%fused_computation.26 | convolution fusion | flops 537395200 | bytes 2621440 | tf_op jit(solution)/shard_map/dot_general | solution.py:118
  27.1 3.5 %collective-permute-start = (bf16[512,1024]{1,0:T(8,128)(2,1)S(1)}, bf16[512,1024]{1,0:T(8,128)(2,1)S(1)}, u32[]{:S(2)}, u32[]{:S(2)}) collective-permute-start(bf16[512,1024]{1,0:T(8,128)(2,1)S(1)} %convolution_convert_fusion.1), channel_id=1, source_target_pairs={{0,1},{1,0},{2,3},{3,2},{4,5},{5,4},{6,7},{7,6},{8,9},{9,8},{10,11... | collective-permute-start | bytes 3145736 | tf_op jit(solution)/shard_map/ppermute | solution.py:19
  30.5 0.0 copy-done.5
  30.6 0.0 copy-done.6
  30.6 2.2 %collective-permute-done = bf16[512,1024]{1,0:T(8,128)(2,1)S(1)} collective-permute-done((bf16[512,1024]{1,0:T(8,128)(2,1)S(1)}, bf16[512,1024]{1,0:T(8,128)(2,1)S(1)}, u32[]{:S(2)}, u32[]{:S(2)}) %collective-permute-start) | collective-permute-done | bytes 1048608 | tf_op jit(solution)/shard_map/ppermute | solution.py:19
  32.8 0.5 fusion.41
  33.3 0.0 copy-start.2
  33.3 0.6 multiply_reduce_fusion.1
  34.0 0.6 copy-done.2
  34.5 0.7 add_convert_fusion.1
  35.2 0.0 copy-done
  35.2 8.8 %convolution_convert_fusion = bf16[512,1024]{1,0:T(8,128)(2,1)} fusion(bf16[1024,1024]{1,0:T(8,128)(2,1)S(1)} %copy-done, bf16[512,1024]{1,0:T(8,128)(2,1)S(1)} %add_convert_fusion.1, bf16[1024,1024]{1,0:T(8,128)(2,1)} %param.23), kind=kOutput, calls=%fused_computation.25 | convolution fusion | flops 2182086656 | bytes 6291456 | tf_op jit(solution)/shard_map/dot_general | solution.py:125
  44.0 0.4 collective-permute-start.1
  44.4 0.0 copy-start.3
  44.4 2.6 %collective-permute-done.1 = bf16[512,1024]{1,0:T(8,128)(2,1)} collective-permute-done((bf16[512,1024]{1,0:T(8,128)(2,1)}, bf16[512,1024]{1,0:T(8,128)(2,1)}, u32[]{:S(2)}, u32[]{:S(2)}) %collective-permute-start.1) | collective-permute-done | bytes 1048608 | tf_op jit(solution)/shard_map/ppermute | solution.py:19
  47.0 2.0 %fusion.42 = f32[512]{0:T(512)S(1)} fusion(bf16[512,1024]{1,0:T(8,128)(2,1)} %collective-permute-done.1, bf16[512,1024]{1,0:T(8,128)(2,1)} %convolution_convert_fusion, bf16[512,1024]{1,0:T(8,128)(2,1)S(1)} %add_convert_fusion.1), kind=kLoop, calls=%fused_computation.62 | loop fusion | flops 3145216 | bytes 3147776 | tf_op jit(solution)/shard_map/reduce_sum | solution.py:12
  49.1 0.0 copy-done.3
  49.1 1.8 %multiply_reduce_fusion = f32[512]{0:T(512)S(1)} fusion(f32[512]{0:T(512)S(1)} %broadcast_multiply_fusion, bf16[512,1024]{1,0:T(8,128)(2,1)} %collective-permute-done.1, bf16[512,1024]{1,0:T(8,128)(2,1)S(1)} %copy-done.3, bf16[512,1024]{1,0:T(8,128)(2,1)S(1)} %add_convert_fusion.1), kind=kLoop, calls=%fused_computation.5 | loop fusion | flops 4193792 | bytes 3149824 | tf_op jit(solution)/shard_map/reduce_sum | solution.py:13
  50.9 1.9 %add_convert_fusion = bf16[512,1024]{1,0:T(8,128)(2,1)S(1)} fusion(f32[1024]{0:T(1024)S(1)} %bitcast.25, f32[1024]{0:T(1024)S(1)} %bitcast.26, f32[512]{0:T(512)S(1)} %add_rsqrt_fusion, f32[512]{0:T(512)S(1)} %broadcast_multiply_fusion, bf16[512,1024]{1,0:T(8,128)(2,1)} %collective-permute-done.1, bf16[512,1024]{1,0:T(8,128)(2,1)S(1)} %copy-done.3, ...), kind=kLoop, calls=%fused_computation.4 | loop fusion | flops 5242880 | bytes 4206592 | tf_op jit(solution)/shard_map/convert_element_type | solution.py:126
  52.8 0.0 copy-start.4
  52.9 1.0 copy-done.4
  53.8 0.0 copy-start.10
  53.8 0.3 broadcast_in_dim.6
  54.1 0.5 broadcast.61
  54.6 2.1 %reduce.4 = bf16[128,1024]{1,0:T(8,128)(2,1)S(1)} reduce(bf16[128,1,1024]{2,1,0:T(2,128)(2,1)S(1)} %broadcast_in_dim.6, bf16[]{:T(256)} %broadcast.61), dimensions={1}, to_apply=%broadcast_in_dim.6.reduce_sub_computation | reduce | bytes 524290 | tf_op jit(solution)/shard_map/broadcast_in_dim | solution.py:132
  56.8 0.2 reshape.45
  57.0 27.7 %all_to_all.19 = bf16[128,2,512]{2,1,0:T(2,128)(2,1)S(1)} all-to-all(bf16[128,2,512]{2,1,0:T(2,128)(2,1)S(1)} %reshape.45), channel_id=1, replica_groups=mesh['req'=128,'tp'=2] {'req'}, dimensions={0} | all-to-all | bytes 524288 | tf_op jit(solution)/shard_map/all_to_all | solution.py:131
  84.7 0.2 reshape.46
  84.9 0.0 copy-done.10
  84.9 0.3 convolution_reduce_fusion
  85.2 0.0 copy-start.7
  85.3 0.1 broadcast_in_dim.7
  85.3 0.2 all_to_all.16
  85.5 19.7 %all_to_all.20 = f32[256,1,1]{2,1,0:T(1,128)S(1)} all-to-all(f32[256,1,1]{2,1,0:T(1,128)S(1)} %all_to_all.16), channel_id=1, replica_groups=mesh['req'=128,'tp'=2] {'req','tp'}, dimensions={0} | all-to-all | bytes 2048 | tf_op jit(solution)/shard_map/all_to_all | solution.py:137
  105.2 0.9 reduce_max.21
  106.0 0.0 copy-done.7
  (7 shorter events, 0.1 us)
Async XLA Ops:
  0.6 34.6 %copy-start = (bf16[1024,1024]{1,0:T(8,128)(2,1)S(1)}, bf16[1024,1024]{1,0:T(8,128)(2,1)}, u32[]{:S(2)}) copy-start(bf16[1024,1024]{1,0:T(8,128)(2,1)} %param.24) | copy-start | bytes 6291460
  0.6 4.0 %copy-start.1 = (bf16[512,1024]{1,0:T(8,128)(2,1)S(1)}, bf16[512,1024]{1,0:T(8,128)(2,1)}, u32[]{:S(2)}) copy-start(bf16[512,1024]{1,0:T(8,128)(2,1)} %param.14) | copy-start | bytes 3145732
  1.5 3.2 %copy-start.8 = (bf16[1024,512]{1,0:T(8,128)(2,1)S(1)}, bf16[1024,512]{1,0:T(8,128)(2,1)}, u32[]{:S(2)}) copy-start(bf16[1024,512]{1,0:T(8,128)(2,1)} %param.20) | copy-start | bytes 3145732
  4.6 1.5 %copy-start.9 = (bf16[1024,512]{1,0:T(8,128)(2,1)S(1)}, bf16[1024,512]{1,0:T(8,128)(2,1)}, u32[]{:S(2)}) copy-start(bf16[1024,512]{1,0:T(8,128)(2,1)} %param.21) | copy-start | bytes 3145732
  6.1 1.5 %copy-start.11 = (s32[128]{0:T(128)S(1)}, s32[128]{0:T(128)}, u32[]{:S(2)}) copy-start(s32[128]{0:T(128)} %param.16) | copy-start | bytes 1540
  25.0 5.6 %copy-start.5 = (f32[2,1024]{1,0:T(2,128)S(1)}, f32[2,1024]{1,0:T(2,128)}, u32[]{:S(2)}) copy-start(f32[2,1024]{1,0:T(2,128)} %param.26) | copy-start | bytes 24580
  25.0 5.6 %copy-start.6 = (f32[2,1024]{1,0:T(2,128)S(1)}, f32[2,1024]{1,0:T(2,128)}, u32[]{:S(2)}) copy-start(f32[2,1024]{1,0:T(2,128)} %param.25) | copy-start | bytes 24580
  27.1 5.7 %collective-permute-start = (bf16[512,1024]{1,0:T(8,128)(2,1)S(1)}, bf16[512,1024]{1,0:T(8,128)(2,1)S(1)}, u32[]{:S(2)}, u32[]{:S(2)}) collective-permute-start(bf16[512,1024]{1,0:T(8,128)(2,1)S(1)} %convolution_convert_fusion.1), channel_id=1, source_target_pairs={{0,1},{1,0},{2,3},{3,2},{4,5},{5,4},{6,7},{7,6},{8,9},{9,8},{10,11... | collective-permute-start | bytes 3145736 | tf_op jit(solution)/shard_map/ppermute | solution.py:19
  33.3 1.2 %copy-start.2 = (bf16[512,1024]{1,0:T(8,128)(2,1)S(1)}, bf16[512,1024]{1,0:T(8,128)(2,1)}, u32[]{:S(2)}) copy-start(bf16[512,1024]{1,0:T(8,128)(2,1)} %param.14) | copy-start | bytes 3145732
  44.0 3.0 %collective-permute-start.1 = (bf16[512,1024]{1,0:T(8,128)(2,1)}, bf16[512,1024]{1,0:T(8,128)(2,1)}, u32[]{:S(2)}, u32[]{:S(2)}) collective-permute-start(bf16[512,1024]{1,0:T(8,128)(2,1)} %convolution_convert_fusion), channel_id=1, source_target_pairs={{0,1},{1,0},{2,3},{3,2},{4,5},{5,4},{6,7},{7,6},{8,9},{9,8},{10,11... | collective-permute-start | bytes 3145736 | tf_op jit(solution)/shard_map/ppermute | solution.py:19
  44.4 4.7 %copy-start.3 = (bf16[512,1024]{1,0:T(8,128)(2,1)S(1)}, bf16[512,1024]{1,0:T(8,128)(2,1)}, u32[]{:S(2)}) copy-start(bf16[512,1024]{1,0:T(8,128)(2,1)} %convolution_convert_fusion) | copy-start | bytes 3145732
  52.8 1.0 copy-start.4
  53.8 31.1 %copy-start.10 = (bf16[192,1024]{1,0:T(8,128)(2,1)S(1)}, bf16[192,1024]{1,0:T(8,128)(2,1)}, u32[]{:S(2)}) copy-start(bf16[192,1024]{1,0:T(8,128)(2,1)} %param.27) | copy-start | bytes 1179652
  85.2 20.8 %copy-start.7 = (f32[128]{0:T(128)}, f32[128]{0:T(128)S(1)}, u32[]{:S(2)}) copy-start(f32[128]{0:T(128)S(1)} %convolution_reduce_fusion) | copy-start | bytes 1540

commit v8 on v7

v8 whole, which is shorter than its diff:
```python
import jax
import jax.numpy as jnp
from jax import lax
from jax.experimental import pallas as pl
from jax.experimental.pallas import tpu as pltpu
from jax.sharding import PartitionSpec as P

HD = 64


def normalize(rows, gain, bias):
    center = rows - jnp.mean(rows, axis=-1, keepdims=True)
    spread = jnp.mean(center * center, axis=-1, keepdims=True)
    return center * lax.rsqrt(spread + 1e-05) * gain + bias


def pair_sum(partial):
    own = partial.astype(jnp.bfloat16)
    other = lax.ppermute(own, "tp", [(0, 1), (1, 0)])
    return own.astype(jnp.float32) + other.astype(jnp.float32)


PAIR = 2 * HD
ROWS = 256


def attention_kernel(lens_ref, x_ref, wq_ref, wk_ref, wv_ref, kc_ref, vc_ref, out_ref):
    cached = lens_ref[0]
    valid = lens_ref[1]
    x = x_ref[...]
    q_all = jnp.dot(x, wq_ref[...], preferred_element_type=jnp.float32).astype(jnp.bfloat16)
    kn = jnp.dot(x, wk_ref[...], preferred_element_type=jnp.float32).astype(jnp.bfloat16)
    vn = jnp.dot(x, wv_ref[...], preferred_element_type=jnp.float32).astype(jnp.bfloat16)
    kc = kc_ref[...]
    vc = vc_ref[...]
    scale = 1.0 / float(HD) ** 0.5
    dims = (((1,), (1,)), ((), ()))
    for chunk in range(x.shape[0] // ROWS):
        row0 = chunk * ROWS
        q = q_all[row0 : row0 + ROWS]
        lanes = lax.broadcasted_iota(jnp.int32, q.shape, 1)
        cache_cols = lax.broadcasted_iota(jnp.int32, (ROWS, kc.shape[0]), 1)
        cache_ok = cache_cols < cached
        new_cols = lax.broadcasted_iota(jnp.int32, (ROWS, kn.shape[0]), 1)
        new_rows = lax.broadcasted_iota(jnp.int32, (ROWS, kn.shape[0]), 0) + row0
        new_ok = (new_cols <= new_rows) & (new_cols < valid)
        result = jnp.zeros(q.shape, jnp.float32)
        for head in range(2):
            mine = (lanes // HD) == head
            qh = jnp.where(mine, q, jnp.zeros_like(q))
            s_c = lax.dot_general(qh, kc, dims, preferred_element_type=jnp.float32) * scale
            s_n = lax.dot_general(qh, kn, dims, preferred_element_type=jnp.float32) * scale
            s_c = jnp.where(cache_ok, s_c, -jnp.inf)
            s_n = jnp.where(new_ok, s_n, -jnp.inf)
            peak = jnp.maximum(
                jnp.max(s_c, axis=1, keepdims=True), jnp.max(s_n, axis=1, keepdims=True)
            )
            e_c = jnp.exp(s_c - peak)
            e_n = jnp.exp(s_n - peak)
            total = jnp.sum(e_c, axis=1, keepdims=True) + jnp.sum(e_n, axis=1, keepdims=True)
            mixed = jnp.dot(
                e_c.astype(jnp.bfloat16), vc, preferred_element_type=jnp.float32
            ) + jnp.dot(e_n.astype(jnp.bfloat16), vn, preferred_element_type=jnp.float32)
            result = jnp.where(mine, mixed / total, result)
        out_ref[row0 : row0 + ROWS, :] = result.astype(out_ref.dtype)


def attention(lens, tokens, w_query, w_key, w_value, cache_k, cache_v):
    rows, model = tokens.shape
    width = w_query.shape[1]
    cache_rows = cache_k.shape[0]
    pairs = width // PAIR
    flops = 4 * rows * (cache_rows + rows) * width * 2 + 6 * rows * model * width
    return pl.pallas_call(
        attention_kernel,
        out_shape=jax.ShapeDtypeStruct((rows, width), jnp.bfloat16),
        grid_spec=pltpu.PrefetchScalarGridSpec(
            num_scalar_prefetch=1,
            grid=(pairs,),
            in_specs=[
                pl.BlockSpec((rows, model), lambda p, lens: (0, 0)),
                pl.BlockSpec((model, PAIR), lambda p, lens: (0, p)),
                pl.BlockSpec((model, PAIR), lambda p, lens: (0, p)),
                pl.BlockSpec((model, PAIR), lambda p, lens: (0, p)),
                pl.BlockSpec((cache_rows, PAIR), lambda p, lens: (0, p)),
                pl.BlockSpec((cache_rows, PAIR), lambda p, lens: (0, p)),
            ],
            out_specs=pl.BlockSpec((rows, PAIR), lambda p, lens: (0, p)),
        ),
        cost_estimate=pl.CostEstimate(
            flops=flops,
            transcendentals=rows * (cache_rows + rows) * width // HD,
            bytes_accessed=2 * (rows * model + 3 * model * width + 2 * cache_rows * width + rows * width),
        ),
    )(lens, tokens, w_query, w_key, w_value, cache_k, cache_v)


def shards(
    tokens,
    group_len,
    cache_len,
    cache_keys,
    cache_values,
    w_query,
    w_key,
    w_value,
    w_out,
    w_up,
    w_down,
    ln_gains,
    ln_biases,
    embed,
):
    block_rows = tokens.shape[0]
    local_width = w_query.shape[1]
    my_index = lax.axis_index("req")
    my_cache = lax.dynamic_index_in_dim(cache_len, my_index, 0, keepdims=False)
    my_valid = group_len[0]
    lens = jnp.stack([my_cache, my_valid]).astype(jnp.int32)
    attn_mixed = attention(lens, tokens, w_query, w_key, w_value, cache_keys[0], cache_values[0])
    attn_sum = pair_sum(jnp.dot(attn_mixed, w_out, preferred_element_type=jnp.float32))
    middle = normalize(tokens.astype(jnp.float32) + attn_sum, ln_gains[0], ln_biases[0]).astype(
        jnp.bfloat16
    )
    active = jax.nn.gelu(
        jnp.dot(middle, w_up, preferred_element_type=jnp.float32), approximate=False
    ).astype(jnp.bfloat16)
    ffn_sum = pair_sum(jnp.dot(active, w_down, preferred_element_type=jnp.float32))
    layer_out = normalize(middle.astype(jnp.float32) + ffn_sum, ln_gains[1], ln_biases[1]).astype(
        jnp.bfloat16
    )
    last_row = lax.dynamic_slice_in_dim(layer_out, my_valid - 1, 1, 0)
    reqs = cache_len.shape[0]
    all_rows = lax.all_to_all(
        jnp.broadcast_to(last_row, (reqs, last_row.shape[1])), "req", 0, 0, tiled=True
    )
    logits = jnp.einsum("rd,vd->rv", all_rows, embed, preferred_element_type=jnp.float32)
    slice_best = jnp.max(logits, axis=1)
    spread = jnp.repeat(slice_best, 2)[:, None]
    best_logit = jnp.max(lax.all_to_all(spread, ("req", "tp"), 0, 0, tiled=True), axis=0)
    return (layer_out, best_logit, slice_best[:, None])


def solution(mesh):
    placed = (
        P("req", None),
        P("req"),
        P(),
        P("req", None, "tp"),
        P("req", None, "tp"),
        P(None, "tp"),
        P(None, "tp"),
        P(None, "tp"),
        P("tp", None),
        P(None, "tp"),
        P("tp", None),
        P(),
        P(),
        P(("req", "tp"), None),
    )
    return jax.shard_map(
        shards,
        mesh=mesh,
        in_specs=placed,
        out_specs=(P("req", None), P("req"), P(None, ("req", "tp"))),
        check_vma=False,
    )
```

time: 106 us -> 102 us (0.962)
  matrix products: 17.4 us -> 11 us
  Pallas kernels: 15.5 us -> 17.6 us
    dot_general x3 -> x0, matrix products: 6.18 us -> none  [the longest x1 3.16 us: shards(): jnp.dot(tokens, w_query, preferred_element_type=jnp.float32)]
    pallas_call x1, Pallas kernels: 15.5 us -> 17.6 us  [attention(): pl.pallas_call(attention_kernel, out_shape=jax.ShapeDtypeStruct((rows, wi...]
where the time goes in v8:
time: 102 us
  blocking collectives  47.4 us (46%)
  Pallas kernels  17.6 us (17%)
  other arithmetic  11.8 us (12%)
  matrix products  11 us (11%)
  waiting for transfers between devices  4.88 us (5%)
  starting transfers between devices  3.83 us (4%)
  local copies, waits for them, and re-layouts  3.71 us (4%)
  between operations  1.58 us (2%)
    all_to_all x1, blocking collectives, shards(): lax.all_to_all(jnp.broadcast_to(last_row, (reqs, last_row.shape[1])), 're...  27.7 us
    all_to_all x1, blocking collectives, shards(): lax.all_to_all(spread, ('req', 'tp'), 0, 0, tiled=True)  19.7 us
    pallas_call x1, Pallas kernels, attention(): pl.pallas_call(attention_kernel, out_shape=jax.ShapeDtypeStruct((rows, wi...  17.6 us
    dot_general x1, matrix products, shards(): jnp.dot(active, w_down, preferred_element_type=jnp.float32)  8.82 us
    ppermute x2, waiting for transfers between devices, pair_sum(): other = lax.ppermute(own, 'tp', [(0, 1), (1, 0)])  4.88 us
    ppermute x2, starting transfers between devices, pair_sum(): other = lax.ppermute(own, 'tp', [(0, 1), (1, 0)])  3.83 us
    reduce_sum x2, other arithmetic, normalize(): center = rows - jnp.mean(rows, axis=-1, keepdims=True)  2.51 us
    reduce_sum x2, other arithmetic, normalize(): spread = jnp.mean(center * center, axis=-1, keepdims=True)  2.47 us
  transfers between devices with their start and end apart: 2, of which 2 were waited for; matrix products, arithmetic and copies ran while one was open for 0% of the time, Pallas kernels for 0%

profile of v8, /device:TPU:1, one launch (start us, length us, event | category | flops | bytes accessed | tf_op | source)
XLA Modules:
  0.0 101.8 jit_solution(2755451592220680777)
XLA Ops:
  0.6 0.0 copy-start
  1.4 1.2 %dynamic_slice.9 = s32[1]{0:T(128)} dynamic-slice(s32[128]{0:T(128)} %param.16, s32[]{:T(128)S(6)} %select_n.7), dynamic_slice_sizes={1} | dynamic-slice | bytes 12 | tf_op jit(solution)/shard_map/jit(dynamic_index_in_dim)/dynamic_slice | solution.py:117
  2.7 1.2 %pad_add_fusion.lens_ref = s32[2]{0:T(128)} fusion(s32[1]{0:T(128)S(6)} %copy.23, s32[1]{0:T(128)} %dynamic_slice.9), kind=kLoop, calls=%fused_computation.67 | loop fusion | flops 2 | bytes 16 | tf_op jit(solution)/shard_map/stack | solution.py:119
  3.9 0.0 copy-start.7
  3.9 17.6 %shard_map.157 = bf16[512,512]{1,0:T(8,128)(2,1)} custom-call(s32[2]{0:T(128)} %pad_add_fusion.lens_ref, bf16[512,1024]{1,0:T(8,128)(2,1)} %x_ref.1, bf16[1024,512]{1,0:T(8,128)(2,1)} %wq_ref.1, bf16[1024,512]{1,0:T(8,128)(2,1)} %wk_ref.1, bf16[1024,512]{1,0:T(8,128)(2,1)} %wv_ref.1, bf16[1024,512]{1,0:T(8,128)(2,1)} %bitcast.24, bf16[1024,512]{1,0:T(8,128)(2,1)} %bitcast.25), custom_call_target="tpu_custom_call" | custom-call | flops 4831838208 | bytes 6815744 | tf_op jit(solution)/shard_map/pallas_call | solution.py:74
  21.5 0.0 copy-done.7
  21.5 0.0 copy-start.4
  21.6 0.0 copy-start.5
  21.6 0.0 copy-start.1
  21.6 1.8 %convolution_convert_fusion.1 = bf16[512,1024]{1,0:T(8,128)(2,1)S(1)} fusion(bf16[512,512]{1,0:T(8,128)(2,1)} %shard_map.157, bf16[512,1024]{1,0:T(8,128)(2,1)S(1)} %copy-done.7), kind=kOutput, calls=%fused_computation.26 | convolution fusion | flops 537395200 | bytes 2621440 | tf_op jit(solution)/shard_map/dot_general | solution.py:121
  23.4 3.5 %collective-permute-start = (bf16[512,1024]{1,0:T(8,128)(2,1)S(1)}, bf16[512,1024]{1,0:T(8,128)(2,1)S(1)}, u32[]{:S(2)}, u32[]{:S(2)}) collective-permute-start(bf16[512,1024]{1,0:T(8,128)(2,1)S(1)} %convolution_convert_fusion.1), channel_id=1, source_target_pairs={{0,1},{1,0},{2,3},{3,2},{4,5},{5,4},{6,7},{7,6},{8,9},{9,8},{10,11... | collective-permute-start | bytes 3145736 | tf_op jit(solution)/shard_map/ppermute | solution.py:19
  26.9 0.0 copy-done.4
  26.9 0.0 copy-done.5
  26.9 2.2 %collective-permute-done = bf16[512,1024]{1,0:T(8,128)(2,1)S(1)} collective-permute-done((bf16[512,1024]{1,0:T(8,128)(2,1)S(1)}, bf16[512,1024]{1,0:T(8,128)(2,1)S(1)}, u32[]{:S(2)}, u32[]{:S(2)}) %collective-permute-start) | collective-permute-done | bytes 1048608 | tf_op jit(solution)/shard_map/ppermute | solution.py:19
  29.2 0.0 copy-done.1
  29.2 0.5 fusion.41
  29.7 0.6 multiply_reduce_fusion.1
  30.3 0.7 add_convert_fusion.1
  31.0 0.0 copy-done
  31.0 8.8 %convolution_convert_fusion = bf16[512,1024]{1,0:T(8,128)(2,1)} fusion(bf16[1024,1024]{1,0:T(8,128)(2,1)S(1)} %copy-done, bf16[512,1024]{1,0:T(8,128)(2,1)S(1)} %add_convert_fusion.1, bf16[1024,1024]{1,0:T(8,128)(2,1)} %param.23), kind=kOutput, calls=%fused_computation.25 | convolution fusion | flops 2182086656 | bytes 6291456 | tf_op jit(solution)/shard_map/dot_general | solution.py:128
  39.8 0.4 collective-permute-start.1
  40.2 0.0 copy-start.2
  40.2 2.6 %collective-permute-done.1 = bf16[512,1024]{1,0:T(8,128)(2,1)} collective-permute-done((bf16[512,1024]{1,0:T(8,128)(2,1)}, bf16[512,1024]{1,0:T(8,128)(2,1)}, u32[]{:S(2)}, u32[]{:S(2)}) %collective-permute-start.1) | collective-permute-done | bytes 1048608 | tf_op jit(solution)/shard_map/ppermute | solution.py:19
  42.8 2.0 %fusion.42 = f32[512]{0:T(512)S(1)} fusion(bf16[512,1024]{1,0:T(8,128)(2,1)} %collective-permute-done.1, bf16[512,1024]{1,0:T(8,128)(2,1)} %convolution_convert_fusion, bf16[512,1024]{1,0:T(8,128)(2,1)S(1)} %add_convert_fusion.1), kind=kLoop, calls=%fused_computation.59 | loop fusion | flops 3145216 | bytes 3147776 | tf_op jit(solution)/shard_map/reduce_sum | solution.py:12
  44.9 0.0 copy-done.2
  44.9 1.8 %multiply_reduce_fusion = f32[512]{0:T(512)S(1)} fusion(f32[512]{0:T(512)S(1)} %broadcast_multiply_fusion, bf16[512,1024]{1,0:T(8,128)(2,1)} %collective-permute-done.1, bf16[512,1024]{1,0:T(8,128)(2,1)S(1)} %copy-done.2, bf16[512,1024]{1,0:T(8,128)(2,1)S(1)} %add_convert_fusion.1), kind=kLoop, calls=%fused_computation.5 | loop fusion | flops 4193792 | bytes 3149824 | tf_op jit(solution)/shard_map/reduce_sum | solution.py:13
  46.7 1.9 %add_convert_fusion = bf16[512,1024]{1,0:T(8,128)(2,1)S(1)} fusion(f32[1024]{0:T(1024)S(1)} %bitcast.19, f32[1024]{0:T(1024)S(1)} %bitcast.20, f32[512]{0:T(512)S(1)} %add_rsqrt_fusion, f32[512]{0:T(512)S(1)} %broadcast_multiply_fusion, bf16[512,1024]{1,0:T(8,128)(2,1)} %collective-permute-done.1, bf16[512,1024]{1,0:T(8,128)(2,1)S(1)} %copy-done.2, ...), kind=kLoop, calls=%fused_computation.4 | loop fusion | flops 5242880 | bytes 4206592 | tf_op jit(solution)/shard_map/convert_element_type | solution.py:129
  48.6 0.0 copy-start.3
  48.6 1.0 copy-done.3
  49.6 0.0 copy-start.8
  49.6 0.3 broadcast_in_dim.6
  49.9 0.5 broadcast.61
  50.4 2.1 %reduce.4 = bf16[128,1024]{1,0:T(8,128)(2,1)S(1)} reduce(bf16[128,1,1024]{2,1,0:T(2,128)(2,1)S(1)} %broadcast_in_dim.6, bf16[]{:T(256)} %broadcast.61), dimensions={1}, to_apply=%broadcast_in_dim.6.reduce_sub_computation | reduce | bytes 524290 | tf_op jit(solution)/shard_map/broadcast_in_dim | solution.py:135
  52.6 0.2 reshape.45
  52.8 27.7 %all_to_all.19 = bf16[128,2,512]{2,1,0:T(2,128)(2,1)S(1)} all-to-all(bf16[128,2,512]{2,1,0:T(2,128)(2,1)S(1)} %reshape.45), channel_id=1, replica_groups=mesh['req'=128,'tp'=2] {'req'}, dimensions={0} | all-to-all | bytes 524288 | tf_op jit(solution)/shard_map/all_to_all | solution.py:134
  80.5 0.2 reshape.46
  80.7 0.0 copy-done.8
  80.7 0.3 convolution_reduce_fusion
  81.0 0.0 copy-start.6
  81.0 0.1 broadcast_in_dim.7
  81.1 0.2 all_to_all.16
  81.3 19.7 %all_to_all.20 = f32[256,1,1]{2,1,0:T(1,128)S(1)} all-to-all(f32[256,1,1]{2,1,0:T(1,128)S(1)} %all_to_all.16), channel_id=1, replica_groups=mesh['req'=128,'tp'=2] {'req','tp'}, dimensions={0} | all-to-all | bytes 2048 | tf_op jit(solution)/shard_map/all_to_all | solution.py:140
  100.9 0.9 reduce_max.21
  101.8 0.0 copy-done.6
  (7 shorter events, 0.1 us)
Async XLA Ops:
  0.6 30.4 %copy-start = (bf16[1024,1024]{1,0:T(8,128)(2,1)S(1)}, bf16[1024,1024]{1,0:T(8,128)(2,1)}, u32[]{:S(2)}) copy-start(bf16[1024,1024]{1,0:T(8,128)(2,1)} %param.24) | copy-start | bytes 6291460
  3.9 17.6 %copy-start.7 = (bf16[512,1024]{1,0:T(8,128)(2,1)S(1)}, bf16[512,1024]{1,0:T(8,128)(2,1)}, u32[]{:S(2)}) copy-start(bf16[512,1024]{1,0:T(8,128)(2,1)} %param.22) | copy-start | bytes 3145732
  21.5 5.4 %copy-start.4 = (f32[2,1024]{1,0:T(2,128)S(1)}, f32[2,1024]{1,0:T(2,128)}, u32[]{:S(2)}) copy-start(f32[2,1024]{1,0:T(2,128)} %param.26) | copy-start | bytes 24580
  21.6 5.4 %copy-start.5 = (f32[2,1024]{1,0:T(2,128)S(1)}, f32[2,1024]{1,0:T(2,128)}, u32[]{:S(2)}) copy-start(f32[2,1024]{1,0:T(2,128)} %param.25) | copy-start | bytes 24580
  21.6 7.6 %copy-start.1 = (bf16[512,1024]{1,0:T(8,128)(2,1)S(1)}, bf16[512,1024]{1,0:T(8,128)(2,1)}, u32[]{:S(2)}) copy-start(bf16[512,1024]{1,0:T(8,128)(2,1)} %x_ref.1) | copy-start | bytes 3145732
  23.4 5.8 %collective-permute-start = (bf16[512,1024]{1,0:T(8,128)(2,1)S(1)}, bf16[512,1024]{1,0:T(8,128)(2,1)S(1)}, u32[]{:S(2)}, u32[]{:S(2)}) collective-permute-start(bf16[512,1024]{1,0:T(8,128)(2,1)S(1)} %convolution_convert_fusion.1), channel_id=1, source_target_pairs={{0,1},{1,0},{2,3},{3,2},{4,5},{5,4},{6,7},{7,6},{8,9},{9,8},{10,11... | collective-permute-start | bytes 3145736 | tf_op jit(solution)/shard_map/ppermute | solution.py:19
  39.8 3.0 %collective-permute-start.1 = (bf16[512,1024]{1,0:T(8,128)(2,1)}, bf16[512,1024]{1,0:T(8,128)(2,1)}, u32[]{:S(2)}, u32[]{:S(2)}) collective-permute-start(bf16[512,1024]{1,0:T(8,128)(2,1)} %convolution_convert_fusion), channel_id=1, source_target_pairs={{0,1},{1,0},{2,3},{3,2},{4,5},{5,4},{6,7},{7,6},{8,9},{9,8},{10,11... | collective-permute-start | bytes 3145736 | tf_op jit(solution)/shard_map/ppermute | solution.py:19
  40.2 4.7 %copy-start.2 = (bf16[512,1024]{1,0:T(8,128)(2,1)S(1)}, bf16[512,1024]{1,0:T(8,128)(2,1)}, u32[]{:S(2)}) copy-start(bf16[512,1024]{1,0:T(8,128)(2,1)} %convolution_convert_fusion) | copy-start | bytes 3145732
  48.6 1.0 copy-start.3
  49.6 31.1 %copy-start.8 = (bf16[192,1024]{1,0:T(8,128)(2,1)S(1)}, bf16[192,1024]{1,0:T(8,128)(2,1)}, u32[]{:S(2)}) copy-start(bf16[192,1024]{1,0:T(8,128)(2,1)} %param.27) | copy-start | bytes 1179652
  81.0 20.8 %copy-start.6 = (f32[128]{0:T(128)}, f32[128]{0:T(128)S(1)}, u32[]{:S(2)}) copy-start(f32[128]{0:T(128)S(1)} %convolution_reduce_fusion) | copy-start | bytes 1540

commit v9 on v8

--- a/solution.py
+++ b/solution.py
@@ -38,18 +38,21 @@
     for chunk in range(x.shape[0] // ROWS):
         row0 = chunk * ROWS
         q = q_all[row0 : row0 + ROWS]
+        reach = row0 + ROWS
+        kn_seen = kn[:reach]
+        vn_seen = vn[:reach]
         lanes = lax.broadcasted_iota(jnp.int32, q.shape, 1)
         cache_cols = lax.broadcasted_iota(jnp.int32, (ROWS, kc.shape[0]), 1)
         cache_ok = cache_cols < cached
-        new_cols = lax.broadcasted_iota(jnp.int32, (ROWS, kn.shape[0]), 1)
-        new_rows = lax.broadcasted_iota(jnp.int32, (ROWS, kn.shape[0]), 0) + row0
+        new_cols = lax.broadcasted_iota(jnp.int32, (ROWS, reach), 1)
+        new_rows = lax.broadcasted_iota(jnp.int32, (ROWS, reach), 0) + row0
         new_ok = (new_cols <= new_rows) & (new_cols < valid)
         result = jnp.zeros(q.shape, jnp.float32)
         for head in range(2):
             mine = (lanes // HD) == head
             qh = jnp.where(mine, q, jnp.zeros_like(q))
             s_c = lax.dot_general(qh, kc, dims, preferred_element_type=jnp.float32) * scale
-            s_n = lax.dot_general(qh, kn, dims, preferred_element_type=jnp.float32) * scale
+            s_n = lax.dot_general(qh, kn_seen, dims, preferred_element_type=jnp.float32) * scale
             s_c = jnp.where(cache_ok, s_c, -jnp.inf)
             s_n = jnp.where(new_ok, s_n, -jnp.inf)
             peak = jnp.maximum(
@@ -60,7 +63,7 @@
             total = jnp.sum(e_c, axis=1, keepdims=True) + jnp.sum(e_n, axis=1, keepdims=True)
             mixed = jnp.dot(
                 e_c.astype(jnp.bfloat16), vc, preferred_element_type=jnp.float32
-            ) + jnp.dot(e_n.astype(jnp.bfloat16), vn, preferred_element_type=jnp.float32)
+            ) + jnp.dot(e_n.astype(jnp.bfloat16), vn_seen, preferred_element_type=jnp.float32)
             result = jnp.where(mine, mixed / total, result)
         out_ref[row0 : row0 + ROWS, :] = result.astype(out_ref.dtype)
 

time: 102 us -> 102 us (level)
  no operation moved by 1% of the time
where the time goes in v9:
time: 102 us
  blocking collectives  47.4 us (46%)
  Pallas kernels  17.7 us (17%)
  other arithmetic  11.8 us (12%)
  matrix products  11 us (11%)
  waiting for transfers between devices  4.88 us (5%)
  starting transfers between devices  3.84 us (4%)
  local copies, waits for them, and re-layouts  3.71 us (4%)
  between operations  1.58 us (2%)
    all_to_all x1, blocking collectives, shards(): lax.all_to_all(jnp.broadcast_to(last_row, (reqs, last_row.shape[1])), 're...  27.7 us
    all_to_all x1, blocking collectives, shards(): lax.all_to_all(spread, ('req', 'tp'), 0, 0, tiled=True)  19.7 us
    pallas_call x1, Pallas kernels, attention(): pl.pallas_call(attention_kernel, out_shape=jax.ShapeDtypeStruct((rows, wi...  17.7 us
    dot_general x1, matrix products, shards(): jnp.dot(active, w_down, preferred_element_type=jnp.float32)  8.81 us
    ppermute x2, waiting for transfers between devices, pair_sum(): other = lax.ppermute(own, 'tp', [(0, 1), (1, 0)])  4.88 us
    ppermute x2, starting transfers between devices, pair_sum(): other = lax.ppermute(own, 'tp', [(0, 1), (1, 0)])  3.84 us
    reduce_sum x2, other arithmetic, normalize(): center = rows - jnp.mean(rows, axis=-1, keepdims=True)  2.51 us
    reduce_sum x2, other arithmetic, normalize(): spread = jnp.mean(center * center, axis=-1, keepdims=True)  2.47 us
  transfers between devices with their start and end apart: 2, of which 2 were waited for; matrix products, arithmetic and copies ran while one was open for 0% of the time, Pallas kernels for 0%

profile of v9, /device:TPU:1, one launch (start us, length us, event | category | flops | bytes accessed | tf_op | source)
XLA Modules:
  0.0 101.9 jit_solution(6605616053602141377)
XLA Ops:
  0.6 0.0 copy-start
  1.4 1.2 %dynamic_slice.9 = s32[1]{0:T(128)} dynamic-slice(s32[128]{0:T(128)} %param.16, s32[]{:T(128)S(6)} %select_n.7), dynamic_slice_sizes={1} | dynamic-slice | bytes 12 | tf_op jit(solution)/shard_map/jit(dynamic_index_in_dim)/dynamic_slice | solution.py:120
  2.7 1.2 %pad_add_fusion.lens_ref = s32[2]{0:T(128)} fusion(s32[1]{0:T(128)S(6)} %copy.23, s32[1]{0:T(128)} %dynamic_slice.9), kind=kLoop, calls=%fused_computation.67 | loop fusion | flops 2 | bytes 16 | tf_op jit(solution)/shard_map/stack | solution.py:122
  3.9 0.0 copy-start.7
  3.9 17.7 %shard_map.157 = bf16[512,512]{1,0:T(8,128)(2,1)} custom-call(s32[2]{0:T(128)} %pad_add_fusion.lens_ref, bf16[512,1024]{1,0:T(8,128)(2,1)} %x_ref.1, bf16[1024,512]{1,0:T(8,128)(2,1)} %wq_ref.1, bf16[1024,512]{1,0:T(8,128)(2,1)} %wk_ref.1, bf16[1024,512]{1,0:T(8,128)(2,1)} %wv_ref.1, bf16[1024,512]{1,0:T(8,128)(2,1)} %bitcast.24, bf16[1024,512]{1,0:T(8,128)(2,1)} %bitcast.25), custom_call_target="tpu_custom_call" | custom-call | flops 4831838208 | bytes 6815744 | tf_op jit(solution)/shard_map/pallas_call | solution.py:77
  21.6 0.0 copy-done.7
  21.6 0.0 copy-start.4
  21.6 0.0 copy-start.5
  21.6 0.0 copy-start.1
  21.6 1.8 %convolution_convert_fusion.1 = bf16[512,1024]{1,0:T(8,128)(2,1)S(1)} fusion(bf16[512,512]{1,0:T(8,128)(2,1)} %shard_map.157, bf16[512,1024]{1,0:T(8,128)(2,1)S(1)} %copy-done.7), kind=kOutput, calls=%fused_computation.26 | convolution fusion | flops 537395200 | bytes 2621440 | tf_op jit(solution)/shard_map/dot_general | solution.py:124
  23.5 3.5 %collective-permute-start = (bf16[512,1024]{1,0:T(8,128)(2,1)S(1)}, bf16[512,1024]{1,0:T(8,128)(2,1)S(1)}, u32[]{:S(2)}, u32[]{:S(2)}) collective-permute-start(bf16[512,1024]{1,0:T(8,128)(2,1)S(1)} %convolution_convert_fusion.1), channel_id=1, source_target_pairs={{0,1},{1,0},{2,3},{3,2},{4,5},{5,4},{6,7},{7,6},{8,9},{9,8},{10,11... | collective-permute-start | bytes 3145736 | tf_op jit(solution)/shard_map/ppermute | solution.py:19
  27.0 0.0 copy-done.4
  27.0 0.0 copy-done.5
  27.0 2.2 %collective-permute-done = bf16[512,1024]{1,0:T(8,128)(2,1)S(1)} collective-permute-done((bf16[512,1024]{1,0:T(8,128)(2,1)S(1)}, bf16[512,1024]{1,0:T(8,128)(2,1)S(1)}, u32[]{:S(2)}, u32[]{:S(2)}) %collective-permute-start) | collective-permute-done | bytes 1048608 | tf_op jit(solution)/shard_map/ppermute | solution.py:19
  29.2 0.0 copy-done.1
  29.2 0.5 fusion.41
  29.7 0.6 multiply_reduce_fusion.1
  30.4 0.7 add_convert_fusion.1
  31.0 0.0 copy-done
  31.1 8.8 %convolution_convert_fusion = bf16[512,1024]{1,0:T(8,128)(2,1)} fusion(bf16[1024,1024]{1,0:T(8,128)(2,1)S(1)} %copy-done, bf16[512,1024]{1,0:T(8,128)(2,1)S(1)} %add_convert_fusion.1, bf16[1024,1024]{1,0:T(8,128)(2,1)} %param.23), kind=kOutput, calls=%fused_computation.25 | convolution fusion | flops 2182086656 | bytes 6291456 | tf_op jit(solution)/shard_map/dot_general | solution.py:131
  39.9 0.4 collective-permute-start.1
  40.2 0.0 copy-start.2
  40.2 2.6 %collective-permute-done.1 = bf16[512,1024]{1,0:T(8,128)(2,1)} collective-permute-done((bf16[512,1024]{1,0:T(8,128)(2,1)}, bf16[512,1024]{1,0:T(8,128)(2,1)}, u32[]{:S(2)}, u32[]{:S(2)}) %collective-permute-start.1) | collective-permute-done | bytes 1048608 | tf_op jit(solution)/shard_map/ppermute | solution.py:19
  42.9 2.0 %fusion.42 = f32[512]{0:T(512)S(1)} fusion(bf16[512,1024]{1,0:T(8,128)(2,1)} %collective-permute-done.1, bf16[512,1024]{1,0:T(8,128)(2,1)} %convolution_convert_fusion, bf16[512,1024]{1,0:T(8,128)(2,1)S(1)} %add_convert_fusion.1), kind=kLoop, calls=%fused_computation.59 | loop fusion | flops 3145216 | bytes 3147776 | tf_op jit(solution)/shard_map/reduce_sum | solution.py:12
  44.9 0.0 copy-done.2
  44.9 1.8 %multiply_reduce_fusion = f32[512]{0:T(512)S(1)} fusion(f32[512]{0:T(512)S(1)} %broadcast_multiply_fusion, bf16[512,1024]{1,0:T(8,128)(2,1)} %collective-permute-done.1, bf16[512,1024]{1,0:T(8,128)(2,1)S(1)} %copy-done.2, bf16[512,1024]{1,0:T(8,128)(2,1)S(1)} %add_convert_fusion.1), kind=kLoop, calls=%fused_computation.5 | loop fusion | flops 4193792 | bytes 3149824 | tf_op jit(solution)/shard_map/reduce_sum | solution.py:13
  46.8 1.9 %add_convert_fusion = bf16[512,1024]{1,0:T(8,128)(2,1)S(1)} fusion(f32[1024]{0:T(1024)S(1)} %bitcast.19, f32[1024]{0:T(1024)S(1)} %bitcast.20, f32[512]{0:T(512)S(1)} %add_rsqrt_fusion, f32[512]{0:T(512)S(1)} %broadcast_multiply_fusion, bf16[512,1024]{1,0:T(8,128)(2,1)} %collective-permute-done.1, bf16[512,1024]{1,0:T(8,128)(2,1)S(1)} %copy-done.2, ...), kind=kLoop, calls=%fused_computation.4 | loop fusion | flops 5242880 | bytes 4206592 | tf_op jit(solution)/shard_map/convert_element_type | solution.py:132
  48.7 0.0 copy-start.3
  48.7 1.0 copy-done.3
  49.7 0.0 copy-start.8
  49.7 0.3 broadcast_in_dim.6
  50.0 0.5 broadcast.61
  50.5 2.1 %reduce.4 = bf16[128,1024]{1,0:T(8,128)(2,1)S(1)} reduce(bf16[128,1,1024]{2,1,0:T(2,128)(2,1)S(1)} %broadcast_in_dim.6, bf16[]{:T(256)} %broadcast.61), dimensions={1}, to_apply=%broadcast_in_dim.6.reduce_sub_computation | reduce | bytes 524290 | tf_op jit(solution)/shard_map/broadcast_in_dim | solution.py:138
  52.6 0.2 reshape.45
  52.8 27.7 %all_to_all.19 = bf16[128,2,512]{2,1,0:T(2,128)(2,1)S(1)} all-to-all(bf16[128,2,512]{2,1,0:T(2,128)(2,1)S(1)} %reshape.45), channel_id=1, replica_groups=mesh['req'=128,'tp'=2] {'req'}, dimensions={0} | all-to-all | bytes 524288 | tf_op jit(solution)/shard_map/all_to_all | solution.py:137
  80.5 0.2 reshape.46
  80.8 0.0 copy-done.8
  80.8 0.3 convolution_reduce_fusion
  81.1 0.0 copy-start.6
  81.1 0.1 broadcast_in_dim.7
  81.2 0.2 all_to_all.16
  81.3 19.7 %all_to_all.20 = f32[256,1,1]{2,1,0:T(1,128)S(1)} all-to-all(f32[256,1,1]{2,1,0:T(1,128)S(1)} %all_to_all.16), channel_id=1, replica_groups=mesh['req'=128,'tp'=2] {'req','tp'}, dimensions={0} | all-to-all | bytes 2048 | tf_op jit(solution)/shard_map/all_to_all | solution.py:143
  101.0 0.9 reduce_max.21
  101.9 0.0 copy-done.6
  (7 shorter events, 0.1 us)
Async XLA Ops:
  0.6 30.4 %copy-start = (bf16[1024,1024]{1,0:T(8,128)(2,1)S(1)}, bf16[1024,1024]{1,0:T(8,128)(2,1)}, u32[]{:S(2)}) copy-start(bf16[1024,1024]{1,0:T(8,128)(2,1)} %param.24) | copy-start | bytes 6291460
  3.9 17.7 %copy-start.7 = (bf16[512,1024]{1,0:T(8,128)(2,1)S(1)}, bf16[512,1024]{1,0:T(8,128)(2,1)}, u32[]{:S(2)}) copy-start(bf16[512,1024]{1,0:T(8,128)(2,1)} %param.22) | copy-start | bytes 3145732
  21.6 5.4 %copy-start.4 = (f32[2,1024]{1,0:T(2,128)S(1)}, f32[2,1024]{1,0:T(2,128)}, u32[]{:S(2)}) copy-start(f32[2,1024]{1,0:T(2,128)} %param.26) | copy-start | bytes 24580
  21.6 5.4 %copy-start.5 = (f32[2,1024]{1,0:T(2,128)S(1)}, f32[2,1024]{1,0:T(2,128)}, u32[]{:S(2)}) copy-start(f32[2,1024]{1,0:T(2,128)} %param.25) | copy-start | bytes 24580
  21.6 7.6 %copy-start.1 = (bf16[512,1024]{1,0:T(8,128)(2,1)S(1)}, bf16[512,1024]{1,0:T(8,128)(2,1)}, u32[]{:S(2)}) copy-start(bf16[512,1024]{1,0:T(8,128)(2,1)} %x_ref.1) | copy-start | bytes 3145732
  23.5 5.8 %collective-permute-start = (bf16[512,1024]{1,0:T(8,128)(2,1)S(1)}, bf16[512,1024]{1,0:T(8,128)(2,1)S(1)}, u32[]{:S(2)}, u32[]{:S(2)}) collective-permute-start(bf16[512,1024]{1,0:T(8,128)(2,1)S(1)} %convolution_convert_fusion.1), channel_id=1, source_target_pairs={{0,1},{1,0},{2,3},{3,2},{4,5},{5,4},{6,7},{7,6},{8,9},{9,8},{10,11... | collective-permute-start | bytes 3145736 | tf_op jit(solution)/shard_map/ppermute | solution.py:19
  39.9 3.0 %collective-permute-start.1 = (bf16[512,1024]{1,0:T(8,128)(2,1)}, bf16[512,1024]{1,0:T(8,128)(2,1)}, u32[]{:S(2)}, u32[]{:S(2)}) collective-permute-start(bf16[512,1024]{1,0:T(8,128)(2,1)} %convolution_convert_fusion), channel_id=1, source_target_pairs={{0,1},{1,0},{2,3},{3,2},{4,5},{5,4},{6,7},{7,6},{8,9},{9,8},{10,11... | collective-permute-start | bytes 3145736 | tf_op jit(solution)/shard_map/ppermute | solution.py:19
  40.2 4.7 %copy-start.2 = (bf16[512,1024]{1,0:T(8,128)(2,1)S(1)}, bf16[512,1024]{1,0:T(8,128)(2,1)}, u32[]{:S(2)}) copy-start(bf16[512,1024]{1,0:T(8,128)(2,1)} %convolution_convert_fusion) | copy-start | bytes 3145732
  48.7 1.0 copy-start.3
  49.7 31.1 %copy-start.8 = (bf16[192,1024]{1,0:T(8,128)(2,1)S(1)}, bf16[192,1024]{1,0:T(8,128)(2,1)}, u32[]{:S(2)}) copy-start(bf16[192,1024]{1,0:T(8,128)(2,1)} %param.27) | copy-start | bytes 1179652
  81.1 20.8 %copy-start.6 = (f32[128]{0:T(128)}, f32[128]{0:T(128)S(1)}, u32[]{:S(2)}) copy-start(f32[128]{0:T(128)S(1)} %convolution_reduce_fusion) | copy-start | bytes 1540

commit v10 on v9

--- a/solution.py
+++ b/solution.py
@@ -24,9 +24,9 @@
 ROWS = 256
 
 
-def attention_kernel(lens_ref, x_ref, wq_ref, wk_ref, wv_ref, kc_ref, vc_ref, out_ref):
-    cached = lens_ref[0]
-    valid = lens_ref[1]
+def attention_kernel(cache_len_ref, group_len_ref, x_ref, wq_ref, wk_ref, wv_ref, kc_ref, vc_ref, out_ref):
+    cached = cache_len_ref[lax.axis_index("req")]
+    valid = group_len_ref[0]
     x = x_ref[...]
     q_all = jnp.dot(x, wq_ref[...], preferred_element_type=jnp.float32).astype(jnp.bfloat16)
     kn = jnp.dot(x, wk_ref[...], preferred_element_type=jnp.float32).astype(jnp.bfloat16)
@@ -68,7 +68,7 @@
         out_ref[row0 : row0 + ROWS, :] = result.astype(out_ref.dtype)
 
 
-def attention(lens, tokens, w_query, w_key, w_value, cache_k, cache_v):
+def attention(cache_len, group_len, tokens, w_query, w_key, w_value, cache_k, cache_v):
     rows, model = tokens.shape
     width = w_query.shape[1]
     cache_rows = cache_k.shape[0]
@@ -78,24 +78,24 @@
         attention_kernel,
         out_shape=jax.ShapeDtypeStruct((rows, width), jnp.bfloat16),
         grid_spec=pltpu.PrefetchScalarGridSpec(
-            num_scalar_prefetch=1,
+            num_scalar_prefetch=2,
             grid=(pairs,),
             in_specs=[
-                pl.BlockSpec((rows, model), lambda p, lens: (0, 0)),
-                pl.BlockSpec((model, PAIR), lambda p, lens: (0, p)),
-                pl.BlockSpec((model, PAIR), lambda p, lens: (0, p)),
-                pl.BlockSpec((model, PAIR), lambda p, lens: (0, p)),
-                pl.BlockSpec((cache_rows, PAIR), lambda p, lens: (0, p)),
-                pl.BlockSpec((cache_rows, PAIR), lambda p, lens: (0, p)),
+                pl.BlockSpec((rows, model), lambda p, c, g: (0, 0)),
+                pl.BlockSpec((model, PAIR), lambda p, c, g: (0, p)),
+                pl.BlockSpec((model, PAIR), lambda p, c, g: (0, p)),
+                pl.BlockSpec((model, PAIR), lambda p, c, g: (0, p)),
+                pl.BlockSpec((cache_rows, PAIR), lambda p, c, g: (0, p)),
+                pl.BlockSpec((cache_rows, PAIR), lambda p, c, g: (0, p)),
             ],
-            out_specs=pl.BlockSpec((rows, PAIR), lambda p, lens: (0, p)),
+            out_specs=pl.BlockSpec((rows, PAIR), lambda p, c, g: (0, p)),
         ),
         cost_estimate=pl.CostEstimate(
             flops=flops,
             transcendentals=rows * (cache_rows + rows) * width // HD,
             bytes_accessed=2 * (rows * model + 3 * model * width + 2 * cache_rows * width + rows * width),
         ),
-    )(lens, tokens, w_query, w_key, w_value, cache_k, cache_v)
+    )(cache_len, group_len, tokens, w_query, w_key, w_value, cache_k, cache_v)
 
 
 def shards(
@@ -117,10 +117,8 @@
     block_rows = tokens.shape[0]
     local_width = w_query.shape[1]
     my_index = lax.axis_index("req")
-    my_cache = lax.dynamic_index_in_dim(cache_len, my_index, 0, keepdims=False)
     my_valid = group_len[0]
-    lens = jnp.stack([my_cache, my_valid]).astype(jnp.int32)
-    attn_mixed = attention(lens, tokens, w_query, w_key, w_value, cache_keys[0], cache_values[0])
+    attn_mixed = attention(cache_len, group_len, tokens, w_query, w_key, w_value, cache_keys[0], cache_values[0])
     attn_sum = pair_sum(jnp.dot(attn_mixed, w_out, preferred_element_type=jnp.float32))
     middle = normalize(tokens.astype(jnp.float32) + attn_sum, ln_gains[0], ln_biases[0]).astype(
         jnp.bfloat16

time: 102 us -> 99.8 us (0.978)
  local copies, waits for them, and re-layouts: 3.71 us -> 2.47 us
  other arithmetic: 11.8 us -> 10.6 us
    dynamic_slice x1 -> x0, local copies, waits for them, and re-layouts: 1.24 us -> none  [shards(): my_cache = lax.dynamic_index_in_dim(cache_len, my_index, 0, keepdims=False)]
    another operation x1 -> x0, other arithmetic: 1.23 us -> none  [shards(): lens = jnp.stack([my_cache, my_valid]).astype(jnp.int32)]
where the time goes in v10:
time: 99.8 us; the launch traced here: 99.4 us
  blocking collectives  47.4 us (47%)
  Pallas kernels  17.7 us (18%)
  matrix products  11 us (11%)
  other arithmetic  10.6 us (11%)
  waiting for transfers between devices  4.88 us (5%)
  starting transfers between devices  3.84 us (4%)
  local copies, waits for them, and re-layouts  2.47 us (2%)
  between operations  1.59 us (2%)
    all_to_all x1, blocking collectives, shards(): lax.all_to_all(jnp.broadcast_to(last_row, (reqs, last_row.shape[1])), 're...  27.7 us
    all_to_all x1, blocking collectives, shards(): lax.all_to_all(spread, ('req', 'tp'), 0, 0, tiled=True)  19.7 us
    pallas_call x1, Pallas kernels, attention(): pl.pallas_call(attention_kernel, out_shape=jax.ShapeDtypeStruct((rows, wi...  17.7 us
    dot_general x1, matrix products, shards(): jnp.dot(active, w_down, preferred_element_type=jnp.float32)  8.81 us
    ppermute x2, waiting for transfers between devices, pair_sum(): other = lax.ppermute(own, 'tp', [(0, 1), (1, 0)])  4.88 us
    ppermute x2, starting transfers between devices, pair_sum(): other = lax.ppermute(own, 'tp', [(0, 1), (1, 0)])  3.84 us
    reduce_sum x2, other arithmetic, normalize(): center = rows - jnp.mean(rows, axis=-1, keepdims=True)  2.51 us
    reduce_sum x2, other arithmetic, normalize(): spread = jnp.mean(center * center, axis=-1, keepdims=True)  2.47 us
  transfers between devices with their start and end apart: 2, of which 2 were waited for; matrix products, arithmetic and copies ran while one was open for 0% of the time, Pallas kernels for 0%

profile of v10, /device:TPU:1, one launch (start us, length us, event | category | flops | bytes accessed | tf_op | source)
XLA Modules:
  0.0 99.4 jit_solution(14597707004480289168)
XLA Ops:
  0.6 0.0 copy-start
  1.4 0.0 copy-start.7
  1.5 17.7 %shard_map.157 = bf16[512,512]{1,0:T(8,128)(2,1)} custom-call(s32[128]{0:T(128)} %cache_len_ref.1, s32[1]{0:T(128)S(6)} %copy.23.group_len_ref, bf16[512,1024]{1,0:T(8,128)(2,1)} %x_ref.1, bf16[1024,512]{1,0:T(8,128)(2,1)} %wq_ref.1, bf16[1024,512]{1,0:T(8,128)(2,1)} %wk_ref.1, bf16[1024,512]{1,0:T(8,128)(2,1)} %wv_ref.1, bf16[1024,512]{1,0:T(8,128)(2,1)} %bitcast.24, ...), custom_call_target="tpu_custom_call" | custom-call | flops 4831838208 | bytes 6815744 | tf_op jit(solution)/shard_map/pallas_call | solution.py:77
  19.1 0.0 copy-done.7
  19.1 0.0 copy-start.4
  19.2 0.0 copy-start.5
  19.2 0.0 copy-start.1
  19.2 1.8 %convolution_convert_fusion.1 = bf16[512,1024]{1,0:T(8,128)(2,1)S(1)} fusion(bf16[512,512]{1,0:T(8,128)(2,1)} %shard_map.157, bf16[512,1024]{1,0:T(8,128)(2,1)S(1)} %copy-done.7), kind=kOutput, calls=%fused_computation.26 | convolution fusion | flops 537395200 | bytes 2621440 | tf_op jit(solution)/shard_map/dot_general | solution.py:122
  21.0 3.5 %collective-permute-start = (bf16[512,1024]{1,0:T(8,128)(2,1)S(1)}, bf16[512,1024]{1,0:T(8,128)(2,1)S(1)}, u32[]{:S(2)}, u32[]{:S(2)}) collective-permute-start(bf16[512,1024]{1,0:T(8,128)(2,1)S(1)} %convolution_convert_fusion.1), channel_id=1, source_target_pairs={{0,1},{1,0},{2,3},{3,2},{4,5},{5,4},{6,7},{7,6},{8,9},{9,8},{10,11... | collective-permute-start | bytes 3145736 | tf_op jit(solution)/shard_map/ppermute | solution.py:19
  24.5 0.0 copy-done.4
  24.5 0.0 copy-done.5
  24.5 2.2 %collective-permute-done = bf16[512,1024]{1,0:T(8,128)(2,1)S(1)} collective-permute-done((bf16[512,1024]{1,0:T(8,128)(2,1)S(1)}, bf16[512,1024]{1,0:T(8,128)(2,1)S(1)}, u32[]{:S(2)}, u32[]{:S(2)}) %collective-permute-start) | collective-permute-done | bytes 1048608 | tf_op jit(solution)/shard_map/ppermute | solution.py:19
  26.8 0.0 copy-done.1
  26.8 0.5 fusion.41
  27.3 0.6 multiply_reduce_fusion.1
  27.9 0.7 add_convert_fusion.1
  28.6 0.0 copy-done
  28.6 8.8 %convolution_convert_fusion = bf16[512,1024]{1,0:T(8,128)(2,1)} fusion(bf16[1024,1024]{1,0:T(8,128)(2,1)S(1)} %copy-done, bf16[512,1024]{1,0:T(8,128)(2,1)S(1)} %add_convert_fusion.1, bf16[1024,1024]{1,0:T(8,128)(2,1)} %param.23), kind=kOutput, calls=%fused_computation.25 | convolution fusion | flops 2182086656 | bytes 6291456 | tf_op jit(solution)/shard_map/dot_general | solution.py:129
  37.4 0.4 collective-permute-start.1
  37.8 0.0 copy-start.2
  37.8 2.6 %collective-permute-done.1 = bf16[512,1024]{1,0:T(8,128)(2,1)} collective-permute-done((bf16[512,1024]{1,0:T(8,128)(2,1)}, bf16[512,1024]{1,0:T(8,128)(2,1)}, u32[]{:S(2)}, u32[]{:S(2)}) %collective-permute-start.1) | collective-permute-done | bytes 1048608 | tf_op jit(solution)/shard_map/ppermute | solution.py:19
  40.4 2.0 %fusion.42 = f32[512]{0:T(512)S(1)} fusion(bf16[512,1024]{1,0:T(8,128)(2,1)} %collective-permute-done.1, bf16[512,1024]{1,0:T(8,128)(2,1)} %convolution_convert_fusion, bf16[512,1024]{1,0:T(8,128)(2,1)S(1)} %add_convert_fusion.1), kind=kLoop, calls=%fused_computation.59 | loop fusion | flops 3145216 | bytes 3147776 | tf_op jit(solution)/shard_map/reduce_sum | solution.py:12
  42.4 0.0 copy-done.2
  42.5 1.8 %multiply_reduce_fusion = f32[512]{0:T(512)S(1)} fusion(f32[512]{0:T(512)S(1)} %broadcast_multiply_fusion, bf16[512,1024]{1,0:T(8,128)(2,1)} %collective-permute-done.1, bf16[512,1024]{1,0:T(8,128)(2,1)S(1)} %copy-done.2, bf16[512,1024]{1,0:T(8,128)(2,1)S(1)} %add_convert_fusion.1), kind=kLoop, calls=%fused_computation.5 | loop fusion | flops 4193792 | bytes 3149824 | tf_op jit(solution)/shard_map/reduce_sum | solution.py:13
  44.3 1.9 %add_convert_fusion = bf16[512,1024]{1,0:T(8,128)(2,1)S(1)} fusion(f32[1024]{0:T(1024)S(1)} %bitcast.19, f32[1024]{0:T(1024)S(1)} %bitcast.20, f32[512]{0:T(512)S(1)} %add_rsqrt_fusion, f32[512]{0:T(512)S(1)} %broadcast_multiply_fusion, bf16[512,1024]{1,0:T(8,128)(2,1)} %collective-permute-done.1, bf16[512,1024]{1,0:T(8,128)(2,1)S(1)} %copy-done.2, ...), kind=kLoop, calls=%fused_computation.4 | loop fusion | flops 5242880 | bytes 4206592 | tf_op jit(solution)/shard_map/convert_element_type | solution.py:130
  46.2 0.0 copy-start.3
  46.2 1.0 copy-done.3
  47.2 0.0 copy-start.8
  47.2 0.3 broadcast_in_dim.6
  47.5 0.5 broadcast.61
  48.0 2.1 %reduce.4 = bf16[128,1024]{1,0:T(8,128)(2,1)S(1)} reduce(bf16[128,1,1024]{2,1,0:T(2,128)(2,1)S(1)} %broadcast_in_dim.6, bf16[]{:T(256)} %broadcast.61), dimensions={1}, to_apply=%broadcast_in_dim.6.reduce_sub_computation | reduce | bytes 524290 | tf_op jit(solution)/shard_map/broadcast_in_dim | solution.py:136
  50.2 0.2 reshape.45
  50.4 27.7 %all_to_all.19 = bf16[128,2,512]{2,1,0:T(2,128)(2,1)S(1)} all-to-all(bf16[128,2,512]{2,1,0:T(2,128)(2,1)S(1)} %reshape.45), channel_id=1, replica_groups=mesh['req'=128,'tp'=2] {'req'}, dimensions={0} | all-to-all | bytes 524288 | tf_op jit(solution)/shard_map/all_to_all | solution.py:135
  78.1 0.2 reshape.46
  78.3 0.0 copy-done.8
  78.3 0.3 convolution_reduce_fusion
  78.6 0.0 copy-start.6
  78.6 0.1 broadcast_in_dim.7
  78.7 0.2 all_to_all.16
  78.9 19.7 %all_to_all.20 = f32[256,1,1]{2,1,0:T(1,128)S(1)} all-to-all(f32[256,1,1]{2,1,0:T(1,128)S(1)} %all_to_all.16), channel_id=1, replica_groups=mesh['req'=128,'tp'=2] {'req','tp'}, dimensions={0} | all-to-all | bytes 2048 | tf_op jit(solution)/shard_map/all_to_all | solution.py:141
  98.5 0.9 reduce_max.21
  99.4 0.0 copy-done.6
  (7 shorter events, 0.1 us)
Async XLA Ops:
  0.6 28.0 %copy-start = (bf16[1024,1024]{1,0:T(8,128)(2,1)S(1)}, bf16[1024,1024]{1,0:T(8,128)(2,1)}, u32[]{:S(2)}) copy-start(bf16[1024,1024]{1,0:T(8,128)(2,1)} %param.24) | copy-start | bytes 6291460
  1.4 17.7 %copy-start.7 = (bf16[512,1024]{1,0:T(8,128)(2,1)S(1)}, bf16[512,1024]{1,0:T(8,128)(2,1)}, u32[]{:S(2)}) copy-start(bf16[512,1024]{1,0:T(8,128)(2,1)} %param.22) | copy-start | bytes 3145732
  19.1 5.4 %copy-start.4 = (f32[2,1024]{1,0:T(2,128)S(1)}, f32[2,1024]{1,0:T(2,128)}, u32[]{:S(2)}) copy-start(f32[2,1024]{1,0:T(2,128)} %param.26) | copy-start | bytes 24580
  19.2 5.4 %copy-start.5 = (f32[2,1024]{1,0:T(2,128)S(1)}, f32[2,1024]{1,0:T(2,128)}, u32[]{:S(2)}) copy-start(f32[2,1024]{1,0:T(2,128)} %param.25) | copy-start | bytes 24580
  19.2 7.6 %copy-start.1 = (bf16[512,1024]{1,0:T(8,128)(2,1)S(1)}, bf16[512,1024]{1,0:T(8,128)(2,1)}, u32[]{:S(2)}) copy-start(bf16[512,1024]{1,0:T(8,128)(2,1)} %x_ref.1) | copy-start | bytes 3145732
  21.0 5.8 %collective-permute-start = (bf16[512,1024]{1,0:T(8,128)(2,1)S(1)}, bf16[512,1024]{1,0:T(8,128)(2,1)S(1)}, u32[]{:S(2)}, u32[]{:S(2)}) collective-permute-start(bf16[512,1024]{1,0:T(8,128)(2,1)S(1)} %convolution_convert_fusion.1), channel_id=1, source_target_pairs={{0,1},{1,0},{2,3},{3,2},{4,5},{5,4},{6,7},{7,6},{8,9},{9,8},{10,11... | collective-permute-start | bytes 3145736 | tf_op jit(solution)/shard_map/ppermute | solution.py:19
  37.4 3.0 %collective-permute-start.1 = (bf16[512,1024]{1,0:T(8,128)(2,1)}, bf16[512,1024]{1,0:T(8,128)(2,1)}, u32[]{:S(2)}, u32[]{:S(2)}) collective-permute-start(bf16[512,1024]{1,0:T(8,128)(2,1)} %convolution_convert_fusion), channel_id=1, source_target_pairs={{0,1},{1,0},{2,3},{3,2},{4,5},{5,4},{6,7},{7,6},{8,9},{9,8},{10,11... | collective-permute-start | bytes 3145736 | tf_op jit(solution)/shard_map/ppermute | solution.py:19
  37.8 4.7 %copy-start.2 = (bf16[512,1024]{1,0:T(8,128)(2,1)S(1)}, bf16[512,1024]{1,0:T(8,128)(2,1)}, u32[]{:S(2)}) copy-start(bf16[512,1024]{1,0:T(8,128)(2,1)} %convolution_convert_fusion) | copy-start | bytes 3145732
  46.2 1.0 copy-start.3
  47.2 31.1 %copy-start.8 = (bf16[192,1024]{1,0:T(8,128)(2,1)S(1)}, bf16[192,1024]{1,0:T(8,128)(2,1)}, u32[]{:S(2)}) copy-start(bf16[192,1024]{1,0:T(8,128)(2,1)} %param.27) | copy-start | bytes 1179652
  78.6 20.8 %copy-start.6 = (f32[128]{0:T(128)}, f32[128]{0:T(128)S(1)}, u32[]{:S(2)}) copy-start(f32[128]{0:T(128)S(1)} %convolution_reduce_fusion) | copy-start | bytes 1540

commit v11 on v10

--- a/solution.py
+++ b/solution.py
@@ -98,6 +98,35 @@
     )(cache_len, group_len, tokens, w_query, w_key, w_value, cache_k, cache_v)
 
 
+NORM_ROWS = 256
+
+
+def residual_norm_kernel(mid_ref, own_ref, other_ref, gain_ref, bias_ref, out_ref):
+    total = own_ref[...].astype(jnp.float32) + other_ref[...].astype(jnp.float32)
+    rows = mid_ref[...].astype(jnp.float32) + total
+    center = rows - jnp.mean(rows, axis=-1, keepdims=True)
+    spread = jnp.mean(center * center, axis=-1, keepdims=True)
+    out_ref[...] = (center * lax.rsqrt(spread + 1e-05) * gain_ref[...] + bias_ref[...]).astype(
+        out_ref.dtype
+    )
+
+
+def residual_norm(middle, own, other, gain, bias):
+    rows, width = middle.shape
+    block = pl.BlockSpec((NORM_ROWS, width), lambda i: (i, 0))
+    vector = pl.BlockSpec((1, width), lambda i: (0, 0))
+    return pl.pallas_call(
+        residual_norm_kernel,
+        out_shape=jax.ShapeDtypeStruct((rows, width), jnp.bfloat16),
+        grid=(rows // NORM_ROWS,),
+        in_specs=[block, block, block, vector, vector],
+        out_specs=block,
+        cost_estimate=pl.CostEstimate(
+            flops=10 * rows * width, transcendentals=rows, bytes_accessed=8 * rows * width
+        ),
+    )(middle, own, other, gain, bias)
+
+
 def shards(
     tokens,
     group_len,
@@ -126,10 +155,9 @@
     active = jax.nn.gelu(
         jnp.dot(middle, w_up, preferred_element_type=jnp.float32), approximate=False
     ).astype(jnp.bfloat16)
-    ffn_sum = pair_sum(jnp.dot(active, w_down, preferred_element_type=jnp.float32))
-    layer_out = normalize(middle.astype(jnp.float32) + ffn_sum, ln_gains[1], ln_biases[1]).astype(
-        jnp.bfloat16
-    )
+    own = jnp.dot(active, w_down, preferred_element_type=jnp.float32).astype(jnp.bfloat16)
+    other = lax.ppermute(own, "tp", [(0, 1), (1, 0)])
+    layer_out = residual_norm(middle, own, other, ln_gains[1:2], ln_biases[1:2])
     last_row = lax.dynamic_slice_in_dim(layer_out, my_valid - 1, 1, 0)
     reqs = cache_len.shape[0]
     all_rows = lax.all_to_all(

time: 99.8 us -> 97.4 us (0.976)
  other arithmetic: 10.6 us -> 4.81 us
  Pallas kernels: 17.7 us -> 20.9 us
    pallas_call x0 -> x1, Pallas kernels: none -> 3.22 us  [residual_norm(): pl.pallas_call(residual_norm_kernel, out_shape=jax.ShapeDtypeStruct((rows...]
    ppermute x2 -> x1, waiting for transfers between devices: 4.88 us -> 1.67 us  [pair_sum(): other = lax.ppermute(own, 'tp', [(0, 1), (1, 0)])]
    ppermute x0 -> x1, waiting for transfers between devices: none -> 2.63 us  [shards(): other = lax.ppermute(own, 'tp', [(0, 1), (1, 0)])]
    reduce_sum x2 -> x1, other arithmetic: 2.51 us -> 0.48 us  [normalize(): center = rows - jnp.mean(rows, axis=-1, keepdims=True)]
    convert_element_type x1 -> x0, other arithmetic: 1.91 us -> none  [shards(): normalize(middle.astype(jnp.float32) + ffn_sum, ln_gains[1], ln_biases[1])]
    reduce_sum x2 -> x1, other arithmetic: 2.47 us -> 0.62 us  [normalize(): spread = jnp.mean(center * center, axis=-1, keepdims=True)]
    ppermute x2 -> x1, starting transfers between devices: 3.84 us -> 3.47 us  [pair_sum(): other = lax.ppermute(own, 'tp', [(0, 1), (1, 0)])]
  transfers between devices with their start and end apart: 2 -> 2, of which waited for: 2 -> 2; matrix products, arithmetic and copies ran while one was open for 0% -> 1% of each run, Pallas kernels for 0% -> 0%
where the time goes in v11:
time: 97.4 us; the launch traced here: 97.1 us
  blocking collectives  47.4 us (49%)
  Pallas kernels  20.9 us (21%)
  matrix products  11.4 us (12%)
  other arithmetic  4.81 us (5%)
  waiting for transfers between devices  4.3 us (4%)
  starting transfers between devices  3.85 us (4%)
  local copies, waits for them, and re-layouts  2.86 us (3%)
  between operations  1.55 us (2%)
    all_to_all x1, blocking collectives, shards(): lax.all_to_all(jnp.broadcast_to(last_row, (reqs, last_row.shape[1])), 're...  27.7 us
    all_to_all x1, blocking collectives, shards(): lax.all_to_all(spread, ('req', 'tp'), 0, 0, tiled=True)  19.7 us
    pallas_call x1, Pallas kernels, attention(): pl.pallas_call(attention_kernel, out_shape=jax.ShapeDtypeStruct((rows, wi...  17.7 us
    dot_general x1, matrix products, shards(): jnp.dot(active, w_down, preferred_element_type=jnp.float32)  9.24 us
    ppermute x1, starting transfers between devices, pair_sum(): other = lax.ppermute(own, 'tp', [(0, 1), (1, 0)])  3.47 us
    pallas_call x1, Pallas kernels, residual_norm(): pl.pallas_call(residual_norm_kernel, out_shape=jax.ShapeDtypeStruct((rows...  3.22 us
    ppermute x1, waiting for transfers between devices, shards(): other = lax.ppermute(own, 'tp', [(0, 1), (1, 0)])  2.63 us
    broadcast_in_dim x1, other arithmetic, shards(): jnp.broadcast_to(last_row, (reqs, last_row.shape[1]))  2.15 us
  transfers between devices with their start and end apart: 2, of which 2 were waited for; matrix products, arithmetic and copies ran while one was open for 1% of the time, Pallas kernels for 0%

profile of v11, /device:TPU:1, one launch (start us, length us, event | category | flops | bytes accessed | tf_op | source)
XLA Modules:
  0.0 97.1 jit_solution(1707491357959397004)
XLA Ops:
  0.6 0.0 copy-start
  1.4 0.0 copy-start.6
  1.5 17.7 %shard_map.157 = bf16[512,512]{1,0:T(8,128)(2,1)} custom-call(s32[128]{0:T(128)} %cache_len_ref.1, s32[1]{0:T(128)S(6)} %copy.23.group_len_ref, bf16[512,1024]{1,0:T(8,128)(2,1)} %x_ref.1, bf16[1024,512]{1,0:T(8,128)(2,1)} %wq_ref.1, bf16[1024,512]{1,0:T(8,128)(2,1)} %wk_ref.1, bf16[1024,512]{1,0:T(8,128)(2,1)} %wv_ref.1, bf16[1024,512]{1,0:T(8,128)(2,1)} %bitcast.20, ...), custom_call_target="tpu_custom_call" | custom-call | flops 4831838208 | bytes 6815744 | tf_op jit(solution)/shard_map/pallas_call | solution.py:77
  19.1 0.0 copy-done.6
  19.1 0.0 copy-start.3
  19.2 0.0 copy-start.4
  19.2 0.0 copy-start.1
  19.2 1.8 %convolution_convert_fusion.1 = bf16[512,1024]{1,0:T(8,128)(2,1)S(1)} fusion(bf16[512,512]{1,0:T(8,128)(2,1)} %shard_map.157, bf16[512,1024]{1,0:T(8,128)(2,1)S(1)} %copy-done.6), kind=kOutput, calls=%fused_computation.23 | convolution fusion | flops 537395200 | bytes 2621440 | tf_op jit(solution)/shard_map/dot_general | solution.py:151
  21.0 3.5 %collective-permute-start = (bf16[512,1024]{1,0:T(8,128)(2,1)S(1)}, bf16[512,1024]{1,0:T(8,128)(2,1)S(1)}, u32[]{:S(2)}, u32[]{:S(2)}) collective-permute-start(bf16[512,1024]{1,0:T(8,128)(2,1)S(1)} %convolution_convert_fusion.1), channel_id=1, source_target_pairs={{0,1},{1,0},{2,3},{3,2},{4,5},{5,4},{6,7},{7,6},{8,9},{9,8},{10,11... | collective-permute-start | bytes 3145736 | tf_op jit(solution)/shard_map/ppermute | solution.py:19
  24.5 0.0 copy-done.3
  24.5 0.0 copy-done.4
  24.5 0.6 fusion.74
  25.1 1.7 %collective-permute-done = bf16[512,1024]{1,0:T(8,128)(2,1)S(1)} collective-permute-done((bf16[512,1024]{1,0:T(8,128)(2,1)S(1)}, bf16[512,1024]{1,0:T(8,128)(2,1)S(1)}, u32[]{:S(2)}, u32[]{:S(2)}) %collective-permute-start) | collective-permute-done | bytes 1048608 | tf_op jit(solution)/shard_map/ppermute | solution.py:19
  26.8 0.0 copy-done.1
  26.8 0.5 fusion.41
  27.3 0.6 multiply_reduce_fusion
  27.9 0.7 add_convert_fusion.mid_ref
  28.6 0.0 copy-done
  28.6 0.0 copy-start.2
  28.6 9.2 %convolution_convert_fusion.own_ref = bf16[512,1024]{1,0:T(8,128)(2,1)} fusion(bf16[1024,1024]{1,0:T(8,128)(2,1)S(1)} %copy-done, bf16[512,1024]{1,0:T(8,128)(2,1)S(1)} %add_convert_fusion.mid_ref, bf16[1024,1024]{1,0:T(8,128)(2,1)} %param.23), kind=kOutput, calls=%fused_computation.22 | convolution fusion | flops 2182086656 | bytes 6291456 | tf_op jit(solution)/shard_map/dot_general | solution.py:158
  37.8 0.0 copy-done.2
  37.9 0.4 collective-permute-start.1
  38.2 2.6 %collective-permute-done.1.other_ref = bf16[512,1024]{1,0:T(8,128)(2,1)} collective-permute-done((bf16[512,1024]{1,0:T(8,128)(2,1)}, bf16[512,1024]{1,0:T(8,128)(2,1)}, u32[]{:S(2)}, u32[]{:S(2)}) %collective-permute-start.1) | collective-permute-done | bytes 1048608 | tf_op jit(solution)/shard_map/ppermute | solution.py:159
  40.9 3.2 %shard_map.158 = bf16[512,1024]{1,0:T(8,128)(2,1)} custom-call(bf16[512,1024]{1,0:T(8,128)(2,1)} %copy-done.2, bf16[512,1024]{1,0:T(8,128)(2,1)} %convolution_convert_fusion.own_ref, bf16[512,1024]{1,0:T(8,128)(2,1)} %collective-permute-done.1.other_ref, f32[1,1024]{1,0:T(1,128)} %get-tuple-element.8.gain_ref, f32[1,1024]{1,0:T(1,128)} %get-tuple-element.3.bias_ref), custom_call_target="tpu_custom_call" | custom-call | flops 5242880 | bytes 4194304 | tf_op jit(solution)/shard_map/pallas_call | solution.py:118
  44.1 0.0 copy-start.7
  44.1 0.8 dynamic-slice_reduce_fusion
  44.9 0.3 broadcast_in_dim.6
  45.2 0.5 broadcast.36
  45.7 2.1 %reduce.4 = bf16[128,1024]{1,0:T(8,128)(2,1)S(1)} reduce(bf16[128,1,1024]{2,1,0:T(2,128)(2,1)S(1)} %broadcast_in_dim.6, bf16[]{:T(256)} %broadcast.36), dimensions={1}, to_apply=%broadcast_in_dim.6.reduce_sub_computation | reduce | bytes 524290 | tf_op jit(solution)/shard_map/broadcast_in_dim | solution.py:164
  47.8 0.2 reshape.33
  48.0 27.7 %all_to_all.19 = bf16[128,2,512]{2,1,0:T(2,128)(2,1)S(1)} all-to-all(bf16[128,2,512]{2,1,0:T(2,128)(2,1)S(1)} %reshape.33), channel_id=1, replica_groups=mesh['req'=128,'tp'=2] {'req'}, dimensions={0} | all-to-all | bytes 524288 | tf_op jit(solution)/shard_map/all_to_all | solution.py:163
  75.7 0.2 reshape.34
  76.0 0.0 copy-done.7
  76.0 0.3 convolution_reduce_fusion
  76.3 0.0 copy-start.5
  76.3 0.1 broadcast_in_dim.14
  76.3 0.2 all_to_all.16
  76.5 19.7 %all_to_all.20 = f32[256,1,1]{2,1,0:T(1,128)S(1)} all-to-all(f32[256,1,1]{2,1,0:T(1,128)S(1)} %all_to_all.16), channel_id=1, replica_groups=mesh['req'=128,'tp'=2] {'req','tp'}, dimensions={0} | all-to-all | bytes 2048 | tf_op jit(solution)/shard_map/all_to_all | solution.py:169
  96.2 0.9 reduce_max.21
  97.1 0.0 copy-done.5
  (2 shorter events, 0.0 us)
Async XLA Ops:
  0.6 28.0 %copy-start = (bf16[1024,1024]{1,0:T(8,128)(2,1)S(1)}, bf16[1024,1024]{1,0:T(8,128)(2,1)}, u32[]{:S(2)}) copy-start(bf16[1024,1024]{1,0:T(8,128)(2,1)} %param.24) | copy-start | bytes 6291460
  1.4 17.7 %copy-start.6 = (bf16[512,1024]{1,0:T(8,128)(2,1)S(1)}, bf16[512,1024]{1,0:T(8,128)(2,1)}, u32[]{:S(2)}) copy-start(bf16[512,1024]{1,0:T(8,128)(2,1)} %param.22) | copy-start | bytes 3145732
  19.1 5.4 %copy-start.3 = (f32[2,1024]{1,0:T(2,128)S(1)}, f32[2,1024]{1,0:T(2,128)}, u32[]{:S(2)}) copy-start(f32[2,1024]{1,0:T(2,128)} %param.26) | copy-start | bytes 24580
  19.2 5.3 %copy-start.4 = (f32[2,1024]{1,0:T(2,128)S(1)}, f32[2,1024]{1,0:T(2,128)}, u32[]{:S(2)}) copy-start(f32[2,1024]{1,0:T(2,128)} %param.25) | copy-start | bytes 24580
  19.2 7.6 %copy-start.1 = (bf16[512,1024]{1,0:T(8,128)(2,1)S(1)}, bf16[512,1024]{1,0:T(8,128)(2,1)}, u32[]{:S(2)}) copy-start(bf16[512,1024]{1,0:T(8,128)(2,1)} %x_ref.1) | copy-start | bytes 3145732
  21.0 5.8 %collective-permute-start = (bf16[512,1024]{1,0:T(8,128)(2,1)S(1)}, bf16[512,1024]{1,0:T(8,128)(2,1)S(1)}, u32[]{:S(2)}, u32[]{:S(2)}) collective-permute-start(bf16[512,1024]{1,0:T(8,128)(2,1)S(1)} %convolution_convert_fusion.1), channel_id=1, source_target_pairs={{0,1},{1,0},{2,3},{3,2},{4,5},{5,4},{6,7},{7,6},{8,9},{9,8},{10,11... | collective-permute-start | bytes 3145736 | tf_op jit(solution)/shard_map/ppermute | solution.py:19
  28.6 9.3 %copy-start.2 = (bf16[512,1024]{1,0:T(8,128)(2,1)}, bf16[512,1024]{1,0:T(8,128)(2,1)S(1)}, u32[]{:S(2)}) copy-start(bf16[512,1024]{1,0:T(8,128)(2,1)S(1)} %add_convert_fusion.mid_ref) | copy-start | bytes 3145732
  37.9 3.0 %collective-permute-start.1 = (bf16[512,1024]{1,0:T(8,128)(2,1)}, bf16[512,1024]{1,0:T(8,128)(2,1)}, u32[]{:S(2)}, u32[]{:S(2)}) collective-permute-start(bf16[512,1024]{1,0:T(8,128)(2,1)} %convolution_convert_fusion.own_ref), channel_id=1, source_target_pairs={{0,1},{1,0},{2,3},{3,2},{4,5},{5,4},{6,7},{7,6},{8,9},{9,8},{10,11... | collective-permute-start | bytes 3145736 | tf_op jit(solution)/shard_map/ppermute | solution.py:159
  44.1 31.9 %copy-start.7 = (bf16[192,1024]{1,0:T(8,128)(2,1)S(1)}, bf16[192,1024]{1,0:T(8,128)(2,1)}, u32[]{:S(2)}) copy-start(bf16[192,1024]{1,0:T(8,128)(2,1)} %param.27) | copy-start | bytes 1179652
  76.3 20.8 %copy-start.5 = (f32[128]{0:T(128)}, f32[128]{0:T(128)S(1)}, u32[]{:S(2)}) copy-start(f32[128]{0:T(128)S(1)} %convolution_reduce_fusion) | copy-start | bytes 1540

commit v12 on v11

--- a/solution.py
+++ b/solution.py
@@ -148,10 +148,9 @@
     my_index = lax.axis_index("req")
     my_valid = group_len[0]
     attn_mixed = attention(cache_len, group_len, tokens, w_query, w_key, w_value, cache_keys[0], cache_values[0])
-    attn_sum = pair_sum(jnp.dot(attn_mixed, w_out, preferred_element_type=jnp.float32))
-    middle = normalize(tokens.astype(jnp.float32) + attn_sum, ln_gains[0], ln_biases[0]).astype(
-        jnp.bfloat16
-    )
+    attn_own = jnp.dot(attn_mixed, w_out, preferred_element_type=jnp.float32).astype(jnp.bfloat16)
+    attn_other = lax.ppermute(attn_own, "tp", [(0, 1), (1, 0)])
+    middle = residual_norm(tokens, attn_own, attn_other, ln_gains[0:1], ln_biases[0:1])
     active = jax.nn.gelu(
         jnp.dot(middle, w_up, preferred_element_type=jnp.float32), approximate=False
     ).astype(jnp.bfloat16)

time: 97.4 us -> 98.7 us (1.013)
  Pallas kernels: 20.9 us -> 24 us
  other arithmetic: 4.81 us -> 3.02 us
  local copies, waits for them, and re-layouts: 2.86 us -> 3.89 us
    pallas_call x1 -> x2, Pallas kernels: 3.22 us -> 6.4 us  [residual_norm(): pl.pallas_call(residual_norm_kernel, out_shape=jax.ShapeDtypeStruct((rows...]
    reduce_sum x2 -> x0, other arithmetic: 1.1 us -> none  [the longest x1 0.62 us: normalize(): spread = jnp.mean(center * center, axis=-1, keepdims=True)]
    dot_general x1, matrix products: 9.24 us -> 8.15 us  [shards(): jnp.dot(active, w_down, preferred_element_type=jnp.float32)]
    unnamed x18, local copies, waits for them, and re-layouts: 0.44 us -> 1.47 us
where the time goes in v12:
time: 98.7 us; the launch traced here: 98.4 us
  blocking collectives  47.4 us (48%)
  Pallas kernels  24 us (24%)
  matrix products  10.6 us (11%)
  waiting for transfers between devices  4.09 us (4%)
  starting transfers between devices  3.93 us (4%)
  local copies, waits for them, and re-layouts  3.89 us (4%)
  other arithmetic  3.02 us (3%)
  between operations  1.53 us (2%)
    all_to_all x1, blocking collectives, shards(): lax.all_to_all(jnp.broadcast_to(last_row, (reqs, last_row.shape[1])), 're...  27.7 us
    all_to_all x1, blocking collectives, shards(): lax.all_to_all(spread, ('req', 'tp'), 0, 0, tiled=True)  19.7 us
    pallas_call x1, Pallas kernels, attention(): pl.pallas_call(attention_kernel, out_shape=jax.ShapeDtypeStruct((rows, wi...  17.6 us
    dot_general x1, matrix products, shards(): jnp.dot(active, w_down, preferred_element_type=jnp.float32)  8.15 us
    pallas_call x2, Pallas kernels, residual_norm(): pl.pallas_call(residual_norm_kernel, out_shape=jax.ShapeDtypeStruct((rows...  6.4 us
    ppermute x1, starting transfers between devices, shards(): attn_other = lax.ppermute(attn_own, 'tp', [(0, 1), (1, 0)])  3.29 us
    ppermute x1, waiting for transfers between devices, shards(): other = lax.ppermute(own, 'tp', [(0, 1), (1, 0)])  2.42 us
    broadcast_in_dim x1, other arithmetic, shards(): jnp.broadcast_to(last_row, (reqs, last_row.shape[1]))  2.15 us
  transfers between devices with their start and end apart: 2, of which 2 were waited for; matrix products, arithmetic and copies ran while one was open for 1% of the time, Pallas kernels for 0%

profile of v12, /device:TPU:1, one launch (start us, length us, event | category | flops | bytes accessed | tf_op | source)
XLA Modules:
  0.0 98.4 jit_solution(17392716798215590881)
XLA Ops:
  0.6 0.0 copy-start
  1.4 17.6 %shard_map.157 = bf16[512,512]{1,0:T(8,128)(2,1)} custom-call(s32[128]{0:T(128)} %cache_len_ref.1, s32[1]{0:T(128)S(6)} %copy.23.group_len_ref, bf16[512,1024]{1,0:T(8,128)(2,1)} %mid_ref.1, bf16[1024,512]{1,0:T(8,128)(2,1)} %wq_ref.1, bf16[1024,512]{1,0:T(8,128)(2,1)} %wk_ref.1, bf16[1024,512]{1,0:T(8,128)(2,1)} %wv_ref.1, bf16[1024,512]{1,0:T(8,128)(2,1)} %bitcast.16, ...), custom_call_target="tpu_custom_call" | custom-call | flops 4831838208 | bytes 6815744 | tf_op jit(solution)/shard_map/pallas_call | solution.py:77
  19.0 0.0 copy-start.4
  19.0 0.0 copy-start.5
  19.0 2.1 %convolution_convert_fusion.1.own_ref = bf16[512,1024]{1,0:T(8,128)(2,1)S(1)} fusion(bf16[512,512]{1,0:T(8,128)(2,1)} %shard_map.157, bf16[512,1024]{1,0:T(8,128)(2,1)} %param.22), kind=kOutput, calls=%fused_computation.20 | convolution fusion | flops 537395200 | bytes 2621440 | tf_op jit(solution)/shard_map/dot_general | solution.py:151
  21.1 0.0 copy-start.2
  21.2 3.3 %collective-permute-start = (bf16[512,1024]{1,0:T(8,128)(2,1)S(1)}, bf16[512,1024]{1,0:T(8,128)(2,1)S(1)}, u32[]{:S(2)}, u32[]{:S(2)}) collective-permute-start(bf16[512,1024]{1,0:T(8,128)(2,1)S(1)} %convolution_convert_fusion.1.own_ref), channel_id=1, source_target_pairs={{0,1},{1,0},{2,3},{3,2},{4,5},{5,4},{6,7},{7,6},{8,9},{9,8},{10,11... | collective-permute-start | bytes 3145736 | tf_op jit(solution)/shard_map/ppermute | solution.py:152
  24.4 0.0 copy-done.4
  24.4 0.0 copy-done.5
  24.4 0.6 fusion.73
  25.1 1.7 %collective-permute-done.other_ref = bf16[512,1024]{1,0:T(8,128)(2,1)S(1)} collective-permute-done((bf16[512,1024]{1,0:T(8,128)(2,1)S(1)}, bf16[512,1024]{1,0:T(8,128)(2,1)S(1)}, u32[]{:S(2)}, u32[]{:S(2)}) %collective-permute-start) | collective-permute-done | bytes 1048608 | tf_op jit(solution)/shard_map/ppermute | solution.py:152
  26.7 0.0 copy-start.3
  26.7 1.0 %copy-done.3 = bf16[512,1024]{1,0:T(8,128)(2,1)} copy-done((bf16[512,1024]{1,0:T(8,128)(2,1)}, bf16[512,1024]{1,0:T(8,128)(2,1)S(1)}, u32[]{:S(2)}) %copy-start.3) | copy-done | bytes 1048600
  27.8 0.0 copy-done.2
  27.8 3.2 %shard_map.158.mid_ref = bf16[512,1024]{1,0:T(8,128)(2,1)} custom-call(bf16[512,1024]{1,0:T(8,128)(2,1)} %mid_ref.1, bf16[512,1024]{1,0:T(8,128)(2,1)} %copy-done.2, bf16[512,1024]{1,0:T(8,128)(2,1)} %copy-done.3, f32[1,1024]{1,0:T(1,128)} %get-tuple-element.7.gain_ref, f32[1,1024]{1,0:T(1,128)} %get-tuple-element.4.bias_ref), custom_call_target="tpu_custom_call" | custom-call | flops 5242880 | bytes 4194304 | tf_op jit(solution)/shard_map/pallas_call | solution.py:118
  30.9 0.0 copy-done
  30.9 8.2 %convolution_convert_fusion.own_ref = bf16[512,1024]{1,0:T(8,128)(2,1)S(1)} fusion(bf16[1024,1024]{1,0:T(8,128)(2,1)S(1)} %copy-done, bf16[512,1024]{1,0:T(8,128)(2,1)} %shard_map.158.mid_ref, bf16[1024,1024]{1,0:T(8,128)(2,1)} %param.23), kind=kOutput, calls=%fused_computation.19 | convolution fusion | flops 2182086656 | bytes 6291456 | tf_op jit(solution)/shard_map/dot_general | solution.py:157
  39.1 0.0 copy-start.1
  39.1 0.6 collective-permute-start.1
  39.8 2.4 %collective-permute-done.1.other_ref = bf16[512,1024]{1,0:T(8,128)(2,1)} collective-permute-done((bf16[512,1024]{1,0:T(8,128)(2,1)S(1)}, bf16[512,1024]{1,0:T(8,128)(2,1)}, u32[]{:S(2)}, u32[]{:S(2)}) %collective-permute-start.1) | collective-permute-done | bytes 1048608 | tf_op jit(solution)/shard_map/ppermute | solution.py:158
  42.2 0.0 copy-done.1
  42.2 3.2 %shard_map.159 = bf16[512,1024]{1,0:T(8,128)(2,1)} custom-call(bf16[512,1024]{1,0:T(8,128)(2,1)} %shard_map.158.mid_ref, bf16[512,1024]{1,0:T(8,128)(2,1)} %copy-done.1, bf16[512,1024]{1,0:T(8,128)(2,1)} %collective-permute-done.1.other_ref, f32[1,1024]{1,0:T(1,128)} %get-tuple-element.8.gain_ref, f32[1,1024]{1,0:T(1,128)} %get-tuple-element.3.bias_ref), custom_call_target="tpu_custom_call" | custom-call | flops 5242880 | bytes 4194304 | tf_op jit(solution)/shard_map/pallas_call | solution.py:118
  45.4 0.0 copy-start.7
  45.4 0.8 dynamic-slice_reduce_fusion
  46.2 0.3 broadcast_in_dim.11
  46.5 0.5 broadcast.13
  47.0 2.1 %reduce.4 = bf16[128,1024]{1,0:T(8,128)(2,1)S(1)} reduce(bf16[128,1,1024]{2,1,0:T(2,128)(2,1)S(1)} %broadcast_in_dim.11, bf16[]{:T(256)} %broadcast.13), dimensions={1}, to_apply=%broadcast_in_dim.11.reduce_sub_computation | reduce | bytes 524290 | tf_op jit(solution)/shard_map/broadcast_in_dim | solution.py:163
  49.1 0.2 reshape.21
  49.3 27.7 %all_to_all.19 = bf16[128,2,512]{2,1,0:T(2,128)(2,1)S(1)} all-to-all(bf16[128,2,512]{2,1,0:T(2,128)(2,1)S(1)} %reshape.21), channel_id=1, replica_groups=mesh['req'=128,'tp'=2] {'req'}, dimensions={0} | all-to-all | bytes 524288 | tf_op jit(solution)/shard_map/all_to_all | solution.py:162
  77.1 0.2 reshape.22
  77.3 0.0 copy-done.7
  77.3 0.3 convolution_reduce_fusion
  77.6 0.0 copy-start.6
  77.6 0.1 broadcast_in_dim.12
  77.7 0.2 all_to_all.16
  77.8 19.7 %all_to_all.20 = f32[256,1,1]{2,1,0:T(1,128)S(1)} all-to-all(f32[256,1,1]{2,1,0:T(1,128)S(1)} %all_to_all.16), channel_id=1, replica_groups=mesh['req'=128,'tp'=2] {'req','tp'}, dimensions={0} | all-to-all | bytes 2048 | tf_op jit(solution)/shard_map/all_to_all | solution.py:168
  97.5 0.9 reduce_max.21
  98.4 0.0 copy-done.6
Async XLA Ops:
  0.6 30.3 %copy-start = (bf16[1024,1024]{1,0:T(8,128)(2,1)S(1)}, bf16[1024,1024]{1,0:T(8,128)(2,1)}, u32[]{:S(2)}) copy-start(bf16[1024,1024]{1,0:T(8,128)(2,1)} %param.24) | copy-start | bytes 6291460
  19.0 5.4 %copy-start.4 = (f32[2,1024]{1,0:T(2,128)S(1)}, f32[2,1024]{1,0:T(2,128)}, u32[]{:S(2)}) copy-start(f32[2,1024]{1,0:T(2,128)} %param.26) | copy-start | bytes 24580
  19.0 5.4 %copy-start.5 = (f32[2,1024]{1,0:T(2,128)S(1)}, f32[2,1024]{1,0:T(2,128)}, u32[]{:S(2)}) copy-start(f32[2,1024]{1,0:T(2,128)} %param.25) | copy-start | bytes 24580
  21.1 6.6 %copy-start.2 = (bf16[512,1024]{1,0:T(8,128)(2,1)}, bf16[512,1024]{1,0:T(8,128)(2,1)S(1)}, u32[]{:S(2)}) copy-start(bf16[512,1024]{1,0:T(8,128)(2,1)S(1)} %convolution_convert_fusion.1.own_ref) | copy-start | bytes 3145732
  21.2 5.6 %collective-permute-start = (bf16[512,1024]{1,0:T(8,128)(2,1)S(1)}, bf16[512,1024]{1,0:T(8,128)(2,1)S(1)}, u32[]{:S(2)}, u32[]{:S(2)}) collective-permute-start(bf16[512,1024]{1,0:T(8,128)(2,1)S(1)} %convolution_convert_fusion.1.own_ref), channel_id=1, source_target_pairs={{0,1},{1,0},{2,3},{3,2},{4,5},{5,4},{6,7},{7,6},{8,9},{9,8},{10,11... | collective-permute-start | bytes 3145736 | tf_op jit(solution)/shard_map/ppermute | solution.py:152
  26.7 1.0 %copy-start.3 = (bf16[512,1024]{1,0:T(8,128)(2,1)}, bf16[512,1024]{1,0:T(8,128)(2,1)S(1)}, u32[]{:S(2)}) copy-start(bf16[512,1024]{1,0:T(8,128)(2,1)S(1)} %collective-permute-done.other_ref) | copy-start | bytes 3145732
  39.1 3.1 %copy-start.1 = (bf16[512,1024]{1,0:T(8,128)(2,1)}, bf16[512,1024]{1,0:T(8,128)(2,1)S(1)}, u32[]{:S(2)}) copy-start(bf16[512,1024]{1,0:T(8,128)(2,1)S(1)} %convolution_convert_fusion.own_ref) | copy-start | bytes 3145732
  39.1 3.1 %collective-permute-start.1 = (bf16[512,1024]{1,0:T(8,128)(2,1)S(1)}, bf16[512,1024]{1,0:T(8,128)(2,1)}, u32[]{:S(2)}, u32[]{:S(2)}) collective-permute-start(bf16[512,1024]{1,0:T(8,128)(2,1)S(1)} %convolution_convert_fusion.own_ref), channel_id=1, source_target_pairs={{0,1},{1,0},{2,3},{3,2},{4,5},{5,4},{6,7},{7,6},{8,9},{9,8},{10,11... | collective-permute-start | bytes 3145736 | tf_op jit(solution)/shard_map/ppermute | solution.py:158
  45.4 31.9 %copy-start.7 = (bf16[192,1024]{1,0:T(8,128)(2,1)S(1)}, bf16[192,1024]{1,0:T(8,128)(2,1)}, u32[]{:S(2)}) copy-start(bf16[192,1024]{1,0:T(8,128)(2,1)} %param.27) | copy-start | bytes 1179652
  77.6 20.8 %copy-start.6 = (f32[128]{0:T(128)}, f32[128]{0:T(128)S(1)}, u32[]{:S(2)}) copy-start(f32[128]{0:T(128)S(1)} %convolution_reduce_fusion) | copy-start | bytes 1540

commit v13 on v11

--- a/solution.py
+++ b/solution.py
@@ -24,7 +24,9 @@
 ROWS = 256
 
 
-def attention_kernel(cache_len_ref, group_len_ref, x_ref, wq_ref, wk_ref, wv_ref, kc_ref, vc_ref, out_ref):
+def attention_kernel(
+    cache_len_ref, group_len_ref, x_ref, wq_ref, wk_ref, wv_ref, kc_ref, vc_ref, wo_ref, out_ref, acc_ref
+):
     cached = cache_len_ref[lax.axis_index("req")]
     valid = group_len_ref[0]
     x = x_ref[...]
@@ -33,6 +35,13 @@
     vn = jnp.dot(x, wv_ref[...], preferred_element_type=jnp.float32).astype(jnp.bfloat16)
     kc = kc_ref[...]
     vc = vc_ref[...]
+    wo = wo_ref[...]
+    pair = pl.program_id(0)
+
+    @pl.when(pair == 0)
+    def _():
+        acc_ref[...] = jnp.zeros_like(acc_ref)
+
     scale = 1.0 / float(HD) ** 0.5
     dims = (((1,), (1,)), ((), ()))
     for chunk in range(x.shape[0] // ROWS):
@@ -65,10 +74,16 @@
                 e_c.astype(jnp.bfloat16), vc, preferred_element_type=jnp.float32
             ) + jnp.dot(e_n.astype(jnp.bfloat16), vn_seen, preferred_element_type=jnp.float32)
             result = jnp.where(mine, mixed / total, result)
-        out_ref[row0 : row0 + ROWS, :] = result.astype(out_ref.dtype)
-
-
-def attention(cache_len, group_len, tokens, w_query, w_key, w_value, cache_k, cache_v):
+        acc_ref[row0 : row0 + ROWS, :] += jnp.dot(
+            result.astype(jnp.bfloat16), wo, preferred_element_type=jnp.float32
+        )
+
+    @pl.when(pair == pl.num_programs(0) - 1)
+    def _():
+        out_ref[...] = acc_ref[...].astype(out_ref.dtype)
+
+
+def attention(cache_len, group_len, tokens, w_query, w_key, w_value, cache_k, cache_v, w_out):
     rows, model = tokens.shape
     width = w_query.shape[1]
     cache_rows = cache_k.shape[0]
@@ -76,7 +91,7 @@
     flops = 4 * rows * (cache_rows + rows) * width * 2 + 6 * rows * model * width
     return pl.pallas_call(
         attention_kernel,
-        out_shape=jax.ShapeDtypeStruct((rows, width), jnp.bfloat16),
+        out_shape=jax.ShapeDtypeStruct((rows, model), jnp.bfloat16),
         grid_spec=pltpu.PrefetchScalarGridSpec(
             num_scalar_prefetch=2,
             grid=(pairs,),
@@ -87,15 +102,17 @@
                 pl.BlockSpec((model, PAIR), lambda p, c, g: (0, p)),
                 pl.BlockSpec((cache_rows, PAIR), lambda p, c, g: (0, p)),
                 pl.BlockSpec((cache_rows, PAIR), lambda p, c, g: (0, p)),
+                pl.BlockSpec((PAIR, model), lambda p, c, g: (p, 0)),
             ],
-            out_specs=pl.BlockSpec((rows, PAIR), lambda p, c, g: (0, p)),
+            out_specs=pl.BlockSpec((rows, model), lambda p, c, g: (0, 0)),
+            scratch_shapes=[pltpu.VMEM((rows, model), jnp.float32)],
         ),
         cost_estimate=pl.CostEstimate(
             flops=flops,
             transcendentals=rows * (cache_rows + rows) * width // HD,
             bytes_accessed=2 * (rows * model + 3 * model * width + 2 * cache_rows * width + rows * width),
         ),
-    )(cache_len, group_len, tokens, w_query, w_key, w_value, cache_k, cache_v)
+    )(cache_len, group_len, tokens, w_query, w_key, w_value, cache_k, cache_v, w_out)
 
 
 NORM_ROWS = 256
@@ -147,8 +164,10 @@
     local_width = w_query.shape[1]
     my_index = lax.axis_index("req")
     my_valid = group_len[0]
-    attn_mixed = attention(cache_len, group_len, tokens, w_query, w_key, w_value, cache_keys[0], cache_values[0])
-    attn_sum = pair_sum(jnp.dot(attn_mixed, w_out, preferred_element_type=jnp.float32))
+    attn_own = attention(
+        cache_len, group_len, tokens, w_query, w_key, w_value, cache_keys[0], cache_values[0], w_out
+    )
+    attn_sum = pair_sum(attn_own)
     middle = normalize(tokens.astype(jnp.float32) + attn_sum, ln_gains[0], ln_biases[0]).astype(
         jnp.bfloat16
     )

time: 97.4 us -> 102 us (1.047)
  Pallas kernels: 20.9 us -> 26.1 us
  matrix products: 11.4 us -> 8.44 us
  other arithmetic: 4.81 us -> 7.06 us
    pallas_call x1, Pallas kernels: 17.7 us -> 22.9 us  [attention(): pl.pallas_call(attention_kernel, out_shape=jax.ShapeDtypeStruct((rows, mo...]
    dot_general x1 -> x0, matrix products: 1.84 us -> none  [shards(): jnp.dot(attn_mixed, w_out, preferred_element_type=jnp.float32)]
    reduce_sum x1, other arithmetic: 0.48 us -> 1.73 us  [normalize(): center = rows - jnp.mean(rows, axis=-1, keepdims=True)]
    dot_general x1, matrix products: 9.24 us -> 8.15 us  [shards(): jnp.dot(active, w_down, preferred_element_type=jnp.float32)]
where the time goes in v13:
time: 102 us; the launch traced here: 101 us
  blocking collectives  47.4 us (46%)
  Pallas kernels  26.1 us (26%)
  matrix products  8.44 us (8%)
  other arithmetic  7.06 us (7%)
  waiting for transfers between devices  4.3 us (4%)
  starting transfers between devices  3.66 us (4%)
  local copies, waits for them, and re-layouts  2.86 us (3%)
  between operations  1.55 us (2%)
    all_to_all x1, blocking collectives, shards(): lax.all_to_all(jnp.broadcast_to(last_row, (reqs, last_row.shape[1])), 're...  27.7 us
    pallas_call x1, Pallas kernels, attention(): pl.pallas_call(attention_kernel, out_shape=jax.ShapeDtypeStruct((rows, mo...  22.9 us
    all_to_all x1, blocking collectives, shards(): lax.all_to_all(spread, ('req', 'tp'), 0, 0, tiled=True)  19.7 us
    dot_general x1, matrix products, shards(): jnp.dot(active, w_down, preferred_element_type=jnp.float32)  8.15 us
    pallas_call x1, Pallas kernels, residual_norm(): pl.pallas_call(residual_norm_kernel, out_shape=jax.ShapeDtypeStruct((rows...  3.22 us
    ppermute x1, starting transfers between devices, pair_sum(): other = lax.ppermute(own, 'tp', [(0, 1), (1, 0)])  3.2 us
    ppermute x1, waiting for transfers between devices, shards(): other = lax.ppermute(own, 'tp', [(0, 1), (1, 0)])  2.42 us
    broadcast_in_dim x1, other arithmetic, shards(): jnp.broadcast_to(last_row, (reqs, last_row.shape[1]))  2.15 us
  transfers between devices with their start and end apart: 2, of which 2 were waited for; matrix products, arithmetic and copies ran while one was open for 1% of the time, Pallas kernels for 0%

profile of v13, /device:TPU:1, one launch (start us, length us, event | category | flops | bytes accessed | tf_op | source)
XLA Modules:
  0.0 101.4 jit_solution(742779330081410397)
XLA Ops:
  0.6 0.0 copy-start
  1.4 0.0 copy-start.4
  1.5 0.0 copy-start.5
  1.5 0.0 copy-start.1
  1.5 22.9 %shard_map.157 = bf16[512,1024]{1,0:T(8,128)(2,1)} custom-call(s32[128]{0:T(128)} %cache_len_ref.1, s32[1]{0:T(128)S(6)} %copy.23.group_len_ref, bf16[512,1024]{1,0:T(8,128)(2,1)} %x_ref.1, bf16[1024,512]{1,0:T(8,128)(2,1)} %wq_ref.1, bf16[1024,512]{1,0:T(8,128)(2,1)} %wk_ref.1, bf16[1024,512]{1,0:T(8,128)(2,1)} %wv_ref.1, bf16[1024,512]{1,0:T(8,128)(2,1)} %bitcast.18, ...), custom_call_target="tpu_custom_call" | custom-call | flops 4831838208 | bytes 6815744 | tf_op jit(solution)/shard_map/pallas_call | solution.py:92
  24.4 0.0 copy-start.2
  24.4 3.2 %collective-permute-start = (bf16[512,1024]{1,0:T(8,128)(2,1)}, bf16[512,1024]{1,0:T(8,128)(2,1)S(1)}, u32[]{:S(2)}, u32[]{:S(2)}) collective-permute-start(bf16[512,1024]{1,0:T(8,128)(2,1)} %shard_map.157), channel_id=1, source_target_pairs={{0,1},{1,0},{2,3},{3,2},{4,5},{5,4},{6,7},{7,6},{8,9},{9,8},{10,11... | collective-permute-start | bytes 3145736 | tf_op jit(solution)/shard_map/ppermute | solution.py:19
  27.6 0.0 copy-done.4
  27.6 0.0 copy-done.5
  27.6 0.6 fusion.74
  28.2 1.9 %collective-permute-done = bf16[512,1024]{1,0:T(8,128)(2,1)S(1)} collective-permute-done((bf16[512,1024]{1,0:T(8,128)(2,1)}, bf16[512,1024]{1,0:T(8,128)(2,1)S(1)}, u32[]{:S(2)}, u32[]{:S(2)}) %collective-permute-start) | collective-permute-done | bytes 1048608 | tf_op jit(solution)/shard_map/ppermute | solution.py:19
  30.1 0.0 copy-done.1
  30.1 1.7 %fusion.41 = f32[512]{0:T(512)S(1)} fusion(bf16[512,1024]{1,0:T(8,128)(2,1)S(1)} %collective-permute-done, bf16[512,1024]{1,0:T(8,128)(2,1)} %shard_map.157, bf16[512,1024]{1,0:T(8,128)(2,1)S(1)} %copy-done.1), kind=kLoop, calls=%fused_computation.54 | loop fusion | flops 3145216 | bytes 3147776 | tf_op jit(solution)/shard_map/reduce_sum | solution.py:12
  31.8 0.0 copy-done.2
  31.8 0.6 multiply_reduce_fusion
  32.5 1.7 %add_convert_fusion.mid_ref = bf16[512,1024]{1,0:T(8,128)(2,1)} fusion(f32[1024]{0:T(1024)S(1)} %bitcast.15, f32[1024]{0:T(1024)S(1)} %bitcast.16, f32[512]{0:T(512)S(1)} %add_rsqrt_fusion, f32[512]{0:T(512)S(1)} %broadcast_multiply_fusion, bf16[512,1024]{1,0:T(8,128)(2,1)S(1)} %collective-permute-done, bf16[512,1024]{1,0:T(8,128)(2,1)S(1)} %copy-done.2, ...), kind=kLoop, calls=%fused_computation.17 | loop fusion | flops 5242880 | bytes 4206592 | tf_op jit(solution)/shard_map/convert_element_type | solution.py:171
  34.1 0.0 copy-done
  34.1 8.2 %convolution_convert_fusion.own_ref = bf16[512,1024]{1,0:T(8,128)(2,1)S(1)} fusion(bf16[1024,1024]{1,0:T(8,128)(2,1)S(1)} %copy-done, bf16[512,1024]{1,0:T(8,128)(2,1)} %add_convert_fusion.mid_ref, bf16[1024,1024]{1,0:T(8,128)(2,1)} %param.23), kind=kOutput, calls=%fused_computation.22 | convolution fusion | flops 2182086656 | bytes 6291456 | tf_op jit(solution)/shard_map/dot_general | solution.py:177
  42.3 0.0 copy-start.3
  42.3 0.5 collective-permute-start.1
  42.8 2.4 %collective-permute-done.1.other_ref = bf16[512,1024]{1,0:T(8,128)(2,1)} collective-permute-done((bf16[512,1024]{1,0:T(8,128)(2,1)S(1)}, bf16[512,1024]{1,0:T(8,128)(2,1)}, u32[]{:S(2)}, u32[]{:S(2)}) %collective-permute-start.1) | collective-permute-done | bytes 1048608 | tf_op jit(solution)/shard_map/ppermute | solution.py:178
  45.2 0.0 copy-done.3
  45.2 3.2 %shard_map.158 = bf16[512,1024]{1,0:T(8,128)(2,1)} custom-call(bf16[512,1024]{1,0:T(8,128)(2,1)} %add_convert_fusion.mid_ref, bf16[512,1024]{1,0:T(8,128)(2,1)} %copy-done.3, bf16[512,1024]{1,0:T(8,128)(2,1)} %collective-permute-done.1.other_ref, f32[1,1024]{1,0:T(1,128)} %get-tuple-element.8.gain_ref, f32[1,1024]{1,0:T(1,128)} %get-tuple-element.3.bias_ref), custom_call_target="tpu_custom_call" | custom-call | flops 5242880 | bytes 4194304 | tf_op jit(solution)/shard_map/pallas_call | solution.py:135
  48.4 0.0 copy-start.7
  48.4 0.8 dynamic-slice_reduce_fusion
  49.2 0.3 broadcast_in_dim.6
  49.5 0.5 broadcast.36
  50.0 2.1 %reduce.4 = bf16[128,1024]{1,0:T(8,128)(2,1)S(1)} reduce(bf16[128,1,1024]{2,1,0:T(2,128)(2,1)S(1)} %broadcast_in_dim.6, bf16[]{:T(256)} %broadcast.36), dimensions={1}, to_apply=%broadcast_in_dim.6.reduce_sub_computation | reduce | bytes 524290 | tf_op jit(solution)/shard_map/broadcast_in_dim | solution.py:183
  52.2 0.2 reshape.33
  52.3 27.7 %all_to_all.19 = bf16[128,2,512]{2,1,0:T(2,128)(2,1)S(1)} all-to-all(bf16[128,2,512]{2,1,0:T(2,128)(2,1)S(1)} %reshape.33), channel_id=1, replica_groups=mesh['req'=128,'tp'=2] {'req'}, dimensions={0} | all-to-all | bytes 524288 | tf_op jit(solution)/shard_map/all_to_all | solution.py:182
  80.1 0.2 reshape.34
  80.3 0.0 copy-done.7
  80.3 0.3 convolution_reduce_fusion
  80.6 0.0 copy-start.6
  80.6 0.1 broadcast_in_dim.14
  80.7 0.2 all_to_all.16
  80.8 19.7 %all_to_all.20 = f32[256,1,1]{2,1,0:T(1,128)S(1)} all-to-all(f32[256,1,1]{2,1,0:T(1,128)S(1)} %all_to_all.16), channel_id=1, replica_groups=mesh['req'=128,'tp'=2] {'req','tp'}, dimensions={0} | all-to-all | bytes 2048 | tf_op jit(solution)/shard_map/all_to_all | solution.py:188
  100.5 0.9 reduce_max.21
  101.4 0.0 copy-done.6
  (2 shorter events, 0.0 us)
Async XLA Ops:
  0.6 33.5 %copy-start = (bf16[1024,1024]{1,0:T(8,128)(2,1)S(1)}, bf16[1024,1024]{1,0:T(8,128)(2,1)}, u32[]{:S(2)}) copy-start(bf16[1024,1024]{1,0:T(8,128)(2,1)} %param.24) | copy-start | bytes 6291460
  1.4 26.1 %copy-start.4 = (f32[2,1024]{1,0:T(2,128)S(1)}, f32[2,1024]{1,0:T(2,128)}, u32[]{:S(2)}) copy-start(f32[2,1024]{1,0:T(2,128)} %param.26) | copy-start | bytes 24580
  1.5 26.1 %copy-start.5 = (f32[2,1024]{1,0:T(2,128)S(1)}, f32[2,1024]{1,0:T(2,128)}, u32[]{:S(2)}) copy-start(f32[2,1024]{1,0:T(2,128)} %param.25) | copy-start | bytes 24580
  1.5 28.6 %copy-start.1 = (bf16[512,1024]{1,0:T(8,128)(2,1)S(1)}, bf16[512,1024]{1,0:T(8,128)(2,1)}, u32[]{:S(2)}) copy-start(bf16[512,1024]{1,0:T(8,128)(2,1)} %x_ref.1) | copy-start | bytes 3145732
  24.4 7.4 %copy-start.2 = (bf16[512,1024]{1,0:T(8,128)(2,1)S(1)}, bf16[512,1024]{1,0:T(8,128)(2,1)}, u32[]{:S(2)}) copy-start(bf16[512,1024]{1,0:T(8,128)(2,1)} %shard_map.157) | copy-start | bytes 3145732
  24.4 5.7 %collective-permute-start = (bf16[512,1024]{1,0:T(8,128)(2,1)}, bf16[512,1024]{1,0:T(8,128)(2,1)S(1)}, u32[]{:S(2)}, u32[]{:S(2)}) collective-permute-start(bf16[512,1024]{1,0:T(8,128)(2,1)} %shard_map.157), channel_id=1, source_target_pairs={{0,1},{1,0},{2,3},{3,2},{4,5},{5,4},{6,7},{7,6},{8,9},{9,8},{10,11... | collective-permute-start | bytes 3145736 | tf_op jit(solution)/shard_map/ppermute | solution.py:19
  42.3 2.9 %copy-start.3 = (bf16[512,1024]{1,0:T(8,128)(2,1)}, bf16[512,1024]{1,0:T(8,128)(2,1)S(1)}, u32[]{:S(2)}) copy-start(bf16[512,1024]{1,0:T(8,128)(2,1)S(1)} %convolution_convert_fusion.own_ref) | copy-start | bytes 3145732
  42.3 2.9 %collective-permute-start.1 = (bf16[512,1024]{1,0:T(8,128)(2,1)S(1)}, bf16[512,1024]{1,0:T(8,128)(2,1)}, u32[]{:S(2)}, u32[]{:S(2)}) collective-permute-start(bf16[512,1024]{1,0:T(8,128)(2,1)S(1)} %convolution_convert_fusion.own_ref), channel_id=1, source_target_pairs={{0,1},{1,0},{2,3},{3,2},{4,5},{5,4},{6,7},{7,6},{8,9},{9,8},{10,11... | collective-permute-start | bytes 3145736 | tf_op jit(solution)/shard_map/ppermute | solution.py:178
  48.4 31.9 %copy-start.7 = (bf16[192,1024]{1,0:T(8,128)(2,1)S(1)}, bf16[192,1024]{1,0:T(8,128)(2,1)}, u32[]{:S(2)}) copy-start(bf16[192,1024]{1,0:T(8,128)(2,1)} %param.27) | copy-start | bytes 1179652
  80.6 20.8 %copy-start.6 = (f32[128]{0:T(128)}, f32[128]{0:T(128)S(1)}, u32[]{:S(2)}) copy-start(f32[128]{0:T(128)S(1)} %convolution_reduce_fusion) | copy-start | bytes 1540

commit v14 on v11

--- a/solution.py
+++ b/solution.py
@@ -98,7 +98,7 @@
     )(cache_len, group_len, tokens, w_query, w_key, w_value, cache_k, cache_v)
 
 
-NORM_ROWS = 256
+NORM_ROWS = 128
 
 
 def residual_norm_kernel(mid_ref, own_ref, other_ref, gain_ref, bias_ref, out_ref):

time: 97.4 us -> 98.4 us (1.010)
  Pallas kernels: 20.9 us -> 21.9 us
    pallas_call x1, Pallas kernels: 3.22 us -> 4.25 us  [residual_norm(): pl.pallas_call(residual_norm_kernel, out_shape=jax.ShapeDtypeStruct((rows...]
where the time goes in v14:
time: 98.4 us; the launch traced here: 98.1 us
  blocking collectives  47.4 us (48%)
  Pallas kernels  21.9 us (22%)
  matrix products  11.4 us (12%)
  other arithmetic  4.81 us (5%)
  waiting for transfers between devices  4.3 us (4%)
  starting transfers between devices  3.85 us (4%)
  local copies, waits for them, and re-layouts  2.86 us (3%)
  between operations  1.55 us (2%)
    all_to_all x1, blocking collectives, shards(): lax.all_to_all(jnp.broadcast_to(last_row, (reqs, last_row.shape[1])), 're...  27.7 us
    all_to_all x1, blocking collectives, shards(): lax.all_to_all(spread, ('req', 'tp'), 0, 0, tiled=True)  19.7 us
    pallas_call x1, Pallas kernels, attention(): pl.pallas_call(attention_kernel, out_shape=jax.ShapeDtypeStruct((rows, wi...  17.7 us
    dot_general x1, matrix products, shards(): jnp.dot(active, w_down, preferred_element_type=jnp.float32)  9.24 us
    pallas_call x1, Pallas kernels, residual_norm(): pl.pallas_call(residual_norm_kernel, out_shape=jax.ShapeDtypeStruct((rows...  4.25 us
    ppermute x1, starting transfers between devices, pair_sum(): other = lax.ppermute(own, 'tp', [(0, 1), (1, 0)])  3.47 us
    ppermute x1, waiting for transfers between devices, shards(): other = lax.ppermute(own, 'tp', [(0, 1), (1, 0)])  2.63 us
    broadcast_in_dim x1, other arithmetic, shards(): jnp.broadcast_to(last_row, (reqs, last_row.shape[1]))  2.15 us
  transfers between devices with their start and end apart: 2, of which 2 were waited for; matrix products, arithmetic and copies ran while one was open for 1% of the time, Pallas kernels for 0%

profile of v14, /device:TPU:1, one launch (start us, length us, event | category | flops | bytes accessed | tf_op | source)
XLA Modules:
  0.0 98.1 jit_solution(9082939044076189795)
XLA Ops:
  0.6 0.0 copy-start
  1.4 0.0 copy-start.6
  1.5 17.7 %shard_map.157 = bf16[512,512]{1,0:T(8,128)(2,1)} custom-call(s32[128]{0:T(128)} %cache_len_ref.1, s32[1]{0:T(128)S(6)} %copy.23.group_len_ref, bf16[512,1024]{1,0:T(8,128)(2,1)} %x_ref.1, bf16[1024,512]{1,0:T(8,128)(2,1)} %wq_ref.1, bf16[1024,512]{1,0:T(8,128)(2,1)} %wk_ref.1, bf16[1024,512]{1,0:T(8,128)(2,1)} %wv_ref.1, bf16[1024,512]{1,0:T(8,128)(2,1)} %bitcast.20, ...), custom_call_target="tpu_custom_call" | custom-call | flops 4831838208 | bytes 6815744 | tf_op jit(solution)/shard_map/pallas_call | solution.py:77
  19.1 0.0 copy-done.6
  19.1 0.0 copy-start.3
  19.2 0.0 copy-start.4
  19.2 0.0 copy-start.1
  19.2 1.8 %convolution_convert_fusion.1 = bf16[512,1024]{1,0:T(8,128)(2,1)S(1)} fusion(bf16[512,512]{1,0:T(8,128)(2,1)} %shard_map.157, bf16[512,1024]{1,0:T(8,128)(2,1)S(1)} %copy-done.6), kind=kOutput, calls=%fused_computation.23 | convolution fusion | flops 537395200 | bytes 2621440 | tf_op jit(solution)/shard_map/dot_general | solution.py:151
  21.0 3.5 %collective-permute-start = (bf16[512,1024]{1,0:T(8,128)(2,1)S(1)}, bf16[512,1024]{1,0:T(8,128)(2,1)S(1)}, u32[]{:S(2)}, u32[]{:S(2)}) collective-permute-start(bf16[512,1024]{1,0:T(8,128)(2,1)S(1)} %convolution_convert_fusion.1), channel_id=1, source_target_pairs={{0,1},{1,0},{2,3},{3,2},{4,5},{5,4},{6,7},{7,6},{8,9},{9,8},{10,11... | collective-permute-start | bytes 3145736 | tf_op jit(solution)/shard_map/ppermute | solution.py:19
  24.5 0.0 copy-done.3
  24.5 0.0 copy-done.4
  24.5 0.6 fusion.74
  25.1 1.7 %collective-permute-done = bf16[512,1024]{1,0:T(8,128)(2,1)S(1)} collective-permute-done((bf16[512,1024]{1,0:T(8,128)(2,1)S(1)}, bf16[512,1024]{1,0:T(8,128)(2,1)S(1)}, u32[]{:S(2)}, u32[]{:S(2)}) %collective-permute-start) | collective-permute-done | bytes 1048608 | tf_op jit(solution)/shard_map/ppermute | solution.py:19
  26.8 0.0 copy-done.1
  26.8 0.5 fusion.41
  27.3 0.6 multiply_reduce_fusion
  27.9 0.7 add_convert_fusion.mid_ref
  28.6 0.0 copy-done
  28.6 0.0 copy-start.2
  28.6 9.2 %convolution_convert_fusion.own_ref = bf16[512,1024]{1,0:T(8,128)(2,1)} fusion(bf16[1024,1024]{1,0:T(8,128)(2,1)S(1)} %copy-done, bf16[512,1024]{1,0:T(8,128)(2,1)S(1)} %add_convert_fusion.mid_ref, bf16[1024,1024]{1,0:T(8,128)(2,1)} %param.23), kind=kOutput, calls=%fused_computation.22 | convolution fusion | flops 2182086656 | bytes 6291456 | tf_op jit(solution)/shard_map/dot_general | solution.py:158
  37.8 0.0 copy-done.2
  37.9 0.4 collective-permute-start.1
  38.2 2.6 %collective-permute-done.1.other_ref = bf16[512,1024]{1,0:T(8,128)(2,1)} collective-permute-done((bf16[512,1024]{1,0:T(8,128)(2,1)}, bf16[512,1024]{1,0:T(8,128)(2,1)}, u32[]{:S(2)}, u32[]{:S(2)}) %collective-permute-start.1) | collective-permute-done | bytes 1048608 | tf_op jit(solution)/shard_map/ppermute | solution.py:159
  40.9 4.2 %shard_map.158 = bf16[512,1024]{1,0:T(8,128)(2,1)} custom-call(bf16[512,1024]{1,0:T(8,128)(2,1)} %copy-done.2, bf16[512,1024]{1,0:T(8,128)(2,1)} %convolution_convert_fusion.own_ref, bf16[512,1024]{1,0:T(8,128)(2,1)} %collective-permute-done.1.other_ref, f32[1,1024]{1,0:T(1,128)} %get-tuple-element.8.gain_ref, f32[1,1024]{1,0:T(1,128)} %get-tuple-element.3.bias_ref), custom_call_target="tpu_custom_call" | custom-call | flops 5242880 | bytes 4194304 | tf_op jit(solution)/shard_map/pallas_call | solution.py:118
  45.1 0.0 copy-start.7
  45.1 0.8 dynamic-slice_reduce_fusion
  45.9 0.3 broadcast_in_dim.6
  46.2 0.5 broadcast.36
  46.7 2.1 %reduce.4 = bf16[128,1024]{1,0:T(8,128)(2,1)S(1)} reduce(bf16[128,1,1024]{2,1,0:T(2,128)(2,1)S(1)} %broadcast_in_dim.6, bf16[]{:T(256)} %broadcast.36), dimensions={1}, to_apply=%broadcast_in_dim.6.reduce_sub_computation | reduce | bytes 524290 | tf_op jit(solution)/shard_map/broadcast_in_dim | solution.py:164
  48.8 0.2 reshape.33
  49.0 27.7 %all_to_all.19 = bf16[128,2,512]{2,1,0:T(2,128)(2,1)S(1)} all-to-all(bf16[128,2,512]{2,1,0:T(2,128)(2,1)S(1)} %reshape.33), channel_id=1, replica_groups=mesh['req'=128,'tp'=2] {'req'}, dimensions={0} | all-to-all | bytes 524288 | tf_op jit(solution)/shard_map/all_to_all | solution.py:163
  76.8 0.2 reshape.34
  77.0 0.0 copy-done.7
  77.0 0.3 convolution_reduce_fusion
  77.3 0.0 copy-start.5
  77.3 0.1 broadcast_in_dim.14
  77.4 0.2 all_to_all.16
  77.5 19.7 %all_to_all.20 = f32[256,1,1]{2,1,0:T(1,128)S(1)} all-to-all(f32[256,1,1]{2,1,0:T(1,128)S(1)} %all_to_all.16), channel_id=1, replica_groups=mesh['req'=128,'tp'=2] {'req','tp'}, dimensions={0} | all-to-all | bytes 2048 | tf_op jit(solution)/shard_map/all_to_all | solution.py:169
  97.2 0.9 reduce_max.21
  98.1 0.0 copy-done.5
  (2 shorter events, 0.0 us)
Async XLA Ops:
  0.6 28.0 %copy-start = (bf16[1024,1024]{1,0:T(8,128)(2,1)S(1)}, bf16[1024,1024]{1,0:T(8,128)(2,1)}, u32[]{:S(2)}) copy-start(bf16[1024,1024]{1,0:T(8,128)(2,1)} %param.24) | copy-start | bytes 6291460
  1.4 17.7 %copy-start.6 = (bf16[512,1024]{1,0:T(8,128)(2,1)S(1)}, bf16[512,1024]{1,0:T(8,128)(2,1)}, u32[]{:S(2)}) copy-start(bf16[512,1024]{1,0:T(8,128)(2,1)} %param.22) | copy-start | bytes 3145732
  19.1 5.4 %copy-start.3 = (f32[2,1024]{1,0:T(2,128)S(1)}, f32[2,1024]{1,0:T(2,128)}, u32[]{:S(2)}) copy-start(f32[2,1024]{1,0:T(2,128)} %param.26) | copy-start | bytes 24580
  19.2 5.3 %copy-start.4 = (f32[2,1024]{1,0:T(2,128)S(1)}, f32[2,1024]{1,0:T(2,128)}, u32[]{:S(2)}) copy-start(f32[2,1024]{1,0:T(2,128)} %param.25) | copy-start | bytes 24580
  19.2 7.6 %copy-start.1 = (bf16[512,1024]{1,0:T(8,128)(2,1)S(1)}, bf16[512,1024]{1,0:T(8,128)(2,1)}, u32[]{:S(2)}) copy-start(bf16[512,1024]{1,0:T(8,128)(2,1)} %x_ref.1) | copy-start | bytes 3145732
  21.0 5.8 %collective-permute-start = (bf16[512,1024]{1,0:T(8,128)(2,1)S(1)}, bf16[512,1024]{1,0:T(8,128)(2,1)S(1)}, u32[]{:S(2)}, u32[]{:S(2)}) collective-permute-start(bf16[512,1024]{1,0:T(8,128)(2,1)S(1)} %convolution_convert_fusion.1), channel_id=1, source_target_pairs={{0,1},{1,0},{2,3},{3,2},{4,5},{5,4},{6,7},{7,6},{8,9},{9,8},{10,11... | collective-permute-start | bytes 3145736 | tf_op jit(solution)/shard_map/ppermute | solution.py:19
  28.6 9.3 %copy-start.2 = (bf16[512,1024]{1,0:T(8,128)(2,1)}, bf16[512,1024]{1,0:T(8,128)(2,1)S(1)}, u32[]{:S(2)}) copy-start(bf16[512,1024]{1,0:T(8,128)(2,1)S(1)} %add_convert_fusion.mid_ref) | copy-start | bytes 3145732
  37.9 3.0 %collective-permute-start.1 = (bf16[512,1024]{1,0:T(8,128)(2,1)}, bf16[512,1024]{1,0:T(8,128)(2,1)}, u32[]{:S(2)}, u32[]{:S(2)}) collective-permute-start(bf16[512,1024]{1,0:T(8,128)(2,1)} %convolution_convert_fusion.own_ref), channel_id=1, source_target_pairs={{0,1},{1,0},{2,3},{3,2},{4,5},{5,4},{6,7},{7,6},{8,9},{9,8},{10,11... | collective-permute-start | bytes 3145736 | tf_op jit(solution)/shard_map/ppermute | solution.py:159
  45.1 31.9 %copy-start.7 = (bf16[192,1024]{1,0:T(8,128)(2,1)S(1)}, bf16[192,1024]{1,0:T(8,128)(2,1)}, u32[]{:S(2)}) copy-start(bf16[192,1024]{1,0:T(8,128)(2,1)} %param.27) | copy-start | bytes 1179652
  77.3 20.8 %copy-start.5 = (f32[128]{0:T(128)}, f32[128]{0:T(128)S(1)}, u32[]{:S(2)}) copy-start(f32[128]{0:T(128)S(1)} %convolution_reduce_fusion) | copy-start | bytes 1540

commit v15 on v11

--- a/solution.py
+++ b/solution.py
@@ -101,7 +101,7 @@
 NORM_ROWS = 256
 
 
-def residual_norm_kernel(mid_ref, own_ref, other_ref, gain_ref, bias_ref, out_ref):
+def residual_norm_kernel(group_len_ref, mid_ref, own_ref, other_ref, gain_ref, bias_ref, out_ref, copies_ref):
     total = own_ref[...].astype(jnp.float32) + other_ref[...].astype(jnp.float32)
     rows = mid_ref[...].astype(jnp.float32) + total
     center = rows - jnp.mean(rows, axis=-1, keepdims=True)
@@ -109,22 +109,38 @@
     out_ref[...] = (center * lax.rsqrt(spread + 1e-05) * gain_ref[...] + bias_ref[...]).astype(
         out_ref.dtype
     )
-
-
-def residual_norm(middle, own, other, gain, bias):
+    last = group_len_ref[0] - 1
+
+    @pl.when(last // NORM_ROWS == pl.program_id(0))
+    def _():
+        within = last % NORM_ROWS
+        start = pl.multiple_of((within // 16) * 16, 16)
+        window = out_ref[pl.ds(start, 16), :].astype(jnp.float32)
+        pick = lax.broadcasted_iota(jnp.int32, window.shape, 0) == within - start
+        row = jnp.sum(jnp.where(pick, window, 0.0), axis=0, keepdims=True)
+        copies_ref[...] = jnp.broadcast_to(row, copies_ref.shape).astype(copies_ref.dtype)
+
+
+def residual_norm(group_len, middle, own, other, gain, bias, reqs):
     rows, width = middle.shape
-    block = pl.BlockSpec((NORM_ROWS, width), lambda i: (i, 0))
-    vector = pl.BlockSpec((1, width), lambda i: (0, 0))
+    block = pl.BlockSpec((NORM_ROWS, width), lambda i, g: (i, 0))
+    vector = pl.BlockSpec((1, width), lambda i, g: (0, 0))
     return pl.pallas_call(
         residual_norm_kernel,
-        out_shape=jax.ShapeDtypeStruct((rows, width), jnp.bfloat16),
-        grid=(rows // NORM_ROWS,),
-        in_specs=[block, block, block, vector, vector],
-        out_specs=block,
+        out_shape=(
+            jax.ShapeDtypeStruct((rows, width), jnp.bfloat16),
+            jax.ShapeDtypeStruct((reqs, width), jnp.bfloat16),
+        ),
+        grid_spec=pltpu.PrefetchScalarGridSpec(
+            num_scalar_prefetch=1,
+            grid=(rows // NORM_ROWS,),
+            in_specs=[block, block, block, vector, vector],
+            out_specs=(block, pl.BlockSpec((reqs, width), lambda i, g: (0, 0))),
+        ),
         cost_estimate=pl.CostEstimate(
             flops=10 * rows * width, transcendentals=rows, bytes_accessed=8 * rows * width
         ),
-    )(middle, own, other, gain, bias)
+    )(group_len, middle, own, other, gain, bias)
 
 
 def shards(
@@ -157,12 +173,11 @@
     ).astype(jnp.bfloat16)
     own = jnp.dot(active, w_down, preferred_element_type=jnp.float32).astype(jnp.bfloat16)
     other = lax.ppermute(own, "tp", [(0, 1), (1, 0)])
-    layer_out = residual_norm(middle, own, other, ln_gains[1:2], ln_biases[1:2])
-    last_row = lax.dynamic_slice_in_dim(layer_out, my_valid - 1, 1, 0)
+    layer_out, copies = residual_norm(
+        group_len, middle, own, other, ln_gains[1:2], ln_biases[1:2], cache_len.shape[0]
+    )
     reqs = cache_len.shape[0]
-    all_rows = lax.all_to_all(
-        jnp.broadcast_to(last_row, (reqs, last_row.shape[1])), "req", 0, 0, tiled=True
-    )
+    all_rows = lax.all_to_all(copies, "req", 0, 0, tiled=True)
     logits = jnp.einsum("rd,vd->rv", all_rows, embed, preferred_element_type=jnp.float32)
     slice_best = jnp.max(logits, axis=1)
     spread = jnp.repeat(slice_best, 2)[:, None]

time: 97.4 us -> 96 us (0.986)
  local copies, waits for them, and re-layouts: 2.86 us -> 1.79 us
    broadcast_in_dim x1 -> x0, other arithmetic: 2.15 us -> none  [shards(): jnp.broadcast_to(last_row, (reqs, last_row.shape[1]))]
    all_to_all x0 -> x1, other arithmetic: none -> 1.72 us  [shards(): all_rows = lax.all_to_all(copies, 'req', 0, 0, tiled=True)]
where the time goes in v15:
time: 96 us; the launch traced here: 95.7 us
  blocking collectives  47.4 us (49%)
  Pallas kernels  21 us (22%)
  matrix products  11.4 us (12%)
  other arithmetic  4.38 us (5%)
  waiting for transfers between devices  4.31 us (4%)
  starting transfers between devices  3.85 us (4%)
  local copies, waits for them, and re-layouts  1.79 us (2%)
  between operations  1.55 us (2%)
    all_to_all x1, blocking collectives, shards(): all_rows = lax.all_to_all(copies, 'req', 0, 0, tiled=True)  27.7 us
    all_to_all x1, blocking collectives, shards(): lax.all_to_all(spread, ('req', 'tp'), 0, 0, tiled=True)  19.7 us
    pallas_call x1, Pallas kernels, attention(): pl.pallas_call(attention_kernel, out_shape=jax.ShapeDtypeStruct((rows, wi...  17.7 us
    dot_general x1, matrix products, shards(): jnp.dot(active, w_down, preferred_element_type=jnp.float32)  9.24 us
    ppermute x1, starting transfers between devices, pair_sum(): other = lax.ppermute(own, 'tp', [(0, 1), (1, 0)])  3.47 us
    pallas_call x1, Pallas kernels, residual_norm(): pl.pallas_call(residual_norm_kernel, out_shape=(jax.ShapeDtypeStruct((row...  3.33 us
    ppermute x1, waiting for transfers between devices, shards(): other = lax.ppermute(own, 'tp', [(0, 1), (1, 0)])  2.63 us
  transfers between devices with their start and end apart: 2, of which 2 were waited for; matrix products, arithmetic and copies ran while one was open for 1% of the time, Pallas kernels for 0%

profile of v15, /device:TPU:1, one launch (start us, length us, event | category | flops | bytes accessed | tf_op | source)
XLA Modules:
  0.0 95.7 jit_solution(17422102135166218778)
XLA Ops:
  0.6 0.0 copy-start
  1.4 0.0 copy-start.6
  1.5 17.7 %shard_map.157 = bf16[512,512]{1,0:T(8,128)(2,1)} custom-call(s32[128]{0:T(128)} %cache_len_ref.1, s32[1]{0:T(128)S(6)} %copy.27.group_len_ref, bf16[512,1024]{1,0:T(8,128)(2,1)} %x_ref.1, bf16[1024,512]{1,0:T(8,128)(2,1)} %wq_ref.1, bf16[1024,512]{1,0:T(8,128)(2,1)} %wk_ref.1, bf16[1024,512]{1,0:T(8,128)(2,1)} %wv_ref.1, bf16[1024,512]{1,0:T(8,128)(2,1)} %bitcast.20, ...), custom_call_target="tpu_custom_call" | custom-call | flops 4831838208 | bytes 6815744 | tf_op jit(solution)/shard_map/pallas_call | solution.py:77
  19.1 0.0 copy-done.6
  19.1 0.0 copy-start.3
  19.2 0.0 copy-start.4
  19.2 0.0 copy-start.1
  19.2 1.8 %convolution_convert_fusion.1 = bf16[512,1024]{1,0:T(8,128)(2,1)S(1)} fusion(bf16[512,512]{1,0:T(8,128)(2,1)} %shard_map.157, bf16[512,1024]{1,0:T(8,128)(2,1)S(1)} %copy-done.6), kind=kOutput, calls=%fused_computation.23 | convolution fusion | flops 537395200 | bytes 2621440 | tf_op jit(solution)/shard_map/dot_general | solution.py:167
  21.0 3.5 %collective-permute-start = (bf16[512,1024]{1,0:T(8,128)(2,1)S(1)}, bf16[512,1024]{1,0:T(8,128)(2,1)S(1)}, u32[]{:S(2)}, u32[]{:S(2)}) collective-permute-start(bf16[512,1024]{1,0:T(8,128)(2,1)S(1)} %convolution_convert_fusion.1), channel_id=1, source_target_pairs={{0,1},{1,0},{2,3},{3,2},{4,5},{5,4},{6,7},{7,6},{8,9},{9,8},{10,11... | collective-permute-start | bytes 3145736 | tf_op jit(solution)/shard_map/ppermute | solution.py:19
  24.5 0.0 copy-done.3
  24.5 0.0 copy-done.4
  24.5 0.6 fusion.74
  25.1 1.7 %collective-permute-done = bf16[512,1024]{1,0:T(8,128)(2,1)S(1)} collective-permute-done((bf16[512,1024]{1,0:T(8,128)(2,1)S(1)}, bf16[512,1024]{1,0:T(8,128)(2,1)S(1)}, u32[]{:S(2)}, u32[]{:S(2)}) %collective-permute-start) | collective-permute-done | bytes 1048608 | tf_op jit(solution)/shard_map/ppermute | solution.py:19
  26.8 0.0 copy-done.1
  26.8 0.5 fusion.41
  27.3 0.6 multiply_reduce_fusion
  27.9 0.7 add_convert_fusion.mid_ref
  28.6 0.0 copy-done
  28.6 0.0 copy-start.2
  28.6 9.2 %convolution_convert_fusion.own_ref = bf16[512,1024]{1,0:T(8,128)(2,1)} fusion(bf16[1024,1024]{1,0:T(8,128)(2,1)S(1)} %copy-done, bf16[512,1024]{1,0:T(8,128)(2,1)S(1)} %add_convert_fusion.mid_ref, bf16[1024,1024]{1,0:T(8,128)(2,1)} %param.23), kind=kOutput, calls=%fused_computation.22 | convolution fusion | flops 2182086656 | bytes 6291456 | tf_op jit(solution)/shard_map/dot_general | solution.py:174
  37.8 0.0 copy-done.2
  37.9 0.4 collective-permute-start.1
  38.2 2.6 %collective-permute-done.1.other_ref = bf16[512,1024]{1,0:T(8,128)(2,1)} collective-permute-done((bf16[512,1024]{1,0:T(8,128)(2,1)}, bf16[512,1024]{1,0:T(8,128)(2,1)}, u32[]{:S(2)}, u32[]{:S(2)}) %collective-permute-start.1) | collective-permute-done | bytes 1048608 | tf_op jit(solution)/shard_map/ppermute | solution.py:175
  40.9 0.0 copy-start.7
  40.9 3.3 %shard_map.158 = (bf16[512,1024]{1,0:T(8,128)(2,1)}, bf16[128,1024]{1,0:T(8,128)(2,1)}) custom-call(s32[1]{0:T(128)S(6)} %copy.27.group_len_ref, bf16[512,1024]{1,0:T(8,128)(2,1)} %copy-done.2, bf16[512,1024]{1,0:T(8,128)(2,1)} %convolution_convert_fusion.own_ref, bf16[512,1024]{1,0:T(8,128)(2,1)} %collective-permute-done.1.other_ref, ...), custom_call_target="tpu_custom_call" | custom-call | flops 5242880 | bytes 4194304 | tf_op jit(solution)/shard_map/pallas_call | solution.py:128
  44.2 0.5 broadcast.31
  44.7 1.7 %reduce.2 = bf16[128,1024]{1,0:T(8,128)(2,1)S(1)} reduce(bf16[128,1,1024]{2,0,1:T(8,128)(2,1)} %bitcast.16, bf16[]{:T(256)} %broadcast.31), dimensions={1}, to_apply=%copy.19.reduce_sub_computation | reduce | bytes 524290 | tf_op jit(solution)/shard_map/all_to_all | solution.py:180
  46.4 0.2 reshape.24
  46.6 27.7 %all_to_all.22 = bf16[128,2,512]{2,1,0:T(2,128)(2,1)S(1)} all-to-all(bf16[128,2,512]{2,1,0:T(2,128)(2,1)S(1)} %reshape.24), channel_id=1, replica_groups=mesh['req'=128,'tp'=2] {'req'}, dimensions={0} | all-to-all | bytes 524288 | tf_op jit(solution)/shard_map/all_to_all | solution.py:180
  74.4 0.2 reshape.25
  74.6 0.0 copy-done.7
  74.6 0.3 convolution_reduce_fusion
  74.9 0.0 copy-start.5
  74.9 0.1 broadcast_in_dim.8
  75.0 0.2 all_to_all.19
  75.1 19.7 %all_to_all.23 = f32[256,1,1]{2,1,0:T(1,128)S(1)} all-to-all(f32[256,1,1]{2,1,0:T(1,128)S(1)} %all_to_all.19), channel_id=1, replica_groups=mesh['req'=128,'tp'=2] {'req','tp'}, dimensions={0} | all-to-all | bytes 2048 | tf_op jit(solution)/shard_map/all_to_all | solution.py:184
  94.8 0.9 reduce_max.21
  95.7 0.0 copy-done.5
  (2 shorter events, 0.0 us)
Async XLA Ops:
  0.6 28.0 %copy-start = (bf16[1024,1024]{1,0:T(8,128)(2,1)S(1)}, bf16[1024,1024]{1,0:T(8,128)(2,1)}, u32[]{:S(2)}) copy-start(bf16[1024,1024]{1,0:T(8,128)(2,1)} %param.24) | copy-start | bytes 6291460
  1.4 17.7 %copy-start.6 = (bf16[512,1024]{1,0:T(8,128)(2,1)S(1)}, bf16[512,1024]{1,0:T(8,128)(2,1)}, u32[]{:S(2)}) copy-start(bf16[512,1024]{1,0:T(8,128)(2,1)} %param.22) | copy-start | bytes 3145732
  19.1 5.4 %copy-start.3 = (f32[2,1024]{1,0:T(2,128)S(1)}, f32[2,1024]{1,0:T(2,128)}, u32[]{:S(2)}) copy-start(f32[2,1024]{1,0:T(2,128)} %param.26) | copy-start | bytes 24580
  19.2 5.3 %copy-start.4 = (f32[2,1024]{1,0:T(2,128)S(1)}, f32[2,1024]{1,0:T(2,128)}, u32[]{:S(2)}) copy-start(f32[2,1024]{1,0:T(2,128)} %param.25) | copy-start | bytes 24580
  19.2 7.6 %copy-start.1 = (bf16[512,1024]{1,0:T(8,128)(2,1)S(1)}, bf16[512,1024]{1,0:T(8,128)(2,1)}, u32[]{:S(2)}) copy-start(bf16[512,1024]{1,0:T(8,128)(2,1)} %x_ref.1) | copy-start | bytes 3145732
  21.0 5.8 %collective-permute-start = (bf16[512,1024]{1,0:T(8,128)(2,1)S(1)}, bf16[512,1024]{1,0:T(8,128)(2,1)S(1)}, u32[]{:S(2)}, u32[]{:S(2)}) collective-permute-start(bf16[512,1024]{1,0:T(8,128)(2,1)S(1)} %convolution_convert_fusion.1), channel_id=1, source_target_pairs={{0,1},{1,0},{2,3},{3,2},{4,5},{5,4},{6,7},{7,6},{8,9},{9,8},{10,11... | collective-permute-start | bytes 3145736 | tf_op jit(solution)/shard_map/ppermute | solution.py:19
  28.6 9.3 %copy-start.2 = (bf16[512,1024]{1,0:T(8,128)(2,1)}, bf16[512,1024]{1,0:T(8,128)(2,1)S(1)}, u32[]{:S(2)}) copy-start(bf16[512,1024]{1,0:T(8,128)(2,1)S(1)} %add_convert_fusion.mid_ref) | copy-start | bytes 3145732
  37.9 3.0 %collective-permute-start.1 = (bf16[512,1024]{1,0:T(8,128)(2,1)}, bf16[512,1024]{1,0:T(8,128)(2,1)}, u32[]{:S(2)}, u32[]{:S(2)}) collective-permute-start(bf16[512,1024]{1,0:T(8,128)(2,1)} %convolution_convert_fusion.own_ref), channel_id=1, source_target_pairs={{0,1},{1,0},{2,3},{3,2},{4,5},{5,4},{6,7},{7,6},{8,9},{9,8},{10,11... | collective-permute-start | bytes 3145736 | tf_op jit(solution)/shard_map/ppermute | solution.py:175
  40.9 33.7 %copy-start.7 = (bf16[192,1024]{1,0:T(8,128)(2,1)S(1)}, bf16[192,1024]{1,0:T(8,128)(2,1)}, u32[]{:S(2)}) copy-start(bf16[192,1024]{1,0:T(8,128)(2,1)} %param.27) | copy-start | bytes 1179652
  74.9 20.8 %copy-start.5 = (f32[128]{0:T(128)}, f32[128]{0:T(128)S(1)}, u32[]{:S(2)}) copy-start(f32[128]{0:T(128)S(1)} %convolution_reduce_fusion) | copy-start | bytes 1540

commit v16 on v15

--- a/solution.py
+++ b/solution.py
@@ -98,7 +98,7 @@
     )(cache_len, group_len, tokens, w_query, w_key, w_value, cache_k, cache_v)
 
 
-NORM_ROWS = 256
+NORM_ROWS = 512
 
 
 def residual_norm_kernel(group_len_ref, mid_ref, own_ref, other_ref, gain_ref, bias_ref, out_ref, copies_ref):

time: 96 us -> 96.6 us (level)
  no operation moved by 1% of the time
where the time goes in v16:
time: 96.6 us; the launch traced here: 96.3 us
  blocking collectives  47.4 us (49%)
  Pallas kernels  21.7 us (22%)
  matrix products  11.4 us (12%)
  other arithmetic  4.38 us (5%)
  waiting for transfers between devices  4.31 us (4%)
  starting transfers between devices  3.85 us (4%)
  local copies, waits for them, and re-layouts  1.79 us (2%)
  between operations  1.55 us (2%)
    all_to_all x1, blocking collectives, shards(): all_rows = lax.all_to_all(copies, 'req', 0, 0, tiled=True)  27.7 us
    all_to_all x1, blocking collectives, shards(): lax.all_to_all(spread, ('req', 'tp'), 0, 0, tiled=True)  19.7 us
    pallas_call x1, Pallas kernels, attention(): pl.pallas_call(attention_kernel, out_shape=jax.ShapeDtypeStruct((rows, wi...  17.7 us
    dot_general x1, matrix products, shards(): jnp.dot(active, w_down, preferred_element_type=jnp.float32)  9.24 us
    pallas_call x1, Pallas kernels, residual_norm(): pl.pallas_call(residual_norm_kernel, out_shape=(jax.ShapeDtypeStruct((row...  3.96 us
    ppermute x1, starting transfers between devices, pair_sum(): other = lax.ppermute(own, 'tp', [(0, 1), (1, 0)])  3.47 us
    ppermute x1, waiting for transfers between devices, shards(): other = lax.ppermute(own, 'tp', [(0, 1), (1, 0)])  2.63 us
  transfers between devices with their start and end apart: 2, of which 2 were waited for; matrix products, arithmetic and copies ran while one was open for 1% of the time, Pallas kernels for 0%

profile of v16, /device:TPU:1, one launch (start us, length us, event | category | flops | bytes accessed | tf_op | source)
XLA Modules:
  0.0 96.3 jit_solution(6303581065231150067)
XLA Ops:
  0.6 0.0 copy-start
  1.4 0.0 copy-start.6
  1.5 17.7 %shard_map.157 = bf16[512,512]{1,0:T(8,128)(2,1)} custom-call(s32[128]{0:T(128)} %cache_len_ref.1, s32[1]{0:T(128)S(6)} %copy.27.group_len_ref, bf16[512,1024]{1,0:T(8,128)(2,1)} %x_ref.1, bf16[1024,512]{1,0:T(8,128)(2,1)} %wq_ref.1, bf16[1024,512]{1,0:T(8,128)(2,1)} %wk_ref.1, bf16[1024,512]{1,0:T(8,128)(2,1)} %wv_ref.1, bf16[1024,512]{1,0:T(8,128)(2,1)} %bitcast.20, ...), custom_call_target="tpu_custom_call" | custom-call | flops 4831838208 | bytes 6815744 | tf_op jit(solution)/shard_map/pallas_call | solution.py:77
  19.1 0.0 copy-done.6
  19.1 0.0 copy-start.3
  19.2 0.0 copy-start.4
  19.2 0.0 copy-start.1
  19.2 1.8 %convolution_convert_fusion.1 = bf16[512,1024]{1,0:T(8,128)(2,1)S(1)} fusion(bf16[512,512]{1,0:T(8,128)(2,1)} %shard_map.157, bf16[512,1024]{1,0:T(8,128)(2,1)S(1)} %copy-done.6), kind=kOutput, calls=%fused_computation.23 | convolution fusion | flops 537395200 | bytes 2621440 | tf_op jit(solution)/shard_map/dot_general | solution.py:167
  21.0 3.5 %collective-permute-start = (bf16[512,1024]{1,0:T(8,128)(2,1)S(1)}, bf16[512,1024]{1,0:T(8,128)(2,1)S(1)}, u32[]{:S(2)}, u32[]{:S(2)}) collective-permute-start(bf16[512,1024]{1,0:T(8,128)(2,1)S(1)} %convolution_convert_fusion.1), channel_id=1, source_target_pairs={{0,1},{1,0},{2,3},{3,2},{4,5},{5,4},{6,7},{7,6},{8,9},{9,8},{10,11... | collective-permute-start | bytes 3145736 | tf_op jit(solution)/shard_map/ppermute | solution.py:19
  24.5 0.0 copy-done.3
  24.5 0.0 copy-done.4
  24.5 0.6 fusion.74
  25.1 1.7 %collective-permute-done = bf16[512,1024]{1,0:T(8,128)(2,1)S(1)} collective-permute-done((bf16[512,1024]{1,0:T(8,128)(2,1)S(1)}, bf16[512,1024]{1,0:T(8,128)(2,1)S(1)}, u32[]{:S(2)}, u32[]{:S(2)}) %collective-permute-start) | collective-permute-done | bytes 1048608 | tf_op jit(solution)/shard_map/ppermute | solution.py:19
  26.8 0.0 copy-done.1
  26.8 0.5 fusion.41
  27.3 0.6 multiply_reduce_fusion
  27.9 0.7 add_convert_fusion.mid_ref
  28.6 0.0 copy-done
  28.6 0.0 copy-start.2
  28.6 9.2 %convolution_convert_fusion.own_ref = bf16[512,1024]{1,0:T(8,128)(2,1)} fusion(bf16[1024,1024]{1,0:T(8,128)(2,1)S(1)} %copy-done, bf16[512,1024]{1,0:T(8,128)(2,1)S(1)} %add_convert_fusion.mid_ref, bf16[1024,1024]{1,0:T(8,128)(2,1)} %param.23), kind=kOutput, calls=%fused_computation.22 | convolution fusion | flops 2182086656 | bytes 6291456 | tf_op jit(solution)/shard_map/dot_general | solution.py:174
  37.8 0.0 copy-done.2
  37.9 0.4 collective-permute-start.1
  38.2 2.6 %collective-permute-done.1.other_ref = bf16[512,1024]{1,0:T(8,128)(2,1)} collective-permute-done((bf16[512,1024]{1,0:T(8,128)(2,1)}, bf16[512,1024]{1,0:T(8,128)(2,1)}, u32[]{:S(2)}, u32[]{:S(2)}) %collective-permute-start.1) | collective-permute-done | bytes 1048608 | tf_op jit(solution)/shard_map/ppermute | solution.py:175
  40.9 0.0 copy-start.7
  40.9 4.0 %shard_map.158 = (bf16[512,1024]{1,0:T(8,128)(2,1)}, bf16[128,1024]{1,0:T(8,128)(2,1)}) custom-call(s32[1]{0:T(128)S(6)} %copy.27.group_len_ref, bf16[512,1024]{1,0:T(8,128)(2,1)} %copy-done.2, bf16[512,1024]{1,0:T(8,128)(2,1)} %convolution_convert_fusion.own_ref, bf16[512,1024]{1,0:T(8,128)(2,1)} %collective-permute-done.1.other_ref, ...), custom_call_target="tpu_custom_call" | custom-call | flops 5242880 | bytes 4194304 | tf_op jit(solution)/shard_map/pallas_call | solution.py:128
  44.8 0.5 broadcast.31
  45.3 1.7 %reduce.2 = bf16[128,1024]{1,0:T(8,128)(2,1)S(1)} reduce(bf16[128,1,1024]{2,0,1:T(8,128)(2,1)} %bitcast.16, bf16[]{:T(256)} %broadcast.31), dimensions={1}, to_apply=%copy.19.reduce_sub_computation | reduce | bytes 524290 | tf_op jit(solution)/shard_map/all_to_all | solution.py:180
  47.1 0.2 reshape.24
  47.2 27.7 %all_to_all.22 = bf16[128,2,512]{2,1,0:T(2,128)(2,1)S(1)} all-to-all(bf16[128,2,512]{2,1,0:T(2,128)(2,1)S(1)} %reshape.24), channel_id=1, replica_groups=mesh['req'=128,'tp'=2] {'req'}, dimensions={0} | all-to-all | bytes 524288 | tf_op jit(solution)/shard_map/all_to_all | solution.py:180
  75.0 0.2 reshape.25
  75.2 0.0 copy-done.7
  75.2 0.3 convolution_reduce_fusion
  75.5 0.0 copy-start.5
  75.5 0.1 broadcast_in_dim.8
  75.6 0.2 all_to_all.19
  75.8 19.7 %all_to_all.23 = f32[256,1,1]{2,1,0:T(1,128)S(1)} all-to-all(f32[256,1,1]{2,1,0:T(1,128)S(1)} %all_to_all.19), channel_id=1, replica_groups=mesh['req'=128,'tp'=2] {'req','tp'}, dimensions={0} | all-to-all | bytes 2048 | tf_op jit(solution)/shard_map/all_to_all | solution.py:184
  95.4 0.9 reduce_max.21
  96.3 0.0 copy-done.5
  (2 shorter events, 0.0 us)
Async XLA Ops:
  0.6 28.0 %copy-start = (bf16[1024,1024]{1,0:T(8,128)(2,1)S(1)}, bf16[1024,1024]{1,0:T(8,128)(2,1)}, u32[]{:S(2)}) copy-start(bf16[1024,1024]{1,0:T(8,128)(2,1)} %param.24) | copy-start | bytes 6291460
  1.4 17.7 %copy-start.6 = (bf16[512,1024]{1,0:T(8,128)(2,1)S(1)}, bf16[512,1024]{1,0:T(8,128)(2,1)}, u32[]{:S(2)}) copy-start(bf16[512,1024]{1,0:T(8,128)(2,1)} %param.22) | copy-start | bytes 3145732
  19.1 5.4 %copy-start.3 = (f32[2,1024]{1,0:T(2,128)S(1)}, f32[2,1024]{1,0:T(2,128)}, u32[]{:S(2)}) copy-start(f32[2,1024]{1,0:T(2,128)} %param.26) | copy-start | bytes 24580
  19.2 5.3 %copy-start.4 = (f32[2,1024]{1,0:T(2,128)S(1)}, f32[2,1024]{1,0:T(2,128)}, u32[]{:S(2)}) copy-start(f32[2,1024]{1,0:T(2,128)} %param.25) | copy-start | bytes 24580
  19.2 7.6 %copy-start.1 = (bf16[512,1024]{1,0:T(8,128)(2,1)S(1)}, bf16[512,1024]{1,0:T(8,128)(2,1)}, u32[]{:S(2)}) copy-start(bf16[512,1024]{1,0:T(8,128)(2,1)} %x_ref.1) | copy-start | bytes 3145732
  21.0 5.8 %collective-permute-start = (bf16[512,1024]{1,0:T(8,128)(2,1)S(1)}, bf16[512,1024]{1,0:T(8,128)(2,1)S(1)}, u32[]{:S(2)}, u32[]{:S(2)}) collective-permute-start(bf16[512,1024]{1,0:T(8,128)(2,1)S(1)} %convolution_convert_fusion.1), channel_id=1, source_target_pairs={{0,1},{1,0},{2,3},{3,2},{4,5},{5,4},{6,7},{7,6},{8,9},{9,8},{10,11... | collective-permute-start | bytes 3145736 | tf_op jit(solution)/shard_map/ppermute | solution.py:19
  28.6 9.3 %copy-start.2 = (bf16[512,1024]{1,0:T(8,128)(2,1)}, bf16[512,1024]{1,0:T(8,128)(2,1)S(1)}, u32[]{:S(2)}) copy-start(bf16[512,1024]{1,0:T(8,128)(2,1)S(1)} %add_convert_fusion.mid_ref) | copy-start | bytes 3145732
  37.9 3.0 %collective-permute-start.1 = (bf16[512,1024]{1,0:T(8,128)(2,1)}, bf16[512,1024]{1,0:T(8,128)(2,1)}, u32[]{:S(2)}, u32[]{:S(2)}) collective-permute-start(bf16[512,1024]{1,0:T(8,128)(2,1)} %convolution_convert_fusion.own_ref), channel_id=1, source_target_pairs={{0,1},{1,0},{2,3},{3,2},{4,5},{5,4},{6,7},{7,6},{8,9},{9,8},{10,11... | collective-permute-start | bytes 3145736 | tf_op jit(solution)/shard_map/ppermute | solution.py:175
  40.9 34.3 %copy-start.7 = (bf16[192,1024]{1,0:T(8,128)(2,1)S(1)}, bf16[192,1024]{1,0:T(8,128)(2,1)}, u32[]{:S(2)}) copy-start(bf16[192,1024]{1,0:T(8,128)(2,1)} %param.27) | copy-start | bytes 1179652
  75.5 20.8 %copy-start.5 = (f32[128]{0:T(128)}, f32[128]{0:T(128)S(1)}, u32[]{:S(2)}) copy-start(f32[128]{0:T(128)S(1)} %convolution_reduce_fusion) | copy-start | bytes 1540
